TPU v7x, 128 devices: a whole 4x4x4 slice. The times are simulated.
128 devices in a mesh: rcv: 16 (over y_hi, x, core), win: 8 (over z, y_lo).
Axes of the slice: x: 4, y: 4 (y_hi: 2, y_lo: 2; y = y_hi * 2 + y_lo), z: 4, core: 2. Of those that a mesh axis runs over, the one named last changes fastest.
Arguments:
- traces: bfloat16 [8192, 8, 6144], P('rcv', 'win'), may hold values from -6 to 6
- sources: int32 [8, 4], replicated, may hold values from 0 to 8191
- offsets: int32 [8], P('win'), may hold values from 0 to 44
Outputs:
- stacks: float32 [32, 101, 8192], P('win', None, 'rcv')
All inputs are finite; a program needn't handle non-finite values.
Results may differ from a plain program's by a relative error of at most 0.0003.
Values may be sent and summed in bfloat16 or wider, within the bound.
No kernel may reach another device: no remote copies, remote signals or barrier semaphores. Data moves between devices by JAX's collectives and lax.ppermute only.
A program may use at most 192 MiB of HBM per device.

v0:
```python
import math

import jax
import jax.numpy as jnp
from jax import lax
from jax.sharding import PartitionSpec as P

SAMPLES = 6000
HALF = 50
LAGS = 101


def lag_matrix(record, start_at):
    span_len = record.shape[-1]
    positions = jnp.arange(span_len, dtype=jnp.int32)
    inside = (positions >= start_at + HALF) & (positions < start_at + HALF + SAMPLES)
    masked = jnp.where(inside[None, :], record, jnp.zeros_like(record))
    padded = jnp.pad(masked, ((0, 0), (LAGS, LAGS)))
    rows = []
    for lag in range(LAGS):
        begin = LAGS + HALF - lag
        rows.append(padded[:, begin : begin + span_len])
    return jnp.stack(rows, axis=1)


def shards(traces, sources, offsets):
    ch_dev = traces.shape[0]
    win_dev = traces.shape[1]
    step_count = sources.shape[0]
    win_count = lax.axis_size("win")
    first_row = lax.axis_index("rcv") * ch_dev
    window_total = win_dev * win_count
    norm_scale = 1.0 / math.sqrt(SAMPLES * window_total)
    channel_ids = jnp.arange(ch_dev, dtype=jnp.int32)
    results = []
    for step in range(step_count):
        select = (
            lax.dynamic_index_in_dim(sources, step, 0, keepdims=False)[:, None] - first_row
            == channel_ids[None, :]
        ).astype(traces.dtype)
        source_rows = lax.psum(
            jnp.einsum("kc,cwt->kwt", select, traces, preferred_element_type=jnp.float32).astype(
                jnp.bfloat16
            ),
            "rcv",
        )
        summed = jnp.zeros((source_rows.shape[0], LAGS, ch_dev), jnp.float32)
        shifted = lag_matrix(source_rows[:, 0, :], offsets[0])
        summed = summed + jnp.einsum(
            "kju,cu->kjc", shifted, traces[:, 0, :], preferred_element_type=jnp.float32
        )
        results.append(summed * norm_scale)
    stacked = jnp.concatenate(results, axis=0)
    return lax.psum_scatter(stacked, "win", scatter_dimension=0, tiled=True)


def solution(mesh):
    in_specs = (P("rcv", "win", None), P(), P("win"))
    out_specs = P("win", None, "rcv")
    return jax.shard_map(shards, mesh=mesh, in_specs=in_specs, out_specs=out_specs, check_vma=False)
```

profile of v0, /device:TPU:8, one launch (start us, length us, event | category | flops | bytes accessed | tf_op | source)
XLA Modules:
  0.0 865.0 jit_solution(3773134209944400224)
XLA Ops:
  6.5 1.3 subtract_reduce_fusion
  7.8 4.7 fusion.7
  12.5 1.6 fusion.5
  14.0 1.6 fusion.4
  15.6 1.6 fusion.3
  17.2 1.6 fusion.2
  18.8 1.6 fusion.1
  20.4 1.6 fusion
  22.0 1.6 fusion.6
  24.6 140.1 %all-reduce.11.cloned.1.call-done = (bf16[4,1,6144]{2,0,1:T(4,128)(2,1)}, bf16[4,1,6144]{2,0,1:T(4,128)(2,1)}, bf16[4,1,6144]{2,0,1:T(4,128)(2,1)}, bf16[4,1,614...) async-done(((bf16[4,1,6144]{2,0,1:T(4,128)(2,1)}, ...) | async-done | bytes 393232 | tf_op jit(solution)/shard_map/psum | solution.py:41
  164.7 1.2 bitcast_select_fusion
  176.6 0.7 constant_dynamic-update-slice_fusion.792
  270.8 0.7 constant_dynamic-update-slice_fusion.255
  341.3 0.7 constant_dynamic-update-slice_fusion.459
  342.0 0.7 constant_dynamic-update-slice_fusion.458
  431.4 0.9 constant_dynamic-update-slice_fusion.79
  452.4 0.9 constant_dynamic-update-slice_fusion.757
  483.5 0.9 constant_dynamic-update-slice_fusion.333
  645.3 0.7 constant_dynamic-update-slice_fusion
  646.1 9.6 %constant_dynamic-update-slice_fusion.815 = f32[32,101,512]{2,1,0:T(8,128)} fusion(bf16[512,1,6144]{2,0,1:T(8,128)(2,1)S(1)} %bitcast.1701, bf16[4,101,6144]{2,0,1:T(4,128)(2,1)} %get-tuple-element.37), kind=kOutput, calls=%fused_computation.863 | convolution fusion | flops 2541955072 | bytes 12107776 | tf_op jit(solution)/shard_map/kju,cu->kjc/dot_general | solution.py:49
  655.6 0.8 constant_dynamic-update-slice_fusion.202
  656.4 0.8 constant_dynamic-update-slice_fusion.404
  657.2 0.8 constant_dynamic-update-slice_fusion.606
  657.9 7.4 constant_dynamic-update-slice_fusion.814
  665.3 7.2 constant_dynamic-update-slice_fusion.813
  672.5 10.0 %constant_dynamic-update-slice_fusion.812 = f32[32,101,512]{2,1,0:T(8,128)} fusion(f32[32,101,512]{2,1,0:T(8,128)} %constant_dynamic-update-slice_fusion.813, bf16[512,1,6144]{2,0,1:T(8,128)(2,1)S(1)} %bitcast.1701, bf16[4,101,6144]{2,0,1:T(4,128)(2,1)} %get-tuple-element.40), kind=kOutput, calls=%fused_computation.860 | convolution fusion | flops 2541955072 | bytes 12107776 | tf_op jit(solution)/shard_map/kju,cu->kjc/dot_general | solution.py:49
  682.4 7.2 constant_dynamic-update-slice_fusion.811
  689.6 7.6 constant_dynamic-update-slice_fusion.810
  697.2 9.6 %constant_dynamic-update-slice_fusion.809 = f32[32,101,512]{2,1,0:T(8,128)} fusion(f32[32,101,512]{2,1,0:T(8,128)} %constant_dynamic-update-slice_fusion.810, bf16[512,1,6144]{2,0,1:T(8,128)(2,1)S(1)} %bitcast.1701, bf16[4,101,6144]{2,0,1:T(4,128)(2,1)} %get-tuple-element.43), kind=kOutput, calls=%fused_computation.857 | convolution fusion | flops 2541955072 | bytes 12107776 | tf_op jit(solution)/shard_map/kju,cu->kjc/dot_general | solution.py:49
  706.7 7.3 constant_dynamic-update-slice_fusion.808
  714.1 141.2 %reduce-scatter.2.cloned.1.call-done = f32[4,101,512]{2,1,0:T(8,128)} async-done(((f32[32,101,512]{2,1,0:T(8,128)}), f32[4,101,512]{2,1,0:T(8,128)}) %reduce-scatter.2.cloned.1.call-update) | async-done | bytes 827408 | tf_op jit(solution)/shard_map/reduce_scatter | solution.py:54
  855.3 2.6 copy.12
  (836 shorter events, 472.5 us)
Async XLA Ops:
  6.5 158.2 %all-reduce.11.cloned.1.call-start = ((), (), s32[]{:S(2)}) async-start(), calls=%async_computation.2 | async-start | bytes 786432 | tf_op jit(solution)/shard_map/psum | solution.py:41
  6.5 5.9 copy-start
  23.6 831.8 %reduce-scatter.2.cloned.1.call-start = ((), (), s32[]{:S(2)}) async-start(), calls=%async_computation.1 | async-start | bytes 7667712 | tf_op jit(solution)/shard_map/reduce_scatter | solution.py:54
  329.9 122.4 %slice-start.4 = ((s8[4964352]{0:T(1024)(128)(4,1)}), s8[4194304]{0:T(1024)(128)(4,1)S(1)}, s32[]{:S(2)}) async-start(s8[4964352]{0:T(1024)(128)(4,1)} %bitcast.1704), calls=%async_computation.7 | async-start | bytes 8388608
  341.3 111.0 %slice-start.2 = ((s8[4964352]{0:T(1024)(128)(4,1)}), s8[4194304]{0:T(1024)(128)(4,1)S(1)}, s32[]{:S(2)}) async-start(s8[4964352]{0:T(1024)(128)(4,1)} %bitcast.1702), calls=%async_computation.5 | async-start | bytes 8388608
  379.9 72.3 %copy-start.1 = (bf16[4,1,6144]{2,0,1:T(4,128)(2,1)S(1)}, bf16[4,1,6144]{2,0,1:T(4,128)(2,1)}, u32[]{:S(2)}) copy-start(bf16[4,1,6144]{2,0,1:T(4,128)(2,1)} %get-tuple-element.13) | copy-start | bytes 147460
  379.9 72.3 %copy-start.2 = (bf16[4,1,6144]{2,0,1:T(4,128)(2,1)S(1)}, bf16[4,1,6144]{2,0,1:T(4,128)(2,1)}, u32[]{:S(2)}) copy-start(bf16[4,1,6144]{2,0,1:T(4,128)(2,1)} %get-tuple-element.14) | copy-start | bytes 147460
  379.9 72.3 %copy-start.3 = (bf16[4,1,6144]{2,0,1:T(4,128)(2,1)S(1)}, bf16[4,1,6144]{2,0,1:T(4,128)(2,1)}, u32[]{:S(2)}) copy-start(bf16[4,1,6144]{2,0,1:T(4,128)(2,1)} %get-tuple-element.15) | copy-start | bytes 147460
  379.9 72.3 %copy-start.4 = (bf16[4,1,6144]{2,0,1:T(4,128)(2,1)S(1)}, bf16[4,1,6144]{2,0,1:T(4,128)(2,1)}, u32[]{:S(2)}) copy-start(bf16[4,1,6144]{2,0,1:T(4,128)(2,1)} %get-tuple-element.16) | copy-start | bytes 147460
  380.0 72.3 %copy-start.5 = (bf16[4,1,6144]{2,0,1:T(4,128)(2,1)S(1)}, bf16[4,1,6144]{2,0,1:T(4,128)(2,1)}, u32[]{:S(2)}) copy-start(bf16[4,1,6144]{2,0,1:T(4,128)(2,1)} %get-tuple-element.17) | copy-start | bytes 147460
  380.0 72.3 %copy-start.6 = (bf16[4,1,6144]{2,0,1:T(4,128)(2,1)S(1)}, bf16[4,1,6144]{2,0,1:T(4,128)(2,1)}, u32[]{:S(2)}) copy-start(bf16[4,1,6144]{2,0,1:T(4,128)(2,1)} %get-tuple-element.18) | copy-start | bytes 147460
  380.0 72.3 %copy-start.7 = (bf16[4,1,6144]{2,0,1:T(4,128)(2,1)S(1)}, bf16[4,1,6144]{2,0,1:T(4,128)(2,1)}, u32[]{:S(2)}) copy-start(bf16[4,1,6144]{2,0,1:T(4,128)(2,1)} %get-tuple-element.19) | copy-start | bytes 147460
  380.0 72.3 %copy-start.8 = (bf16[4,1,6144]{2,0,1:T(4,128)(2,1)S(1)}, bf16[4,1,6144]{2,0,1:T(4,128)(2,1)}, u32[]{:S(2)}) copy-start(bf16[4,1,6144]{2,0,1:T(4,128)(2,1)} %get-tuple-element.20) | copy-start | bytes 147460
  380.0 72.3 %copy-start.9 = (bf16[4,101,6144]{2,0,1:T(4,128)(2,1)S(1)}, bf16[4,101,6144]{2,0,1:T(4,128)(2,1)}, u32[]{:S(2)}) copy-start(bf16[4,101,6144]{2,0,1:T(4,128)(2,1)} %constant_dynamic-update-slice_fusion.253) | copy-start | bytes 14893060
  390.7 61.6 %slice-start.5 = ((s8[4964352]{0:T(1024)(128)(4,1)}), s8[770048]{0:T(1024)(128)(4,1)S(1)}, s32[]{:S(2)}) async-start(s8[4964352]{0:T(1024)(128)(4,1)} %bitcast.1704), calls=%async_computation.8 | async-start | bytes 1540096
  396.4 55.9 %slice-start.3 = ((s8[4964352]{0:T(1024)(128)(4,1)}), s8[770048]{0:T(1024)(128)(4,1)S(1)}, s32[]{:S(2)}) async-start(s8[4964352]{0:T(1024)(128)(4,1)} %bitcast.1702), calls=%async_computation.6 | async-start | bytes 1540096
  527.9 118.1 %slice-start = ((s8[6291456]{0:T(1024)(128)(4,1)}), s8[4194304]{0:T(1024)(128)(4,1)S(1)}, s32[]{:S(2)}) async-start(s8[6291456]{0:T(1024)(128)(4,1)} %bitcast.1700), calls=%async_computation.3 | async-start | bytes 8388608
  587.1 59.0 %slice-start.1 = ((s8[6291456]{0:T(1024)(128)(4,1)}), s8[2097152]{0:T(1024)(128)(4,1)S(1)}, s32[]{:S(2)}) async-start(s8[6291456]{0:T(1024)(128)(4,1)} %bitcast.1700), calls=%async_computation.4 | async-start | bytes 4194304
  665.3 17.1 %slice-start.6 = ((s8[4964352]{0:T(1024)(128)(4,1)}), s8[4194304]{0:T(1024)(128)(4,1)S(1)}, s32[]{:S(2)}) async-start(s8[4964352]{0:T(1024)(128)(4,1)} %bitcast.1706), calls=%async_computation.9 | async-start | bytes 8388608
  672.5 10.0 %slice-start.7 = ((s8[4964352]{0:T(1024)(128)(4,1)}), s8[770048]{0:T(1024)(128)(4,1)S(1)}, s32[]{:S(2)}) async-start(s8[4964352]{0:T(1024)(128)(4,1)} %bitcast.1706), calls=%async_computation.10 | async-start | bytes 1540096
  672.5 17.1 %slice-start.8 = ((s8[4964352]{0:T(1024)(128)(4,1)}), s8[4194304]{0:T(1024)(128)(4,1)S(1)}, s32[]{:S(2)}) async-start(s8[4964352]{0:T(1024)(128)(4,1)} %bitcast.1708), calls=%async_computation.11 | async-start | bytes 8388608
  682.4 7.2 slice-start.9
Sparse Core Ops, SparseCore 0:
  23.7 140.9 all-reduce.10
  714.2 141.0 reduce-scatter.1
where the time goes:
time: 872 us; the launch traced here: 865 us
  local copies, waits for them, and re-layouts  482 us (55%)
  waiting for transfers between devices  281 us (32%)
  matrix products  81.4 us (9%)
  between operations  16 us (2%)
    unnamed x832, local copies, waits for them, and re-layouts  477 us
    reduce_scatter x1, waiting for transfers between devices, shards(): return lax.psum_scatter(stacked, 'win', scatter_dimension=0, tiled=True)  141 us
    psum x1, waiting for transfers between devices, shards(): lax.psum(jnp.einsum('kc,cwt->kwt', select, traces, preferred_element_type...  140 us
    dot_general x8, matrix products, shards(): jnp.einsum('kju,cu->kjc', shifted, traces[:, 0, :], preferred_element_typ...  65.7 us
  transfers between devices with their start and end apart: 2, of which 2 were waited for; matrix products, arithmetic and copies ran while one was open for 0% of the time, Pallas kernels for 0%

commit v1 on v0

v1 whole, which is shorter than its diff:
```python
import math

import jax
import jax.numpy as jnp
from jax import lax
from jax.experimental import pallas as pl
from jax.experimental.pallas import tpu as pltpu
from jax.sharding import PartitionSpec as P

SAMPLES = 6000
HALF = 50
LAGS = 101
ROWS = 128
LANE = 128
FRONT = ROWS - HALF
CHUNK = 1024


def corr_kernel(mq_ref, rt_ref, out_ref, acc_ref, *, scale, pairs, width):
    q = pl.program_id(0)
    u0 = pl.multiple_of(q * width, LANE)
    row = lax.broadcasted_iota(jnp.int32, (ROWS, LANE), 0)
    lane = lax.broadcasted_iota(jnp.int32, (ROWS, LANE), 1)
    keep = lane >= row
    blocks = width // LANE

    def lagged(k):
        line = mq_ref[pl.ds(k, 1), pl.ds(u0, width + LANE)]
        wide = jnp.broadcast_to(line, (ROWS, width + LANE))
        turned = [
            pltpu.roll(wide[:, b * LANE : (b + 1) * LANE], 0, 1, stride=1, stride_axis=0)
            for b in range(blocks + 1)
        ]
        parts = [jnp.where(keep, turned[b + 1], turned[b]) for b in range(blocks)]
        return jnp.concatenate(parts, axis=1).astype(jnp.bfloat16)

    def body(p, carry):
        lhs = jnp.concatenate([lagged(2 * p), lagged(2 * p + 1)], axis=0)
        prod = jnp.dot(lhs, rt_ref[...], preferred_element_type=jnp.float32)

        @pl.when(q == 0)
        def _():
            acc_ref[p] = prod

        @pl.when(q > 0)
        def _():
            acc_ref[p] = acc_ref[p] + prod

        return carry

    lax.fori_loop(0, pairs, body, 0)

    @pl.when(q == pl.num_programs(0) - 1)
    def _():
        for k in range(2 * pairs):
            half = (k % 2) * ROWS
            out_ref[k] = acc_ref[k // 2, half : half + LAGS, :] * scale


def correlate(mq, rt, scale):
    n_src = mq.shape[0]
    span, ch = rt.shape
    pairs = n_src // 2
    width = CHUNK if span % CHUNK == 0 else span
    kernel = lambda *refs: corr_kernel(*refs, scale=scale, pairs=pairs, width=width)
    return pl.pallas_call(
        kernel,
        grid=(span // width,),
        in_specs=[
            pl.BlockSpec(mq.shape, lambda q: (0, 0)),
            pl.BlockSpec((width, ch), lambda q: (q, 0)),
        ],
        out_specs=pl.BlockSpec((n_src, LAGS, ch), lambda q: (0, 0, 0)),
        out_shape=jax.ShapeDtypeStruct((n_src, LAGS, ch), jnp.float32),
        scratch_shapes=[pltpu.VMEM((pairs, 2 * ROWS, ch), jnp.float32)],
        compiler_params=pltpu.CompilerParams(dimension_semantics=("arbitrary",)),
    )(mq, rt)


def shards(traces, sources, offsets):
    ch_dev = traces.shape[0]
    span = traces.shape[2]
    win_count = lax.axis_size("win")
    first_row = lax.axis_index("rcv") * ch_dev
    norm_scale = 1.0 / math.sqrt(SAMPLES * traces.shape[1] * win_count)
    record = traces[:, 0, :]
    channel_ids = jnp.arange(ch_dev, dtype=jnp.int32)
    select = (sources.reshape(-1)[:, None] - first_row == channel_ids[None, :]).astype(
        traces.dtype
    )
    picked = jnp.dot(select, record, preferred_element_type=jnp.float32).astype(jnp.bfloat16)
    source_rows = lax.psum(picked, "rcv")
    start_at = offsets[0]
    positions = jnp.arange(span, dtype=jnp.int32)
    inside = (positions >= start_at + HALF) & (positions < start_at + HALF + SAMPLES)
    masked = jnp.where(inside[None, :], source_rows, jnp.zeros_like(source_rows))
    mq = jnp.pad(masked.astype(jnp.float32), ((0, 0), (FRONT, LANE - FRONT)))
    stacked = correlate(mq, record.T, norm_scale)
    return lax.psum_scatter(stacked, "win", scatter_dimension=0, tiled=True)


def solution(mesh):
    in_specs = (P("rcv", "win", None), P(), P("win"))
    out_specs = P("win", None, "rcv")
    return jax.shard_map(shards, mesh=mesh, in_specs=in_specs, out_specs=out_specs, check_vma=False)
```

time: 872 us -> 363 us (0.42)
  local copies, waits for them, and re-layouts: 482 us -> 11.4 us
  matrix products: 81.4 us -> 4.73 us
  Pallas kernels: 0 us -> 56.3 us
  waiting for transfers between devices: 281 us -> 272 us
    unnamed x832 -> x1, local copies, waits for them, and re-layouts: 477 us -> 8.69 us
    dot_general x16 -> x1, matrix products: 81.4 us -> 4.73 us  [shards(): jnp.dot(select, record, preferred_element_type=jnp.float32)]
    pallas_call x0 -> x1, Pallas kernels: none -> 56.3 us  [correlate(): pl.pallas_call(kernel, grid=(span // width,), in_specs=[pl.BlockSpec(mq.s...]
    psum x1, waiting for transfers between devices: 140 us -> 131 us  [shards(): source_rows = lax.psum(picked, 'rcv')]
  transfers between devices with their start and end apart: 2 -> 2, of which waited for: 2 -> 2; matrix products, arithmetic and copies ran while one was open for 0% -> 2% of each run, Pallas kernels for 0% -> 0%
where the time goes in v1:
time: 363 us; the launch traced here: 361 us
  waiting for transfers between devices  272 us (75%)
  Pallas kernels  56.3 us (16%)
  between operations  14.1 us (4%)
  local copies, waits for them, and re-layouts  11.4 us (3%)
  matrix products  4.73 us (1%)
    reduce_scatter x1, waiting for transfers between devices, shards(): return lax.psum_scatter(stacked, 'win', scatter_dimension=0, tiled=True)  141 us
    psum x1, waiting for transfers between devices, shards(): source_rows = lax.psum(picked, 'rcv')  131 us
    pallas_call x1, Pallas kernels, correlate(): pl.pallas_call(kernel, grid=(span // width,), in_specs=[pl.BlockSpec(mq.s...  56.3 us
    unnamed x1, local copies, waits for them, and re-layouts  8.69 us
  transfers between devices with their start and end apart: 2, of which 2 were waited for; matrix products, arithmetic and copies ran while one was open for 2% of the time, Pallas kernels for 0%

profile of v1, /device:TPU:8, one launch (start us, length us, event | category | flops | bytes accessed | tf_op | source)
XLA Modules:
  0.0 361.4 jit_solution(16046018828540874753)
XLA Ops:
  6.5 0.0 all-reduce.3.cloned.1.call-start
  6.5 0.7 broadcast_subtract_fusion
  7.2 0.1 copy.7
  7.3 0.1 sub.16
  7.4 4.7 %convolution_convert_fusion = bf16[32,6144]{1,0:T(8,128)(2,1)} fusion(bf16[512,1,6144]{2,0,1:T(8,128)(2,1)} %param.3, s32[32]{0:T(128)S(1)} %sub.16), kind=kOutput, calls=%fused_computation | convolution fusion | flops 201539584 | bytes 6684800 | tf_op jit(solution)/shard_map/dot_general | solution.py:91
  12.1 0.0 all-reduce.3.cloned.1.call-update
  12.1 0.0 reduce-scatter.2.cloned.1.call-start
  12.2 8.7 %copy.8 = bf16[512,1,6144]{0,2,1:T(8,128)(2,1)} copy(bf16[512,1,6144]{2,0,1:T(8,128)(2,1)} %param.3) | data formatting | bytes 12582912 | tf_op args[0]
  21.6 130.7 %all-reduce.3.cloned.1.call-done = bf16[32,6144]{1,0:T(8,128)(2,1)} async-done(((bf16[32,6144]{1,0:T(8,128)(2,1)}), bf16[32,6144]{1,0:T(8,128)(2,1)}) %all-reduce.3.cloned.1.call-update) | async-done | bytes 393232 | tf_op jit(solution)/shard_map/psum | solution.py:92
  152.3 1.0 broadcast_select_fusion
  153.3 1.1 pad_convert_fusion.refs_0_
  154.4 56.3 %shard_map.37 = f32[32,101,512]{2,1,0:T(8,128)} custom-call(f32[32,6272]{1,0:T(8,128)} %pad_convert_fusion.refs_0_, bf16[6144,512]{1,0:T(8,128)(2,1)} %bitcast.8), custom_call_target="tpu_custom_call" | custom-call | tf_op jit(solution)/shard_map/pallas_call | solution.py:66
  210.7 0.0 reduce-scatter.2.cloned.1.call-update
  210.7 141.2 %reduce-scatter.2.cloned.1.call-done = f32[4,101,512]{2,1,0:T(8,128)} async-done(((f32[32,101,512]{2,1,0:T(8,128)}), f32[4,101,512]{2,1,0:T(8,128)}) %reduce-scatter.2.cloned.1.call-update) | async-done | bytes 827408 | tf_op jit(solution)/shard_map/reduce_scatter | solution.py:99
  352.0 2.6 copy.9
  (1 shorter events, 0.0 us)
Async XLA Ops:
  6.5 145.8 %all-reduce.3.cloned.1.call-start = ((), (), s32[]{:S(2)}) async-start(), calls=%async_computation.1 | async-start | bytes 786432 | tf_op jit(solution)/shard_map/psum | solution.py:92
  12.1 339.8 %reduce-scatter.2.cloned.1.call-start = ((), (), s32[]{:S(2)}) async-start(), calls=%async_computation.2 | async-start | bytes 7667712 | tf_op jit(solution)/shard_map/reduce_scatter | solution.py:99
Sparse Core Ops, SparseCore 0:
  12.3 139.9 all-reduce.2
  210.9 141.0 reduce-scatter.1

commit v2 on v1

--- a/solution.py
+++ b/solution.py
@@ -77,6 +77,16 @@
     )(mq, rt)
 
 
+def gather_sources(picked):
+    parts = lax.axis_size("rcv")
+    rows, span = picked.shape
+    pieces = picked.reshape(rows, parts, span // parts).transpose(1, 0, 2)
+    own = lax.all_to_all(pieces, "rcv", 0, 0).sum(axis=0, dtype=jnp.float32)
+    spread = jnp.broadcast_to(own.astype(picked.dtype)[None], (parts,) + own.shape)
+    every = lax.all_to_all(spread, "rcv", 0, 0)
+    return every.transpose(1, 0, 2).reshape(rows, span)
+
+
 def shards(traces, sources, offsets):
     ch_dev = traces.shape[0]
     span = traces.shape[2]
@@ -89,14 +99,15 @@
         traces.dtype
     )
     picked = jnp.dot(select, record, preferred_element_type=jnp.float32).astype(jnp.bfloat16)
-    source_rows = lax.psum(picked, "rcv")
+    source_rows = gather_sources(picked)
     start_at = offsets[0]
     positions = jnp.arange(span, dtype=jnp.int32)
     inside = (positions >= start_at + HALF) & (positions < start_at + HALF + SAMPLES)
     masked = jnp.where(inside[None, :], source_rows, jnp.zeros_like(source_rows))
     mq = jnp.pad(masked.astype(jnp.float32), ((0, 0), (FRONT, LANE - FRONT)))
     stacked = correlate(mq, record.T, norm_scale)
-    return lax.psum_scatter(stacked, "win", scatter_dimension=0, tiled=True)
+    groups = stacked.reshape((win_count, -1) + stacked.shape[1:])
+    return lax.all_to_all(groups, "win", 0, 0).sum(axis=0)
 
 
 def solution(mesh):

time: 363 us -> 188 us (0.52)
  waiting for transfers between devices: 272 us -> 1.35 us
  blocking collectives: 0 us -> 97.2 us
  between operations: 14.1 us -> 0.71 us
  local copies, waits for them, and re-layouts: 11.4 us -> 16.9 us
  other arithmetic: 2.79 us -> 6.88 us
    reduce_scatter x1 -> x0, waiting for transfers between devices: 141 us -> none  [shards(): return lax.psum_scatter(stacked, 'win', scatter_dimension=0, tiled=True)]
    psum x1 -> x0, waiting for transfers between devices: 131 us -> none  [shards(): source_rows = lax.psum(picked, 'rcv')]
    all_to_all x0 -> x2, blocking collectives: none -> 97.2 us  [the longest x1 80.5 us: shards(): return lax.all_to_all(groups, 'win', 0, 0).sum(axis=0)]
    reshape x0 -> x3, local copies, waits for them, and re-layouts: none -> 7.27 us  [the longest x1 7.19 us: shards(): groups = stacked.reshape((win_count, -1) + stacked.shape[1:])]
    reduce_sum x0 -> x2, other arithmetic: none -> 5.07 us  [the longest x1 5.01 us: shards(): return lax.all_to_all(groups, 'win', 0, 0).sum(axis=0)]
  transfers between devices with their start and end apart: 2 -> 1, of which waited for: 2 -> 1; matrix products, arithmetic and copies ran while one was open for 2% -> 5% of each run, Pallas kernels for 0% -> 0%
where the time goes in v2:
time: 188 us; the launch traced here: 187 us
  blocking collectives  97.2 us (52%)
  Pallas kernels  56.3 us (30%)
  local copies, waits for them, and re-layouts  16.9 us (9%)
  other arithmetic  6.88 us (4%)
  matrix products  3.98 us (2%)
  starting transfers between devices  3.55 us (2%)
    all_to_all x1, blocking collectives, shards(): return lax.all_to_all(groups, 'win', 0, 0).sum(axis=0)  80.5 us
    pallas_call x1, Pallas kernels, correlate(): pl.pallas_call(kernel, grid=(span // width,), in_specs=[pl.BlockSpec(mq.s...  56.3 us
    all_to_all x1, blocking collectives, gather_sources(): own = lax.all_to_all(pieces, 'rcv', 0, 0).sum(axis=0, dtype=jnp.float32)  16.7 us
    unnamed x1, local copies, waits for them, and re-layouts  8.67 us
    reshape x1, local copies, waits for them, and re-layouts, shards(): groups = stacked.reshape((win_count, -1) + stacked.shape[1:])  7.19 us
    reduce_sum x1, other arithmetic, shards(): return lax.all_to_all(groups, 'win', 0, 0).sum(axis=0)  5.01 us
    dot_general x1, matrix products, shards(): jnp.dot(select, record, preferred_element_type=jnp.float32)  3.98 us
  transfers between devices with their start and end apart: 1, of which 1 were waited for; matrix products, arithmetic and copies ran while one was open for 5% of the time, Pallas kernels for 0%

profile of v2, /device:TPU:8, one launch (start us, length us, event | category | flops | bytes accessed | tf_op | source)
XLA Modules:
  0.0 186.9 jit_solution(13907151757191176121)
XLA Ops:
  0.0 0.7 broadcast_subtract_fusion
  0.7 0.1 copy.8
  0.8 0.1 sub.16
  0.9 4.0 %convolution_convert_fusion = bf16[32,6144]{1,0:T(8,128)(2,1)S(1)} fusion(bf16[512,1,6144]{2,0,1:T(8,128)(2,1)} %param.3, s32[32]{0:T(128)S(1)} %sub.16), kind=kOutput, calls=%fused_computation | convolution fusion | flops 201539584 | bytes 6684800 | tf_op jit(solution)/shard_map/dot_general | solution.py:101
  4.9 16.7 %all_to_all.15 = bf16[16,32,384]{2,1,0:T(8,128)(2,1)S(1)} all-to-all(bf16[16,32,384]{2,1,0:T(8,128)(2,1)S(1)} %bitcast.23), channel_id=1, replica_groups=mesh['rcv'=16,'win'=8] {'rcv'}, dimensions={0} | all-to-all | bytes 786432 | tf_op jit(solution)/shard_map/all_to_all | solution.py:84
  21.5 0.1 reduce_sum.21
  21.6 0.8 broadcast_in_dim.20
  22.4 3.6 %all-to-all-start.1 = ((bf16[16,32,384]{2,1,0:T(8,128)(2,1)}), bf16[16,32,384]{2,1,0:T(8,128)(2,1)S(1)}, u32[]{:S(2)}, u32[]{:S(2)}) async-start(bf16[16,32,384]{2,1,0:T(8,128)(2,1)} %broadcast_in_dim.20), calls=%async_computation.1 | async-start | bytes 786432 | tf_op jit(solution)/shard_map/all_to_all | solution.py:86
  25.9 8.7 %copy.9 = bf16[512,1,6144]{0,2,1:T(8,128)(2,1)} copy(bf16[512,1,6144]{2,0,1:T(8,128)(2,1)} %param.3) | data formatting | bytes 12582912 | tf_op args[0]
  35.3 1.4 all-to-all-done.1
  36.7 1.1 pad_convert_fusion.refs_0_
  37.8 56.3 %shard_map.37 = f32[32,101,512]{2,1,0:T(8,128)} custom-call(f32[32,6272]{1,0:T(8,128)} %pad_convert_fusion.refs_0_, bf16[6144,512]{1,0:T(8,128)(2,1)} %bitcast.20), custom_call_target="tpu_custom_call" | custom-call | tf_op jit(solution)/shard_map/pallas_call | solution.py:66
  94.1 7.2 %copy.12 = f32[8,4,101,512]{3,1,2,0:T(4,128)S(1)} copy(f32[8,4,101,512]{3,2,1,0:T(8,128)} %bitcast.19) | data formatting | bytes 13238272 | tf_op jit(solution)/shard_map/reshape | solution.py:109
  101.3 80.5 %all_to_all.16 = f32[8,4,101,512]{3,1,2,0:T(4,128)} all-to-all(f32[8,4,101,512]{3,1,2,0:T(4,128)S(1)} %copy.12), channel_id=1, replica_groups=mesh['rcv'=16,'win'=8] {'win'}, dimensions={0} | all-to-all | bytes 13238272 | tf_op jit(solution)/shard_map/all_to_all | solution.py:110
  181.8 5.0 %reduce_sum.22 = f32[4,101,512]{2,0,1:T(4,128)} reduce(f32[8,4,101,512]{3,1,2,0:T(4,128)} %all_to_all.16, f32[]{:T(128)} %constant.22.clone.1), dimensions={0}, to_apply=%region_1.2 | reduce | flops 1447936 | bytes 7446532 | tf_op jit(solution)/shard_map/reduce_sum | solution.py:110
  (4 shorter events, 0.1 us)
Async XLA Ops:
  22.4 14.3 %all-to-all-start.1 = ((bf16[16,32,384]{2,1,0:T(8,128)(2,1)}), bf16[16,32,384]{2,1,0:T(8,128)(2,1)S(1)}, u32[]{:S(2)}, u32[]{:S(2)}) async-start(bf16[16,32,384]{2,1,0:T(8,128)(2,1)} %broadcast_in_dim.20), calls=%async_computation.1 | async-start | bytes 786432 | tf_op jit(solution)/shard_map/all_to_all | solution.py:86

commit v3 on v2

--- a/solution.py
+++ b/solution.py
@@ -36,7 +36,9 @@
 
     def body(p, carry):
         lhs = jnp.concatenate([lagged(2 * p), lagged(2 * p + 1)], axis=0)
-        prod = jnp.dot(lhs, rt_ref[...], preferred_element_type=jnp.float32)
+        prod = lax.dot_general(
+            lhs, rt_ref[...], (((1,), (1,)), ((), ())), preferred_element_type=jnp.float32
+        )
 
         @pl.when(q == 0)
         def _():
@@ -57,9 +59,9 @@
             out_ref[k] = acc_ref[k // 2, half : half + LAGS, :] * scale
 
 
-def correlate(mq, rt, scale):
+def correlate(mq, traces, scale):
     n_src = mq.shape[0]
-    span, ch = rt.shape
+    ch, _, span = traces.shape
     pairs = n_src // 2
     width = CHUNK if span % CHUNK == 0 else span
     kernel = lambda *refs: corr_kernel(*refs, scale=scale, pairs=pairs, width=width)
@@ -68,13 +70,13 @@
         grid=(span // width,),
         in_specs=[
             pl.BlockSpec(mq.shape, lambda q: (0, 0)),
-            pl.BlockSpec((width, ch), lambda q: (q, 0)),
+            pl.BlockSpec((ch, None, width), lambda q: (0, 0, q)),
         ],
         out_specs=pl.BlockSpec((n_src, LAGS, ch), lambda q: (0, 0, 0)),
         out_shape=jax.ShapeDtypeStruct((n_src, LAGS, ch), jnp.float32),
         scratch_shapes=[pltpu.VMEM((pairs, 2 * ROWS, ch), jnp.float32)],
         compiler_params=pltpu.CompilerParams(dimension_semantics=("arbitrary",)),
-    )(mq, rt)
+    )(mq, traces)
 
 
 def gather_sources(picked):
@@ -105,9 +107,13 @@
     inside = (positions >= start_at + HALF) & (positions < start_at + HALF + SAMPLES)
     masked = jnp.where(inside[None, :], source_rows, jnp.zeros_like(source_rows))
     mq = jnp.pad(masked.astype(jnp.float32), ((0, 0), (FRONT, LANE - FRONT)))
-    stacked = correlate(mq, record.T, norm_scale)
-    groups = stacked.reshape((win_count, -1) + stacked.shape[1:])
-    return lax.all_to_all(groups, "win", 0, 0).sum(axis=0)
+    per_group = mq.shape[0] // win_count
+    by_group = mq.reshape(win_count, per_group, mq.shape[1])
+    outs = []
+    for i in range(per_group):
+        part = correlate(by_group[:, i, :], traces, norm_scale)
+        outs.append(lax.all_to_all(part, "win", 0, 0).sum(axis=0))
+    return jnp.stack(outs, axis=0)
 
 
 def solution(mesh):

time: 188 us -> 391 us (2.08)
  Pallas kernels: 56.3 us -> 296 us
  blocking collectives: 97.2 us -> 16.7 us
  starting transfers between devices: 3.55 us -> 27.4 us
  waiting for transfers between devices: 1.35 us -> 17.7 us
    pallas_call x1 -> x4, Pallas kernels: 56.3 us -> 296 us  [correlate(): pl.pallas_call(kernel, grid=(span // width,), in_specs=[pl.BlockSpec(mq.s...]
    all_to_all x1 -> x0, blocking collectives: 80.5 us -> none  [shards(): return lax.all_to_all(groups, 'win', 0, 0).sum(axis=0)]
    all_to_all x0 -> x4, starting transfers between devices: none -> 23.9 us  [shards(): outs.append(lax.all_to_all(part, 'win', 0, 0).sum(axis=0))]
    all_to_all x0 -> x4, waiting for transfers between devices: none -> 17.7 us  [shards(): outs.append(lax.all_to_all(part, 'win', 0, 0).sum(axis=0))]
    unnamed x1 -> x7, local copies, waits for them, and re-layouts: 8.67 us -> 16.8 us
    reshape x1, local copies, waits for them, and re-layouts: 7.19 us -> 0.23 us  [shards(): by_group = mq.reshape(win_count, per_group, mq.shape[1])]
  transfers between devices with their start and end apart: 1 -> 5, of which waited for: 1 -> 1; matrix products, arithmetic and copies ran while one was open for 5% -> 5% of each run, Pallas kernels for 0% -> 57%
where the time goes in v3:
time: 391 us; the launch traced here: 389 us
  Pallas kernels  296 us (76%)
  starting transfers between devices  27.4 us (7%)
  local copies, waits for them, and re-layouts  20.7 us (5%)
  waiting for transfers between devices  17.7 us (5%)
  blocking collectives  16.7 us (4%)
  other arithmetic  5.35 us (1%)
  matrix products  3.98 us (1%)
    pallas_call x4, Pallas kernels, correlate(): pl.pallas_call(kernel, grid=(span // width,), in_specs=[pl.BlockSpec(mq.s...  296 us
    all_to_all x4, starting transfers between devices, shards(): outs.append(lax.all_to_all(part, 'win', 0, 0).sum(axis=0))  23.9 us
    all_to_all x4, waiting for transfers between devices, shards(): outs.append(lax.all_to_all(part, 'win', 0, 0).sum(axis=0))  17.7 us
    unnamed x7, local copies, waits for them, and re-layouts  16.8 us
    all_to_all x1, blocking collectives, gather_sources(): own = lax.all_to_all(pieces, 'rcv', 0, 0).sum(axis=0, dtype=jnp.float32)  16.7 us
  transfers between devices with their start and end apart: 5, of which 1 were waited for; matrix products, arithmetic and copies ran while one was open for 5% of the time, Pallas kernels for 57%

profile of v3, /device:TPU:8, one launch (start us, length us, event | category | flops | bytes accessed | tf_op | source)
XLA Modules:
  0.0 389.0 jit_solution(17117879590490953808)
XLA Ops:
  0.0 0.7 broadcast_subtract_fusion
  0.7 0.1 copy.30
  0.8 0.1 sub.16
  0.9 4.0 %convolution_convert_fusion = bf16[32,6144]{1,0:T(8,128)(2,1)S(1)} fusion(bf16[512,1,6144]{2,0,1:T(8,128)(2,1)} %param.3, s32[32]{0:T(128)S(1)} %sub.16), kind=kOutput, calls=%fused_computation | convolution fusion | flops 201539584 | bytes 6684800 | tf_op jit(solution)/shard_map/dot_general | solution.py:103
  4.9 16.7 %all_to_all.30 = bf16[16,32,384]{2,1,0:T(8,128)(2,1)S(1)} all-to-all(bf16[16,32,384]{2,1,0:T(8,128)(2,1)S(1)} %bitcast.33), channel_id=1, replica_groups=mesh['rcv'=16,'win'=8] {'rcv'}, dimensions={0} | all-to-all | bytes 786432 | tf_op jit(solution)/shard_map/all_to_all | solution.py:86
  21.5 0.1 reduce_sum.48
  21.6 0.8 broadcast_in_dim.20
  22.4 3.6 all-to-all-start.1
  25.9 12.2 %copy.34.refs_1_ = bf16[512,1,6144]{2,1,0:T(2,128)(2,1)} copy(bf16[512,1,6144]{2,0,1:T(8,128)(2,1)} %param.3) | data formatting | bytes 12582912 | tf_op args[0]
  38.9 0.2 pad_convert_fusion
  39.1 0.2 reshape.38
  39.3 1.3 fusion.3
  40.6 0.7 copy.54
  41.3 74.1 %shard_map.40 = f32[8,101,512]{2,1,0:T(8,128)} custom-call(f32[8,6272]{1,0:T(8,128)} %bitcast.40, bf16[512,1,6144]{2,1,0:T(2,128)(2,1)} %copy.34.refs_1_), custom_call_target="tpu_custom_call" | custom-call | tf_op jit(solution)/shard_map/pallas_call | solution.py:68
  115.4 6.8 %all-to-all-start.5 = ((f32[8,101,512]{2,1,0:T(8,128)}), f32[8,101,512]{2,1,0:T(8,128)S(1)}, u32[]{:S(2)}, u32[]{:S(2)}) async-start(f32[8,101,512]{2,1,0:T(8,128)} %shard_map.40), calls=%async_computation.5 | async-start | bytes 3407872 | tf_op jit(solution)/shard_map/all_to_all | solution.py:115
  122.2 0.7 copy.55
  122.8 74.0 %shard_map.39 = f32[8,101,512]{2,1,0:T(8,128)} custom-call(f32[8,6272]{1,0:T(8,128)} %bitcast.41, bf16[512,1,6144]{2,1,0:T(2,128)(2,1)} %copy.34.refs_1_), custom_call_target="tpu_custom_call" | custom-call | tf_op jit(solution)/shard_map/pallas_call | solution.py:68
  196.9 5.7 %all-to-all-start.4 = ((f32[8,101,512]{2,1,0:T(8,128)}), f32[8,101,512]{2,1,0:T(8,128)S(1)}, u32[]{:S(2)}, u32[]{:S(2)}) async-start(f32[8,101,512]{2,1,0:T(8,128)} %shard_map.39), calls=%async_computation.4 | async-start | bytes 3407872 | tf_op jit(solution)/shard_map/all_to_all | solution.py:115
  202.6 1.6 copy.57
  204.2 74.1 %shard_map.37 = f32[8,101,512]{2,1,0:T(8,128)} custom-call(f32[8,6272]{1,0:T(8,128)} %bitcast.42, bf16[512,1,6144]{2,1,0:T(2,128)(2,1)} %copy.34.refs_1_), custom_call_target="tpu_custom_call" | custom-call | tf_op jit(solution)/shard_map/pallas_call | solution.py:68
  278.3 5.7 %all-to-all-start.2 = ((f32[8,101,512]{2,1,0:T(8,128)}), f32[8,101,512]{2,1,0:T(8,128)}, u32[]{:S(2)}, u32[]{:S(2)}) async-start(f32[8,101,512]{2,1,0:T(8,128)} %shard_map.37), calls=%async_computation.2 | async-start | bytes 3407872 | tf_op jit(solution)/shard_map/all_to_all | solution.py:115
  284.0 1.6 copy.56
  285.6 74.1 %shard_map.38 = f32[8,101,512]{2,1,0:T(8,128)} custom-call(f32[8,6272]{1,0:T(8,128)} %bitcast.39, bf16[512,1,6144]{2,1,0:T(2,128)(2,1)} %copy.34.refs_1_), custom_call_target="tpu_custom_call" | custom-call | tf_op jit(solution)/shard_map/pallas_call | solution.py:68
  359.7 5.7 %all-to-all-start.3 = ((f32[8,101,512]{2,1,0:T(8,128)}), f32[8,101,512]{2,1,0:T(8,128)}, u32[]{:S(2)}, u32[]{:S(2)}) async-start(f32[8,101,512]{2,1,0:T(8,128)} %shard_map.38), calls=%async_computation.3 | async-start | bytes 3407872 | tf_op jit(solution)/shard_map/all_to_all | solution.py:115
  365.4 0.8 reduce_sum.52
  366.2 0.2 reduce_sum.51
  366.4 0.0 copy-start
  366.4 1.7 reduce_sum.49
  368.1 17.7 %all-to-all-done.3 = f32[8,101,512]{2,1,0:T(8,128)} async-done(((f32[8,101,512]{2,1,0:T(8,128)}), f32[8,101,512]{2,1,0:T(8,128)}, u32[]{:S(2)}, u32[]{:S(2)}) %all-to-all-start.3) | async-done | bytes 1654816 | tf_op jit(solution)/shard_map/all_to_all | solution.py:115
  385.8 1.6 reduce_sum.50
  387.5 0.1 pad_maximum_fusion
  387.5 1.4 copy.41
  (9 shorter events, 0.2 us)
Async XLA Ops:
  22.4 16.4 %all-to-all-start.1 = ((bf16[16,32,384]{2,1,0:T(8,128)(2,1)}), bf16[16,32,384]{2,1,0:T(8,128)(2,1)S(1)}, u32[]{:S(2)}, u32[]{:S(2)}) async-start(bf16[16,32,384]{2,1,0:T(8,128)(2,1)} %broadcast_in_dim.20), calls=%async_computation.1 | async-start | bytes 786432 | tf_op jit(solution)/shard_map/all_to_all | solution.py:88
  115.4 81.5 %all-to-all-start.5 = ((f32[8,101,512]{2,1,0:T(8,128)}), f32[8,101,512]{2,1,0:T(8,128)S(1)}, u32[]{:S(2)}, u32[]{:S(2)}) async-start(f32[8,101,512]{2,1,0:T(8,128)} %shard_map.40), calls=%async_computation.5 | async-start | bytes 3407872 | tf_op jit(solution)/shard_map/all_to_all | solution.py:115
  196.9 81.4 %all-to-all-start.4 = ((f32[8,101,512]{2,1,0:T(8,128)}), f32[8,101,512]{2,1,0:T(8,128)S(1)}, u32[]{:S(2)}, u32[]{:S(2)}) async-start(f32[8,101,512]{2,1,0:T(8,128)} %shard_map.39), calls=%async_computation.4 | async-start | bytes 3407872 | tf_op jit(solution)/shard_map/all_to_all | solution.py:115
  278.3 81.4 %all-to-all-start.2 = ((f32[8,101,512]{2,1,0:T(8,128)}), f32[8,101,512]{2,1,0:T(8,128)}, u32[]{:S(2)}, u32[]{:S(2)}) async-start(f32[8,101,512]{2,1,0:T(8,128)} %shard_map.37), calls=%async_computation.2 | async-start | bytes 3407872 | tf_op jit(solution)/shard_map/all_to_all | solution.py:115
  359.7 26.1 %all-to-all-start.3 = ((f32[8,101,512]{2,1,0:T(8,128)}), f32[8,101,512]{2,1,0:T(8,128)}, u32[]{:S(2)}, u32[]{:S(2)}) async-start(f32[8,101,512]{2,1,0:T(8,128)} %shard_map.38), calls=%async_computation.3 | async-start | bytes 3407872 | tf_op jit(solution)/shard_map/all_to_all | solution.py:115
  366.4 21.1 %copy-start = (f32[101,512]{1,0:T(8,128)S(1)}, f32[101,512]{1,0:T(8,128)}, u32[]{:S(2)}) copy-start(f32[101,512]{1,0:T(8,128)} %reduce_sum.52) | copy-start | bytes 620548

commit v4 on v2

--- a/solution.py
+++ b/solution.py
@@ -105,9 +105,14 @@
     inside = (positions >= start_at + HALF) & (positions < start_at + HALF + SAMPLES)
     masked = jnp.where(inside[None, :], source_rows, jnp.zeros_like(source_rows))
     mq = jnp.pad(masked.astype(jnp.float32), ((0, 0), (FRONT, LANE - FRONT)))
-    stacked = correlate(mq, record.T, norm_scale)
-    groups = stacked.reshape((win_count, -1) + stacked.shape[1:])
-    return lax.all_to_all(groups, "win", 0, 0).sum(axis=0)
+    per_group = mq.shape[0] // win_count
+    by_group = mq.reshape(win_count, per_group, mq.shape[1])
+    rt = record.T
+    outs = []
+    for i in range(per_group):
+        part = correlate(by_group[:, i, :], rt, norm_scale)
+        outs.append(lax.all_to_all(part, "win", 0, 0).sum(axis=0))
+    return jnp.stack(outs, axis=0)
 
 
 def solution(mesh):

time: 188 us -> 164 us (0.87)
  blocking collectives: 97.2 us -> 16.7 us
  waiting for transfers between devices: 1.35 us -> 30.4 us
  starting transfers between devices: 3.55 us -> 25.8 us
  Pallas kernels: 56.3 us -> 62.3 us
    all_to_all x1 -> x0, blocking collectives: 80.5 us -> none  [shards(): return lax.all_to_all(groups, 'win', 0, 0).sum(axis=0)]
    all_to_all x0 -> x4, waiting for transfers between devices: none -> 29.1 us  [shards(): outs.append(lax.all_to_all(part, 'win', 0, 0).sum(axis=0))]
    all_to_all x0 -> x4, starting transfers between devices: none -> 22.2 us  [shards(): outs.append(lax.all_to_all(part, 'win', 0, 0).sum(axis=0))]
    reshape x1, local copies, waits for them, and re-layouts: 7.19 us -> 0.23 us  [shards(): by_group = mq.reshape(win_count, per_group, mq.shape[1])]
    pallas_call x1 -> x4, Pallas kernels: 56.3 us -> 62.3 us  [correlate(): pl.pallas_call(kernel, grid=(span // width,), in_specs=[pl.BlockSpec(mq.s...]
    unnamed x1 -> x7, local copies, waits for them, and re-layouts: 8.67 us -> 13.3 us
    reduce_sum x1 -> x4, other arithmetic: 5.01 us -> 4.32 us  [shards(): outs.append(lax.all_to_all(part, 'win', 0, 0).sum(axis=0))]
  transfers between devices with their start and end apart: 1 -> 5, of which waited for: 1 -> 5; matrix products, arithmetic and copies ran while one was open for 5% -> 9% of each run, Pallas kernels for 0% -> 29%
where the time goes in v4:
time: 164 us; the launch traced here: 162 us
  Pallas kernels  62.3 us (38%)
  waiting for transfers between devices  30.4 us (19%)
  starting transfers between devices  25.8 us (16%)
  local copies, waits for them, and re-layouts  17.3 us (11%)
  blocking collectives  16.7 us (10%)
  other arithmetic  5.35 us (3%)
  matrix products  3.98 us (2%)
    pallas_call x4, Pallas kernels, correlate(): pl.pallas_call(kernel, grid=(span // width,), in_specs=[pl.BlockSpec(mq.s...  62.3 us
    all_to_all x4, waiting for transfers between devices, shards(): outs.append(lax.all_to_all(part, 'win', 0, 0).sum(axis=0))  29.1 us
    all_to_all x4, starting transfers between devices, shards(): outs.append(lax.all_to_all(part, 'win', 0, 0).sum(axis=0))  22.2 us
    all_to_all x1, blocking collectives, gather_sources(): own = lax.all_to_all(pieces, 'rcv', 0, 0).sum(axis=0, dtype=jnp.float32)  16.7 us
    unnamed x7, local copies, waits for them, and re-layouts  13.3 us
    reduce_sum x4, other arithmetic, shards(): outs.append(lax.all_to_all(part, 'win', 0, 0).sum(axis=0))  4.32 us
    dot_general x1, matrix products, shards(): jnp.dot(select, record, preferred_element_type=jnp.float32)  3.98 us
    all_to_all x1, starting transfers between devices, gather_sources(): every = lax.all_to_all(spread, 'rcv', 0, 0)  3.55 us
  transfers between devices with their start and end apart: 5, of which 5 were waited for; matrix products, arithmetic and copies ran while one was open for 9% of the time, Pallas kernels for 29%

profile of v4, /device:TPU:8, one launch (start us, length us, event | category | flops | bytes accessed | tf_op | source)
XLA Modules:
  0.0 162.5 jit_solution(8762959590859810654)
XLA Ops:
  0.0 0.7 broadcast_subtract_fusion
  0.7 0.1 copy.21
  0.9 4.0 %convolution_convert_fusion = bf16[32,6144]{1,0:T(8,128)(2,1)S(1)} fusion(bf16[512,1,6144]{2,0,1:T(8,128)(2,1)} %param.3, s32[32]{0:T(128)S(1)} %sub.16), kind=kOutput, calls=%fused_computation | convolution fusion | flops 201539584 | bytes 6684800 | tf_op jit(solution)/shard_map/dot_general | solution.py:101
  4.9 16.7 %all_to_all.30 = bf16[16,32,384]{2,1,0:T(8,128)(2,1)S(1)} all-to-all(bf16[16,32,384]{2,1,0:T(8,128)(2,1)S(1)} %bitcast.40), channel_id=1, replica_groups=mesh['rcv'=16,'win'=8] {'rcv'}, dimensions={0} | all-to-all | bytes 786432 | tf_op jit(solution)/shard_map/all_to_all | solution.py:84
  21.6 0.8 broadcast_in_dim.20
  22.4 3.6 %all-to-all-start.1 = ((bf16[16,32,384]{2,1,0:T(8,128)(2,1)}), bf16[16,32,384]{2,1,0:T(8,128)(2,1)S(1)}, u32[]{:S(2)}, u32[]{:S(2)}) async-start(bf16[16,32,384]{2,1,0:T(8,128)(2,1)} %broadcast_in_dim.20), calls=%async_computation.1 | async-start | bytes 786432 | tf_op jit(solution)/shard_map/all_to_all | solution.py:86
  25.9 8.7 %copy.22 = bf16[512,1,6144]{0,2,1:T(8,128)(2,1)} copy(bf16[512,1,6144]{2,0,1:T(8,128)(2,1)} %param.3) | data formatting | bytes 12582912 | tf_op args[0]
  35.3 1.3 all-to-all-done.1
  36.7 0.2 pad_convert_fusion
  36.9 0.2 reshape.38
  37.2 1.3 fusion.3
  38.4 0.7 copy.42
  39.1 15.5 %shard_map.40 = f32[8,101,512]{2,1,0:T(8,128)} custom-call(f32[8,6272]{1,0:T(8,128)} %bitcast.47, bf16[6144,512]{1,0:T(8,128)(2,1)} %bitcast.34), custom_call_target="tpu_custom_call" | custom-call | tf_op jit(solution)/shard_map/pallas_call | solution.py:66
  54.7 6.8 %all-to-all-start.5 = ((f32[8,101,512]{2,1,0:T(8,128)}), f32[8,101,512]{2,1,0:T(8,128)S(1)}, u32[]{:S(2)}, u32[]{:S(2)}) async-start(f32[8,101,512]{2,1,0:T(8,128)} %shard_map.40), calls=%async_computation.5 | async-start | bytes 3407872 | tf_op jit(solution)/shard_map/all_to_all | solution.py:114
  61.4 0.7 copy.43
  62.1 15.6 %shard_map.39 = f32[8,101,512]{2,1,0:T(8,128)} custom-call(f32[8,6272]{1,0:T(8,128)} %bitcast.48, bf16[6144,512]{1,0:T(8,128)(2,1)} %bitcast.35), custom_call_target="tpu_custom_call" | custom-call | tf_op jit(solution)/shard_map/pallas_call | solution.py:66
  77.8 4.9 %all-to-all-done.5 = f32[8,101,512]{2,1,0:T(8,128)S(1)} async-done(((f32[8,101,512]{2,1,0:T(8,128)}), f32[8,101,512]{2,1,0:T(8,128)S(1)}, u32[]{:S(2)}, u32[]{:S(2)}) %all-to-all-start.5) | async-done | bytes 1654816 | tf_op jit(solution)/shard_map/all_to_all | solution.py:114
  82.6 4.7 %all-to-all-start.4 = ((f32[8,101,512]{2,1,0:T(8,128)}), f32[8,101,512]{2,1,0:T(8,128)S(1)}, u32[]{:S(2)}, u32[]{:S(2)}) async-start(f32[8,101,512]{2,1,0:T(8,128)} %shard_map.39), calls=%async_computation.4 | async-start | bytes 3407872 | tf_op jit(solution)/shard_map/all_to_all | solution.py:114
  87.3 1.6 copy.45
  88.9 15.5 %shard_map.37 = f32[8,101,512]{2,1,0:T(8,128)} custom-call(f32[8,6272]{1,0:T(8,128)} %bitcast.49, bf16[6144,512]{1,0:T(8,128)(2,1)} %bitcast.36), custom_call_target="tpu_custom_call" | custom-call | tf_op jit(solution)/shard_map/pallas_call | solution.py:66
  104.5 3.8 %all-to-all-done.4 = f32[8,101,512]{2,1,0:T(8,128)S(1)} async-done(((f32[8,101,512]{2,1,0:T(8,128)}), f32[8,101,512]{2,1,0:T(8,128)S(1)}, u32[]{:S(2)}, u32[]{:S(2)}) %all-to-all-start.4) | async-done | bytes 1654816 | tf_op jit(solution)/shard_map/all_to_all | solution.py:114
  108.3 5.4 %all-to-all-start.2 = ((f32[8,101,512]{2,1,0:T(8,128)}), f32[8,101,512]{2,1,0:T(8,128)}, u32[]{:S(2)}, u32[]{:S(2)}) async-start(f32[8,101,512]{2,1,0:T(8,128)} %shard_map.37), calls=%async_computation.2 | async-start | bytes 3407872 | tf_op jit(solution)/shard_map/all_to_all | solution.py:114
  113.7 1.6 copy.44
  115.3 15.5 %shard_map.38 = f32[8,101,512]{2,1,0:T(8,128)} custom-call(f32[8,6272]{1,0:T(8,128)} %bitcast.46, bf16[6144,512]{1,0:T(8,128)(2,1)} %bitcast.37), custom_call_target="tpu_custom_call" | custom-call | tf_op jit(solution)/shard_map/pallas_call | solution.py:66
  130.8 3.2 %all-to-all-done.2 = f32[8,101,512]{2,1,0:T(8,128)} async-done(((f32[8,101,512]{2,1,0:T(8,128)}), f32[8,101,512]{2,1,0:T(8,128)}, u32[]{:S(2)}, u32[]{:S(2)}) %all-to-all-start.2) | async-done | bytes 1654816 | tf_op jit(solution)/shard_map/all_to_all | solution.py:114
  134.0 5.3 %all-to-all-start.3 = ((f32[8,101,512]{2,1,0:T(8,128)}), f32[8,101,512]{2,1,0:T(8,128)}, u32[]{:S(2)}, u32[]{:S(2)}) async-start(f32[8,101,512]{2,1,0:T(8,128)} %shard_map.38), calls=%async_computation.3 | async-start | bytes 3407872 | tf_op jit(solution)/shard_map/all_to_all | solution.py:114
  139.3 0.8 reduce_sum.52
  140.2 0.2 reduce_sum.51
  140.4 1.7 %reduce_sum.49 = f32[101,512]{1,0:T(8,128)S(1)} reduce(f32[8,101,512]{2,1,0:T(8,128)} %all-to-all-done.2, f32[]{:T(128)} %constant.22.clone.1), dimensions={0}, to_apply=%region_1.2 | reduce | flops 361984 | bytes 1861636 | tf_op jit(solution)/shard_map/reduce_sum | solution.py:114
  142.1 17.3 %all-to-all-done.3 = f32[8,101,512]{2,1,0:T(8,128)} async-done(((f32[8,101,512]{2,1,0:T(8,128)}), f32[8,101,512]{2,1,0:T(8,128)}, u32[]{:S(2)}, u32[]{:S(2)}) %all-to-all-start.3) | async-done | bytes 1654816 | tf_op jit(solution)/shard_map/all_to_all | solution.py:114
  159.3 1.6 %reduce_sum.50 = f32[101,512]{1,0:T(8,128)S(1)} reduce(f32[8,101,512]{2,1,0:T(8,128)} %all-to-all-done.3, f32[]{:T(128)} %constant.22.clone.1), dimensions={0}, to_apply=%region_2.3 | reduce | flops 361984 | bytes 1861636 | tf_op jit(solution)/shard_map/reduce_sum | solution.py:114
  161.0 1.4 copy.29
  (9 shorter events, 0.3 us)
Async XLA Ops:
  22.4 14.3 %all-to-all-start.1 = ((bf16[16,32,384]{2,1,0:T(8,128)(2,1)}), bf16[16,32,384]{2,1,0:T(8,128)(2,1)S(1)}, u32[]{:S(2)}, u32[]{:S(2)}) async-start(bf16[16,32,384]{2,1,0:T(8,128)(2,1)} %broadcast_in_dim.20), calls=%async_computation.1 | async-start | bytes 786432 | tf_op jit(solution)/shard_map/all_to_all | solution.py:86
  54.7 28.0 %all-to-all-start.5 = ((f32[8,101,512]{2,1,0:T(8,128)}), f32[8,101,512]{2,1,0:T(8,128)S(1)}, u32[]{:S(2)}, u32[]{:S(2)}) async-start(f32[8,101,512]{2,1,0:T(8,128)} %shard_map.40), calls=%async_computation.5 | async-start | bytes 3407872 | tf_op jit(solution)/shard_map/all_to_all | solution.py:114
  82.6 25.6 %all-to-all-start.4 = ((f32[8,101,512]{2,1,0:T(8,128)}), f32[8,101,512]{2,1,0:T(8,128)S(1)}, u32[]{:S(2)}, u32[]{:S(2)}) async-start(f32[8,101,512]{2,1,0:T(8,128)} %shard_map.39), calls=%async_computation.4 | async-start | bytes 3407872 | tf_op jit(solution)/shard_map/all_to_all | solution.py:114
  108.3 25.7 %all-to-all-start.2 = ((f32[8,101,512]{2,1,0:T(8,128)}), f32[8,101,512]{2,1,0:T(8,128)}, u32[]{:S(2)}, u32[]{:S(2)}) async-start(f32[8,101,512]{2,1,0:T(8,128)} %shard_map.37), calls=%async_computation.2 | async-start | bytes 3407872 | tf_op jit(solution)/shard_map/all_to_all | solution.py:114
  134.0 25.3 %all-to-all-start.3 = ((f32[8,101,512]{2,1,0:T(8,128)}), f32[8,101,512]{2,1,0:T(8,128)}, u32[]{:S(2)}, u32[]{:S(2)}) async-start(f32[8,101,512]{2,1,0:T(8,128)} %shard_map.38), calls=%async_computation.3 | async-start | bytes 3407872 | tf_op jit(solution)/shard_map/all_to_all | solution.py:114
  140.4 20.6 %copy-start = (f32[101,512]{1,0:T(8,128)S(1)}, f32[101,512]{1,0:T(8,128)}, u32[]{:S(2)}) copy-start(f32[101,512]{1,0:T(8,128)} %reduce_sum.52) | copy-start | bytes 620548

commit v5 on v4

--- a/solution.py
+++ b/solution.py
@@ -13,10 +13,10 @@
 ROWS = 128
 LANE = 128
 FRONT = ROWS - HALF
-CHUNK = 1024
+CHUNK = 2048
 
 
-def corr_kernel(mq_ref, rt_ref, out_ref, acc_ref, *, scale, pairs, width):
+def corr_kernel(mq_ref, rt_ref, out_ref, acc_ref, lag_ref, *, scale, pairs, width):
     q = pl.program_id(0)
     u0 = pl.multiple_of(q * width, LANE)
     row = lax.broadcasted_iota(jnp.int32, (ROWS, LANE), 0)
@@ -24,31 +24,28 @@
     keep = lane >= row
     blocks = width // LANE
 
-    def lagged(k):
-        line = mq_ref[pl.ds(k, 1), pl.ds(u0, width + LANE)]
-        wide = jnp.broadcast_to(line, (ROWS, width + LANE))
-        turned = [
-            pltpu.roll(wide[:, b * LANE : (b + 1) * LANE], 0, 1, stride=1, stride_axis=0)
-            for b in range(blocks + 1)
-        ]
-        parts = [jnp.where(keep, turned[b + 1], turned[b]) for b in range(blocks)]
-        return jnp.concatenate(parts, axis=1).astype(jnp.bfloat16)
+    def turned(k, b):
+        line = mq_ref[pl.ds(k, 1), pl.ds(u0 + b * LANE, LANE)]
+        return pltpu.roll(jnp.broadcast_to(line, (ROWS, LANE)), 0, 1, stride=1, stride_axis=0)
 
-    def body(p, carry):
-        lhs = jnp.concatenate([lagged(2 * p), lagged(2 * p + 1)], axis=0)
-        prod = jnp.dot(lhs, rt_ref[...], preferred_element_type=jnp.float32)
+    def build(k, slot, half):
+        prev = turned(k, 0)
+        for b in range(blocks):
+            cur = turned(k, b + 1)
+            lag_ref[slot, half * ROWS : (half + 1) * ROWS, b * LANE : (b + 1) * LANE] = jnp.where(
+                keep, cur, prev
+            ).astype(jnp.bfloat16)
+            prev = cur
 
-        @pl.when(q == 0)
-        def _():
-            acc_ref[p] = prod
+    @pl.when(q == 0)
+    def _():
+        acc_ref[...] = jnp.zeros_like(acc_ref)
 
-        @pl.when(q > 0)
-        def _():
-            acc_ref[p] = acc_ref[p] + prod
-
-        return carry
-
-    lax.fori_loop(0, pairs, body, 0)
+    for p in range(pairs):
+        slot = p % 2
+        build(2 * p, slot, 0)
+        build(2 * p + 1, slot, 1)
+        acc_ref[p] += jnp.dot(lag_ref[slot], rt_ref[...], preferred_element_type=jnp.float32)
 
     @pl.when(q == pl.num_programs(0) - 1)
     def _():
@@ -72,7 +69,10 @@
         ],
         out_specs=pl.BlockSpec((n_src, LAGS, ch), lambda q: (0, 0, 0)),
         out_shape=jax.ShapeDtypeStruct((n_src, LAGS, ch), jnp.float32),
-        scratch_shapes=[pltpu.VMEM((pairs, 2 * ROWS, ch), jnp.float32)],
+        scratch_shapes=[
+            pltpu.VMEM((pairs, 2 * ROWS, ch), jnp.float32),
+            pltpu.VMEM((2, 2 * ROWS, width), jnp.bfloat16),
+        ],
         compiler_params=pltpu.CompilerParams(dimension_semantics=("arbitrary",)),
     )(mq, rt)
 

time: 164 us -> 159 us (0.970)
  Pallas kernels: 62.3 us -> 41.7 us
  waiting for transfers between devices: 30.4 us -> 45.8 us
    pallas_call x4, Pallas kernels: 62.3 us -> 41.7 us  [correlate(): pl.pallas_call(kernel, grid=(span // width,), in_specs=[pl.BlockSpec(mq.s...]
    all_to_all x4, waiting for transfers between devices: 29.1 us -> 44.5 us  [shards(): outs.append(lax.all_to_all(part, 'win', 0, 0).sum(axis=0))]
  transfers between devices with their start and end apart: 5 -> 5, of which waited for: 5 -> 5; matrix products, arithmetic and copies ran while one was open for 9% -> 10% of each run, Pallas kernels for 29% -> 20%
where the time goes in v5:
time: 159 us; the launch traced here: 157 us
  waiting for transfers between devices  45.8 us (29%)
  Pallas kernels  41.7 us (26%)
  starting transfers between devices  25.8 us (16%)
  local copies, waits for them, and re-layouts  17.3 us (11%)
  blocking collectives  16.7 us (11%)
  other arithmetic  5.35 us (3%)
  matrix products  3.98 us (3%)
    all_to_all x4, waiting for transfers between devices, shards(): outs.append(lax.all_to_all(part, 'win', 0, 0).sum(axis=0))  44.5 us
    pallas_call x4, Pallas kernels, correlate(): pl.pallas_call(kernel, grid=(span // width,), in_specs=[pl.BlockSpec(mq.s...  41.7 us
    all_to_all x4, starting transfers between devices, shards(): outs.append(lax.all_to_all(part, 'win', 0, 0).sum(axis=0))  22.2 us
    all_to_all x1, blocking collectives, gather_sources(): own = lax.all_to_all(pieces, 'rcv', 0, 0).sum(axis=0, dtype=jnp.float32)  16.7 us
    unnamed x7, local copies, waits for them, and re-layouts  13.3 us
    reduce_sum x4, other arithmetic, shards(): outs.append(lax.all_to_all(part, 'win', 0, 0).sum(axis=0))  4.32 us
    dot_general x1, matrix products, shards(): jnp.dot(select, record, preferred_element_type=jnp.float32)  3.98 us
    all_to_all x1, starting transfers between devices, gather_sources(): every = lax.all_to_all(spread, 'rcv', 0, 0)  3.55 us
  transfers between devices with their start and end apart: 5, of which 5 were waited for; matrix products, arithmetic and copies ran while one was open for 10% of the time, Pallas kernels for 20%

profile of v5, /device:TPU:8, one launch (start us, length us, event | category | flops | bytes accessed | tf_op | source)
XLA Modules:
  0.0 157.3 jit_solution(7720049244919523370)
XLA Ops:
  0.0 0.7 broadcast_subtract_fusion
  0.7 0.1 copy.21
  0.9 4.0 %convolution_convert_fusion = bf16[32,6144]{1,0:T(8,128)(2,1)S(1)} fusion(bf16[512,1,6144]{2,0,1:T(8,128)(2,1)} %param.3, s32[32]{0:T(128)S(1)} %sub.16), kind=kOutput, calls=%fused_computation | convolution fusion | flops 201539584 | bytes 6684800 | tf_op jit(solution)/shard_map/dot_general | solution.py:101
  4.9 16.7 %all_to_all.30 = bf16[16,32,384]{2,1,0:T(8,128)(2,1)S(1)} all-to-all(bf16[16,32,384]{2,1,0:T(8,128)(2,1)S(1)} %bitcast.40), channel_id=1, replica_groups=mesh['rcv'=16,'win'=8] {'rcv'}, dimensions={0} | all-to-all | bytes 786432 | tf_op jit(solution)/shard_map/all_to_all | solution.py:84
  21.6 0.8 broadcast_in_dim.20
  22.4 3.6 %all-to-all-start.1 = ((bf16[16,32,384]{2,1,0:T(8,128)(2,1)}), bf16[16,32,384]{2,1,0:T(8,128)(2,1)S(1)}, u32[]{:S(2)}, u32[]{:S(2)}) async-start(bf16[16,32,384]{2,1,0:T(8,128)(2,1)} %broadcast_in_dim.20), calls=%async_computation.1 | async-start | bytes 786432 | tf_op jit(solution)/shard_map/all_to_all | solution.py:86
  25.9 8.7 %copy.22 = bf16[512,1,6144]{0,2,1:T(8,128)(2,1)} copy(bf16[512,1,6144]{2,0,1:T(8,128)(2,1)} %param.3) | data formatting | bytes 12582912 | tf_op args[0]
  35.3 1.3 all-to-all-done.1
  36.7 0.2 pad_convert_fusion
  36.9 0.2 reshape.38
  37.2 1.3 fusion.3
  38.4 0.7 copy.42
  39.1 10.4 %shard_map.40 = f32[8,101,512]{2,1,0:T(8,128)} custom-call(f32[8,6272]{1,0:T(8,128)} %bitcast.47, bf16[6144,512]{1,0:T(8,128)(2,1)} %bitcast.34), custom_call_target="tpu_custom_call" | custom-call | tf_op jit(solution)/shard_map/pallas_call | solution.py:63
  49.5 6.8 %all-to-all-start.5 = ((f32[8,101,512]{2,1,0:T(8,128)}), f32[8,101,512]{2,1,0:T(8,128)S(1)}, u32[]{:S(2)}, u32[]{:S(2)}) async-start(f32[8,101,512]{2,1,0:T(8,128)} %shard_map.40), calls=%async_computation.5 | async-start | bytes 3407872 | tf_op jit(solution)/shard_map/all_to_all | solution.py:114
  56.3 0.7 copy.43
  57.0 10.5 %shard_map.39 = f32[8,101,512]{2,1,0:T(8,128)} custom-call(f32[8,6272]{1,0:T(8,128)} %bitcast.48, bf16[6144,512]{1,0:T(8,128)(2,1)} %bitcast.35), custom_call_target="tpu_custom_call" | custom-call | tf_op jit(solution)/shard_map/pallas_call | solution.py:63
  67.5 10.0 %all-to-all-done.5 = f32[8,101,512]{2,1,0:T(8,128)S(1)} async-done(((f32[8,101,512]{2,1,0:T(8,128)}), f32[8,101,512]{2,1,0:T(8,128)S(1)}, u32[]{:S(2)}, u32[]{:S(2)}) %all-to-all-start.5) | async-done | bytes 1654816 | tf_op jit(solution)/shard_map/all_to_all | solution.py:114
  77.5 4.7 %all-to-all-start.4 = ((f32[8,101,512]{2,1,0:T(8,128)}), f32[8,101,512]{2,1,0:T(8,128)S(1)}, u32[]{:S(2)}, u32[]{:S(2)}) async-start(f32[8,101,512]{2,1,0:T(8,128)} %shard_map.39), calls=%async_computation.4 | async-start | bytes 3407872 | tf_op jit(solution)/shard_map/all_to_all | solution.py:114
  82.2 1.6 %copy.45 = f32[8,1,6272]{2,0,1:T(8,128)} copy(f32[8,1,6272]{2,1,0:T(1,128)} %get-tuple-element.5) | data formatting | bytes 401408
  83.8 10.4 %shard_map.37 = f32[8,101,512]{2,1,0:T(8,128)} custom-call(f32[8,6272]{1,0:T(8,128)} %bitcast.49, bf16[6144,512]{1,0:T(8,128)(2,1)} %bitcast.36), custom_call_target="tpu_custom_call" | custom-call | tf_op jit(solution)/shard_map/pallas_call | solution.py:63
  94.2 8.9 %all-to-all-done.4 = f32[8,101,512]{2,1,0:T(8,128)S(1)} async-done(((f32[8,101,512]{2,1,0:T(8,128)}), f32[8,101,512]{2,1,0:T(8,128)S(1)}, u32[]{:S(2)}, u32[]{:S(2)}) %all-to-all-start.4) | async-done | bytes 1654816 | tf_op jit(solution)/shard_map/all_to_all | solution.py:114
  103.1 5.4 %all-to-all-start.2 = ((f32[8,101,512]{2,1,0:T(8,128)}), f32[8,101,512]{2,1,0:T(8,128)}, u32[]{:S(2)}, u32[]{:S(2)}) async-start(f32[8,101,512]{2,1,0:T(8,128)} %shard_map.37), calls=%async_computation.2 | async-start | bytes 3407872 | tf_op jit(solution)/shard_map/all_to_all | solution.py:114
  108.5 1.6 %copy.44 = f32[8,1,6272]{2,0,1:T(8,128)} copy(f32[8,1,6272]{2,1,0:T(1,128)} %get-tuple-element.7) | data formatting | bytes 401408
  110.1 10.4 %shard_map.38 = f32[8,101,512]{2,1,0:T(8,128)} custom-call(f32[8,6272]{1,0:T(8,128)} %bitcast.46, bf16[6144,512]{1,0:T(8,128)(2,1)} %bitcast.37), custom_call_target="tpu_custom_call" | custom-call | tf_op jit(solution)/shard_map/pallas_call | solution.py:63
  120.5 8.3 %all-to-all-done.2 = f32[8,101,512]{2,1,0:T(8,128)} async-done(((f32[8,101,512]{2,1,0:T(8,128)}), f32[8,101,512]{2,1,0:T(8,128)}, u32[]{:S(2)}, u32[]{:S(2)}) %all-to-all-start.2) | async-done | bytes 1654816 | tf_op jit(solution)/shard_map/all_to_all | solution.py:114
  128.9 5.3 %all-to-all-start.3 = ((f32[8,101,512]{2,1,0:T(8,128)}), f32[8,101,512]{2,1,0:T(8,128)}, u32[]{:S(2)}, u32[]{:S(2)}) async-start(f32[8,101,512]{2,1,0:T(8,128)} %shard_map.38), calls=%async_computation.3 | async-start | bytes 3407872 | tf_op jit(solution)/shard_map/all_to_all | solution.py:114
  134.2 0.8 reduce_sum.52
  135.0 0.2 reduce_sum.51
  135.2 1.7 %reduce_sum.49 = f32[101,512]{1,0:T(8,128)S(1)} reduce(f32[8,101,512]{2,1,0:T(8,128)} %all-to-all-done.2, f32[]{:T(128)} %constant.22.clone.1), dimensions={0}, to_apply=%region_1.2 | reduce | flops 361984 | bytes 1861636 | tf_op jit(solution)/shard_map/reduce_sum | solution.py:114
  136.9 17.3 %all-to-all-done.3 = f32[8,101,512]{2,1,0:T(8,128)} async-done(((f32[8,101,512]{2,1,0:T(8,128)}), f32[8,101,512]{2,1,0:T(8,128)}, u32[]{:S(2)}, u32[]{:S(2)}) %all-to-all-start.3) | async-done | bytes 1654816 | tf_op jit(solution)/shard_map/all_to_all | solution.py:114
  154.2 1.6 %reduce_sum.50 = f32[101,512]{1,0:T(8,128)S(1)} reduce(f32[8,101,512]{2,1,0:T(8,128)} %all-to-all-done.3, f32[]{:T(128)} %constant.22.clone.1), dimensions={0}, to_apply=%region_2.3 | reduce | flops 361984 | bytes 1861636 | tf_op jit(solution)/shard_map/reduce_sum | solution.py:114
  155.9 1.4 copy.29
  (9 shorter events, 0.3 us)
Async XLA Ops:
  22.4 14.3 %all-to-all-start.1 = ((bf16[16,32,384]{2,1,0:T(8,128)(2,1)}), bf16[16,32,384]{2,1,0:T(8,128)(2,1)S(1)}, u32[]{:S(2)}, u32[]{:S(2)}) async-start(bf16[16,32,384]{2,1,0:T(8,128)(2,1)} %broadcast_in_dim.20), calls=%async_computation.1 | async-start | bytes 786432 | tf_op jit(solution)/shard_map/all_to_all | solution.py:86
  49.5 28.0 %all-to-all-start.5 = ((f32[8,101,512]{2,1,0:T(8,128)}), f32[8,101,512]{2,1,0:T(8,128)S(1)}, u32[]{:S(2)}, u32[]{:S(2)}) async-start(f32[8,101,512]{2,1,0:T(8,128)} %shard_map.40), calls=%async_computation.5 | async-start | bytes 3407872 | tf_op jit(solution)/shard_map/all_to_all | solution.py:114
  77.5 25.6 %all-to-all-start.4 = ((f32[8,101,512]{2,1,0:T(8,128)}), f32[8,101,512]{2,1,0:T(8,128)S(1)}, u32[]{:S(2)}, u32[]{:S(2)}) async-start(f32[8,101,512]{2,1,0:T(8,128)} %shard_map.39), calls=%async_computation.4 | async-start | bytes 3407872 | tf_op jit(solution)/shard_map/all_to_all | solution.py:114
  103.1 25.7 %all-to-all-start.2 = ((f32[8,101,512]{2,1,0:T(8,128)}), f32[8,101,512]{2,1,0:T(8,128)}, u32[]{:S(2)}, u32[]{:S(2)}) async-start(f32[8,101,512]{2,1,0:T(8,128)} %shard_map.37), calls=%async_computation.2 | async-start | bytes 3407872 | tf_op jit(solution)/shard_map/all_to_all | solution.py:114
  128.9 25.3 %all-to-all-start.3 = ((f32[8,101,512]{2,1,0:T(8,128)}), f32[8,101,512]{2,1,0:T(8,128)}, u32[]{:S(2)}, u32[]{:S(2)}) async-start(f32[8,101,512]{2,1,0:T(8,128)} %shard_map.38), calls=%async_computation.3 | async-start | bytes 3407872 | tf_op jit(solution)/shard_map/all_to_all | solution.py:114
  135.2 20.6 %copy-start = (f32[101,512]{1,0:T(8,128)S(1)}, f32[101,512]{1,0:T(8,128)}, u32[]{:S(2)}) copy-start(f32[101,512]{1,0:T(8,128)} %reduce_sum.52) | copy-start | bytes 620548

commit v6 on v5

--- a/solution.py
+++ b/solution.py
@@ -87,6 +87,15 @@
     return every.transpose(1, 0, 2).reshape(rows, span)
 
 
+def exchange(part, count):
+    me = lax.axis_index("win")
+    total = lax.dynamic_index_in_dim(part, me, 0, keepdims=False)
+    for d in range(1, count):
+        sent = lax.dynamic_index_in_dim(part, (me + d) % count, 0, keepdims=False)
+        total = total + lax.ppermute(sent, "win", [(i, (i + d) % count) for i in range(count)])
+    return total
+
+
 def shards(traces, sources, offsets):
     ch_dev = traces.shape[0]
     span = traces.shape[2]
@@ -111,7 +120,7 @@
     outs = []
     for i in range(per_group):
         part = correlate(by_group[:, i, :], rt, norm_scale)
-        outs.append(lax.all_to_all(part, "win", 0, 0).sum(axis=0))
+        outs.append(exchange(part, win_count))
     return jnp.stack(outs, axis=0)
 
 

time: 159 us -> 164 us (1.031)
  starting transfers between devices: 25.8 us -> 40.2 us
  waiting for transfers between devices: 45.8 us -> 32.8 us
  local copies, waits for them, and re-layouts: 17.3 us -> 21.6 us
    all_to_all x4 -> x0, waiting for transfers between devices: 44.5 us -> none  [shards(): outs.append(lax.all_to_all(part, 'win', 0, 0).sum(axis=0))]
    ppermute x0 -> x28, starting transfers between devices: none -> 36.6 us  [exchange(): lax.ppermute(sent, 'win', [(i, (i + d) % count) for i in range(count)])]
    ppermute x0 -> x28, waiting for transfers between devices: none -> 31.6 us  [exchange(): lax.ppermute(sent, 'win', [(i, (i + d) % count) for i in range(count)])]
    all_to_all x4 -> x0, starting transfers between devices: 22.2 us -> none  [shards(): outs.append(lax.all_to_all(part, 'win', 0, 0).sum(axis=0))]
    squeeze x0 -> x6, local copies, waits for them, and re-layouts: none -> 9.66 us  [the longest x4 8.1 us: exchange(): sent = lax.dynamic_index_in_dim(part, (me + d) % count, 0, keepdims=False)]
    unnamed x7 -> x13, local copies, waits for them, and re-layouts: 13.3 us -> 8.67 us
    another operation x1 -> x5, other arithmetic: 0.06 us -> 4.63 us  [shards(): return jnp.stack(outs, axis=0)]
    reduce_sum x4 -> x0, other arithmetic: 4.32 us -> none  [shards(): outs.append(lax.all_to_all(part, 'win', 0, 0).sum(axis=0))]
  transfers between devices with their start and end apart: 5 -> 29, of which waited for: 5 -> 7; matrix products, arithmetic and copies ran while one was open for 10% -> 12% of each run, Pallas kernels for 20% -> 19%
where the time goes in v6:
time: 164 us
  Pallas kernels  41.8 us (25%)
  starting transfers between devices  40.2 us (25%)
  waiting for transfers between devices  32.8 us (20%)
  local copies, waits for them, and re-layouts  21.6 us (13%)
  blocking collectives  16.7 us (10%)
  other arithmetic  5.61 us (3%)
  matrix products  3.98 us (2%)
    pallas_call x4, Pallas kernels, correlate(): pl.pallas_call(kernel, grid=(span // width,), in_specs=[pl.BlockSpec(mq.s...  41.8 us
    ppermute x28, starting transfers between devices, exchange(): lax.ppermute(sent, 'win', [(i, (i + d) % count) for i in range(count)])  36.6 us
    ppermute x28, waiting for transfers between devices, exchange(): lax.ppermute(sent, 'win', [(i, (i + d) % count) for i in range(count)])  31.6 us
    all_to_all x1, blocking collectives, gather_sources(): own = lax.all_to_all(pieces, 'rcv', 0, 0).sum(axis=0, dtype=jnp.float32)  16.7 us
    unnamed x13, local copies, waits for them, and re-layouts  8.67 us
    squeeze x4, local copies, waits for them, and re-layouts, exchange(): sent = lax.dynamic_index_in_dim(part, (me + d) % count, 0, keepdims=False)  8.1 us
    another operation x5, other arithmetic, shards(): return jnp.stack(outs, axis=0)  4.63 us
    dot_general x1, matrix products, shards(): jnp.dot(select, record, preferred_element_type=jnp.float32)  3.98 us
  transfers between devices with their start and end apart: 29, of which 7 were waited for; matrix products, arithmetic and copies ran while one was open for 12% of the time, Pallas kernels for 19%

profile of v6, /device:TPU:8, one launch (start us, length us, event | category | flops | bytes accessed | tf_op | source)
XLA Modules:
  0.0 163.7 jit_solution(9570370350080633636)
XLA Ops:
  0.9 4.0 %convolution_convert_fusion = bf16[32,6144]{1,0:T(8,128)(2,1)S(1)} fusion(bf16[512,1,6144]{2,0,1:T(8,128)(2,1)} %param.3, s32[32]{0:T(128)S(1)} %sub.16), kind=kOutput, calls=%fused_computation | convolution fusion | flops 201539584 | bytes 6684800 | tf_op jit(solution)/shard_map/dot_general | solution.py:110
  4.9 16.7 %all_to_all.10 = bf16[16,32,384]{2,1,0:T(8,128)(2,1)S(1)} all-to-all(bf16[16,32,384]{2,1,0:T(8,128)(2,1)S(1)} %bitcast.160), channel_id=1, replica_groups=mesh['rcv'=16,'win'=8] {'rcv'}, dimensions={0} | all-to-all | bytes 786432 | tf_op jit(solution)/shard_map/all_to_all | solution.py:84
  22.4 3.6 %all-to-all-start.1 = ((bf16[16,32,384]{2,1,0:T(8,128)(2,1)}), bf16[16,32,384]{2,1,0:T(8,128)(2,1)S(1)}, u32[]{:S(2)}, u32[]{:S(2)}) async-start(bf16[16,32,384]{2,1,0:T(8,128)(2,1)} %broadcast_in_dim.20), calls=%async_computation.1 | async-start | bytes 786432 | tf_op jit(solution)/shard_map/all_to_all | solution.py:86
  26.0 8.6 %copy.22 = bf16[512,1,6144]{0,2,1:T(8,128)(2,1)} copy(bf16[512,1,6144]{2,0,1:T(8,128)(2,1)} %param.3) | data formatting | bytes 12582912 | tf_op args[0]
  38.5 10.5 %shard_map.40 = f32[8,101,512]{2,1,0:T(8,128)} custom-call(f32[8,6272]{1,0:T(8,128)} %get-tuple-element.37.refs_0_, bf16[6144,512]{1,0:T(8,128)(2,1)} %bitcast.154), custom_call_target="tpu_custom_call" | custom-call | tf_op jit(solution)/shard_map/pallas_call | solution.py:63
  49.0 1.6 dynamic-slice_bitcast_fusion.6
  50.5 2.8 %collective-permute-start.21 = (f32[101,512]{1,0:T(8,128)S(1)}, f32[101,512]{1,0:T(8,128)S(1)}, u32[]{:S(2)}, u32[]{:S(2)}) collective-permute-start(f32[101,512]{1,0:T(8,128)S(1)} %get-tuple-element.26), channel_id=1, source_target_pairs={{0,1},{1,2},{2,3},{3,4},{4,5},{5,6},{6,7},{7,0},{8,9},{9,10},{10,1... | collective-permute-start | bytes 620552 | tf_op jit(solution)/shard_map/ppermute | solution.py:95
  53.3 3.4 %collective-permute-start.26 = (f32[101,512]{1,0:T(8,128)S(1)}, f32[101,512]{1,0:T(8,128)S(1)}, u32[]{:S(2)}, u32[]{:S(2)}) collective-permute-start(f32[101,512]{1,0:T(8,128)S(1)} %get-tuple-element.28), channel_id=1, source_target_pairs={{0,6},{1,7},{2,0},{3,1},{4,2},{5,3},{6,4},{7,5},{8,14},{9,15},{10,... | collective-permute-start | bytes 620552 | tf_op jit(solution)/shard_map/ppermute | solution.py:95
  56.7 2.1 %collective-permute-start.25 = (f32[101,512]{1,0:T(8,128)S(1)}, f32[101,512]{1,0:T(8,128)S(1)}, u32[]{:S(2)}, u32[]{:S(2)}) collective-permute-start(f32[101,512]{1,0:T(8,128)S(1)} %get-tuple-element.29), channel_id=1, source_target_pairs={{0,5},{1,6},{2,7},{3,0},{4,1},{5,2},{6,3},{7,4},{8,13},{9,14},{10,... | collective-permute-start | bytes 620552 | tf_op jit(solution)/shard_map/ppermute | solution.py:95
  59.7 10.5 %shard_map.39 = f32[8,101,512]{2,1,0:T(8,128)} custom-call(f32[8,6272]{1,0:T(8,128)} %get-tuple-element.38.refs_0_, bf16[6144,512]{1,0:T(8,128)(2,1)} %bitcast.155), custom_call_target="tpu_custom_call" | custom-call | tf_op jit(solution)/shard_map/pallas_call | solution.py:63
  70.2 2.4 %dynamic-slice_bitcast_fusion.13 = (f32[101,512]{1,0:T(8,128)}, f32[101,512]{1,0:T(8,128)}, f32[101,512]{1,0:T(8,128)}, f32[101,512]{1,0:T(8,128)}, f32[101,512]...) fusion(f32[8,101,512]{2,1,0:T(8,128)} %shard_map.39, s32[]{:T(128)S(6)} %select_n.129, s32[]{:T(128)S(6)} %select_n.141, ...), kind=kLoop, calls=%fused_computation.51 | loop fusion | bytes 2895900 | tf_op jit(solution)/shard_map/jit(dynamic_index_in_dim)/squeeze | solution.py:94
  72.6 2.2 %collective-permute-start.23 = (f32[101,512]{1,0:T(8,128)S(1)}, f32[101,512]{1,0:T(8,128)S(1)}, u32[]{:S(2)}, u32[]{:S(2)}) collective-permute-start(f32[101,512]{1,0:T(8,128)S(1)} %get-tuple-element.31), channel_id=1, source_target_pairs={{0,3},{1,4},{2,5},{3,6},{4,7},{5,0},{6,1},{7,2},{8,11},{9,12},{10,... | collective-permute-start | bytes 620552 | tf_op jit(solution)/shard_map/ppermute | solution.py:95
  75.6 2.6 %collective-permute-start.14 = (f32[101,512]{1,0:T(8,128)}, f32[101,512]{1,0:T(8,128)S(1)}, u32[]{:S(2)}, u32[]{:S(2)}) collective-permute-start(f32[101,512]{1,0:T(8,128)} %get-tuple-element.19), channel_id=1, source_target_pairs={{0,1},{1,2},{2,3},{3,4},{4,5},{5,6},{6,7},{7,0},{8,9},{9,10},{10,1... | collective-permute-start | bytes 620552 | tf_op jit(solution)/shard_map/ppermute | solution.py:95
  79.0 10.4 %shard_map.37 = f32[8,101,512]{2,1,0:T(8,128)} custom-call(f32[8,6272]{1,0:T(8,128)} %get-tuple-element.40.refs_0_, bf16[6144,512]{1,0:T(8,128)(2,1)} %bitcast.156), custom_call_target="tpu_custom_call" | custom-call | tf_op jit(solution)/shard_map/pallas_call | solution.py:63
  89.5 1.8 %collective-permute-start.19 = (f32[101,512]{1,0:T(8,128)}, f32[101,512]{1,0:T(8,128)S(1)}, u32[]{:S(2)}, u32[]{:S(2)}) collective-permute-start(f32[101,512]{1,0:T(8,128)} %get-tuple-element.21), channel_id=1, source_target_pairs={{0,6},{1,7},{2,0},{3,1},{4,2},{5,3},{6,4},{7,5},{8,14},{9,15},{10,... | collective-permute-start | bytes 620552 | tf_op jit(solution)/shard_map/ppermute | solution.py:95
  91.3 2.0 %collective-permute-start.18 = (f32[101,512]{1,0:T(8,128)}, f32[101,512]{1,0:T(8,128)S(1)}, u32[]{:S(2)}, u32[]{:S(2)}) collective-permute-start(f32[101,512]{1,0:T(8,128)} %get-tuple-element.22), channel_id=1, source_target_pairs={{0,5},{1,6},{2,7},{3,0},{4,1},{5,2},{6,3},{7,4},{8,13},{9,14},{10,... | collective-permute-start | bytes 620552 | tf_op jit(solution)/shard_map/ppermute | solution.py:95
  93.3 2.2 %collective-permute-start.17 = (f32[101,512]{1,0:T(8,128)}, f32[101,512]{1,0:T(8,128)}, u32[]{:S(2)}, u32[]{:S(2)}) collective-permute-start(f32[101,512]{1,0:T(8,128)} %get-tuple-element.23), channel_id=1, source_target_pairs={{0,4},{1,5},{2,6},{3,7},{4,0},{5,1},{6,2},{7,3},{8,12},{9,13},{10,... | collective-permute-start | bytes 620552 | tf_op jit(solution)/shard_map/ppermute | solution.py:95
  95.5 1.7 %collective-permute-start.16 = (f32[101,512]{1,0:T(8,128)S(1)}, f32[101,512]{1,0:T(8,128)}, u32[]{:S(2)}, u32[]{:S(2)}) collective-permute-start(f32[101,512]{1,0:T(8,128)S(1)} %get-tuple-element.24), channel_id=1, source_target_pairs={{0,3},{1,4},{2,5},{3,6},{4,7},{5,0},{6,1},{7,2},{8,11},{9,12},{10,... | collective-permute-start | bytes 620552 | tf_op jit(solution)/shard_map/ppermute | solution.py:95
  97.2 2.5 %dynamic-slice_bitcast_fusion.27 = (f32[101,512]{1,0:T(8,128)}, f32[101,512]{1,0:T(8,128)}, f32[101,512]{1,0:T(8,128)}, f32[101,512]{1,0:T(8,128)}, f32[101,512]...) fusion(f32[8,101,512]{2,1,0:T(8,128)} %shard_map.37, s32[]{:T(128)S(6)} %select_n.129, s32[]{:T(128)S(6)} %select_n.141, ...), kind=kLoop, calls=%fused_computation.65 | loop fusion | bytes 2895900 | tf_op jit(solution)/shard_map/jit(dynamic_index_in_dim)/squeeze | solution.py:94
  99.7 10.5 %shard_map.38 = f32[8,101,512]{2,1,0:T(8,128)} custom-call(f32[8,6272]{1,0:T(8,128)} %get-tuple-element.39.refs_0_, bf16[6144,512]{1,0:T(8,128)(2,1)} %bitcast.157), custom_call_target="tpu_custom_call" | custom-call | tf_op jit(solution)/shard_map/pallas_call | solution.py:63
  110.2 1.6 %dynamic-slice_bitcast_fusion.20 = (f32[101,512]{1,0:T(8,128)S(1)}, f32[101,512]{1,0:T(8,128)S(1)}, f32[101,512]{1,0:T(8,128)S(1)}, f32[101,512]{1,0:T(8,128)S(1...) fusion(f32[8,101,512]{2,1,0:T(8,128)} %shard_map.38, s32[]{:T(128)S(6)} %select_n.129, ...), kind=kLoop, calls=%fused_computation.58 | loop fusion | bytes 2895900 | tf_op jit(solution)/shard_map/jit(dynamic_index_in_dim)/squeeze | solution.py:94
  112.0 1.3 collective-permute-start
  114.1 3.1 %collective-permute-start.5 = (f32[101,512]{1,0:T(8,128)S(1)}, f32[101,512]{1,0:T(8,128)S(1)}, u32[]{:S(2)}, u32[]{:S(2)}) collective-permute-start(f32[101,512]{1,0:T(8,128)S(1)} %copy-done.3), channel_id=1, source_target_pairs={{0,6},{1,7},{2,0},{3,1},{4,2},{5,3},{6,4},{7,5},{8,14},{9,15},{10,... | collective-permute-start | bytes 620552 | tf_op jit(solution)/shard_map/ppermute | solution.py:95
  117.2 2.1 %collective-permute-start.4 = (f32[101,512]{1,0:T(8,128)S(1)}, f32[101,512]{1,0:T(8,128)S(1)}, u32[]{:S(2)}, u32[]{:S(2)}) collective-permute-start(f32[101,512]{1,0:T(8,128)S(1)} %copy-done.2), channel_id=1, source_target_pairs={{0,5},{1,6},{2,7},{3,0},{4,1},{5,2},{6,3},{7,4},{8,13},{9,14},{10,... | collective-permute-start | bytes 620552 | tf_op jit(solution)/shard_map/ppermute | solution.py:95
  120.4 5.6 %collective-permute-done.15 = f32[101,512]{1,0:T(8,128)S(1)} collective-permute-done((f32[101,512]{1,0:T(8,128)S(1)}, f32[101,512]{1,0:T(8,128)S(1)}, u32[]{:S(2)}, u32[]{:S(2)}) %collective-permute-start.15) | collective-permute-done | bytes 206880 | tf_op jit(solution)/shard_map/ppermute | solution.py:95
  127.1 3.4 %collective-permute-start.7 = (f32[101,512]{1,0:T(8,128)S(1)}, f32[101,512]{1,0:T(8,128)S(1)}, u32[]{:S(2)}, u32[]{:S(2)}) collective-permute-start(f32[101,512]{1,0:T(8,128)S(1)} %get-tuple-element.12), channel_id=1, source_target_pairs={{0,1},{1,2},{2,3},{3,4},{4,5},{5,6},{6,7},{7,0},{8,9},{9,10},{10,1... | collective-permute-start | bytes 620552 | tf_op jit(solution)/shard_map/ppermute | solution.py:95
  132.3 1.3 fusion.14
  133.6 5.1 %collective-permute-done.3 = f32[101,512]{1,0:T(8,128)S(1)} collective-permute-done((f32[101,512]{1,0:T(8,128)S(1)}, f32[101,512]{1,0:T(8,128)S(1)}, u32[]{:S(2)}, u32[]{:S(2)}) %collective-permute-start.3) | collective-permute-done | bytes 206880 | tf_op jit(solution)/shard_map/ppermute | solution.py:95
  139.3 9.7 %collective-permute-done.1 = f32[101,512]{1,0:T(8,128)S(1)} collective-permute-done((f32[101,512]{1,0:T(8,128)S(1)}, f32[101,512]{1,0:T(8,128)S(1)}, u32[]{:S(2)}, u32[]{:S(2)}) %collective-permute-start.1) | collective-permute-done | bytes 206880 | tf_op jit(solution)/shard_map/ppermute | solution.py:95
  151.1 8.5 %collective-permute-done.10 = f32[101,512]{1,0:T(8,128)S(1)} collective-permute-done((f32[101,512]{1,0:T(8,128)S(1)}, f32[101,512]{1,0:T(8,128)S(1)}, u32[]{:S(2)}, u32[]{:S(2)}) %collective-permute-start.10) | collective-permute-done | bytes 206880 | tf_op jit(solution)/shard_map/ppermute | solution.py:95
  159.6 1.4 collective-permute-done.8
  162.2 1.4 copy.29
  (69 shorter events, 16.2 us)
Async XLA Ops:
  22.4 14.3 %all-to-all-start.1 = ((bf16[16,32,384]{2,1,0:T(8,128)(2,1)}), bf16[16,32,384]{2,1,0:T(8,128)(2,1)S(1)}, u32[]{:S(2)}, u32[]{:S(2)}) async-start(bf16[16,32,384]{2,1,0:T(8,128)(2,1)} %broadcast_in_dim.20), calls=%async_computation.1 | async-start | bytes 786432 | tf_op jit(solution)/shard_map/all_to_all | solution.py:86
  50.5 22.1 %collective-permute-start.21 = (f32[101,512]{1,0:T(8,128)S(1)}, f32[101,512]{1,0:T(8,128)S(1)}, u32[]{:S(2)}, u32[]{:S(2)}) collective-permute-start(f32[101,512]{1,0:T(8,128)S(1)} %get-tuple-element.26), channel_id=1, source_target_pairs={{0,1},{1,2},{2,3},{3,4},{4,5},{5,6},{6,7},{7,0},{8,9},{9,10},{10,1... | collective-permute-start | bytes 620552 | tf_op jit(solution)/shard_map/ppermute | solution.py:95
  53.3 21.5 %collective-permute-start.27 = (f32[101,512]{1,0:T(8,128)S(1)}, f32[101,512]{1,0:T(8,128)S(1)}, u32[]{:S(2)}, u32[]{:S(2)}) collective-permute-start(f32[101,512]{1,0:T(8,128)S(1)} %get-tuple-element.27), channel_id=1, source_target_pairs={{0,7},{1,0},{2,1},{3,2},{4,3},{5,4},{6,5},{7,6},{8,15},{9,8},{10,9... | collective-permute-start | bytes 620552 | tf_op jit(solution)/shard_map/ppermute | solution.py:95
  53.3 22.3 %collective-permute-start.26 = (f32[101,512]{1,0:T(8,128)S(1)}, f32[101,512]{1,0:T(8,128)S(1)}, u32[]{:S(2)}, u32[]{:S(2)}) collective-permute-start(f32[101,512]{1,0:T(8,128)S(1)} %get-tuple-element.28), channel_id=1, source_target_pairs={{0,6},{1,7},{2,0},{3,1},{4,2},{5,3},{6,4},{7,5},{8,14},{9,15},{10,... | collective-permute-start | bytes 620552 | tf_op jit(solution)/shard_map/ppermute | solution.py:95
  56.7 32.8 %collective-permute-start.25 = (f32[101,512]{1,0:T(8,128)S(1)}, f32[101,512]{1,0:T(8,128)S(1)}, u32[]{:S(2)}, u32[]{:S(2)}) collective-permute-start(f32[101,512]{1,0:T(8,128)S(1)} %get-tuple-element.29), channel_id=1, source_target_pairs={{0,5},{1,6},{2,7},{3,0},{4,1},{5,2},{6,3},{7,4},{8,13},{9,14},{10,... | collective-permute-start | bytes 620552 | tf_op jit(solution)/shard_map/ppermute | solution.py:95
  58.7 30.7 %collective-permute-start.24 = (f32[101,512]{1,0:T(8,128)S(1)}, f32[101,512]{1,0:T(8,128)S(1)}, u32[]{:S(2)}, u32[]{:S(2)}) collective-permute-start(f32[101,512]{1,0:T(8,128)S(1)} %get-tuple-element.30), channel_id=1, source_target_pairs={{0,4},{1,5},{2,6},{3,7},{4,0},{5,1},{6,2},{7,3},{8,12},{9,13},{10,... | collective-permute-start | bytes 620552 | tf_op jit(solution)/shard_map/ppermute | solution.py:95
  72.6 18.7 %collective-permute-start.23 = (f32[101,512]{1,0:T(8,128)S(1)}, f32[101,512]{1,0:T(8,128)S(1)}, u32[]{:S(2)}, u32[]{:S(2)}) collective-permute-start(f32[101,512]{1,0:T(8,128)S(1)} %get-tuple-element.31), channel_id=1, source_target_pairs={{0,3},{1,4},{2,5},{3,6},{4,7},{5,0},{6,1},{7,2},{8,11},{9,12},{10,... | collective-permute-start | bytes 620552 | tf_op jit(solution)/shard_map/ppermute | solution.py:95
  74.8 18.5 %collective-permute-start.22 = (f32[101,512]{1,0:T(8,128)S(1)}, f32[101,512]{1,0:T(8,128)S(1)}, u32[]{:S(2)}, u32[]{:S(2)}) collective-permute-start(f32[101,512]{1,0:T(8,128)S(1)} %get-tuple-element.32), channel_id=1, source_target_pairs={{0,2},{1,3},{2,4},{3,5},{4,6},{5,7},{6,0},{7,1},{8,10},{9,11},{10,... | collective-permute-start | bytes 620552 | tf_op jit(solution)/shard_map/ppermute | solution.py:95
  75.6 19.9 %collective-permute-start.14 = (f32[101,512]{1,0:T(8,128)}, f32[101,512]{1,0:T(8,128)S(1)}, u32[]{:S(2)}, u32[]{:S(2)}) collective-permute-start(f32[101,512]{1,0:T(8,128)} %get-tuple-element.19), channel_id=1, source_target_pairs={{0,1},{1,2},{2,3},{3,4},{4,5},{5,6},{6,7},{7,0},{8,9},{9,10},{10,1... | collective-permute-start | bytes 620552 | tf_op jit(solution)/shard_map/ppermute | solution.py:95
  89.5 22.4 %collective-permute-start.20 = (f32[101,512]{1,0:T(8,128)}, f32[101,512]{1,0:T(8,128)S(1)}, u32[]{:S(2)}, u32[]{:S(2)}) collective-permute-start(f32[101,512]{1,0:T(8,128)} %get-tuple-element.20), channel_id=1, source_target_pairs={{0,7},{1,0},{2,1},{3,2},{4,3},{5,4},{6,5},{7,6},{8,15},{9,8},{10,9... | collective-permute-start | bytes 620552 | tf_op jit(solution)/shard_map/ppermute | solution.py:95
  89.5 22.5 %collective-permute-start.19 = (f32[101,512]{1,0:T(8,128)}, f32[101,512]{1,0:T(8,128)S(1)}, u32[]{:S(2)}, u32[]{:S(2)}) collective-permute-start(f32[101,512]{1,0:T(8,128)} %get-tuple-element.21), channel_id=1, source_target_pairs={{0,6},{1,7},{2,0},{3,1},{4,2},{5,3},{6,4},{7,5},{8,14},{9,15},{10,... | collective-permute-start | bytes 620552 | tf_op jit(solution)/shard_map/ppermute | solution.py:95
  91.3 22.1 %collective-permute-start.18 = (f32[101,512]{1,0:T(8,128)}, f32[101,512]{1,0:T(8,128)S(1)}, u32[]{:S(2)}, u32[]{:S(2)}) collective-permute-start(f32[101,512]{1,0:T(8,128)} %get-tuple-element.22), channel_id=1, source_target_pairs={{0,5},{1,6},{2,7},{3,0},{4,1},{5,2},{6,3},{7,4},{8,13},{9,14},{10,... | collective-permute-start | bytes 620552 | tf_op jit(solution)/shard_map/ppermute | solution.py:95
  93.3 20.8 %collective-permute-start.17 = (f32[101,512]{1,0:T(8,128)}, f32[101,512]{1,0:T(8,128)}, u32[]{:S(2)}, u32[]{:S(2)}) collective-permute-start(f32[101,512]{1,0:T(8,128)} %get-tuple-element.23), channel_id=1, source_target_pairs={{0,4},{1,5},{2,6},{3,7},{4,0},{5,1},{6,2},{7,3},{8,12},{9,13},{10,... | collective-permute-start | bytes 620552 | tf_op jit(solution)/shard_map/ppermute | solution.py:95
  95.5 21.7 %collective-permute-start.16 = (f32[101,512]{1,0:T(8,128)S(1)}, f32[101,512]{1,0:T(8,128)}, u32[]{:S(2)}, u32[]{:S(2)}) collective-permute-start(f32[101,512]{1,0:T(8,128)S(1)} %get-tuple-element.24), channel_id=1, source_target_pairs={{0,3},{1,4},{2,5},{3,6},{4,7},{5,0},{6,1},{7,2},{8,11},{9,12},{10,... | collective-permute-start | bytes 620552 | tf_op jit(solution)/shard_map/ppermute | solution.py:95
  110.2 7.0 %copy-start.2 = (f32[101,512]{1,0:T(8,128)S(1)}, f32[101,512]{1,0:T(8,128)}, u32[]{:S(2)}) copy-start(f32[101,512]{1,0:T(8,128)} %get-tuple-element.8) | copy-start | bytes 620548
  111.8 14.2 %copy-start.1 = (f32[101,512]{1,0:T(8,128)S(1)}, f32[101,512]{1,0:T(8,128)}, u32[]{:S(2)}) copy-start(f32[101,512]{1,0:T(8,128)} %get-tuple-element.9) | copy-start | bytes 620548
  111.9 14.2 %copy-start = (f32[101,512]{1,0:T(8,128)S(1)}, f32[101,512]{1,0:T(8,128)}, u32[]{:S(2)}) copy-start(f32[101,512]{1,0:T(8,128)} %get-tuple-element.10) | copy-start | bytes 620548
  111.9 14.2 %collective-permute-start.15 = (f32[101,512]{1,0:T(8,128)S(1)}, f32[101,512]{1,0:T(8,128)S(1)}, u32[]{:S(2)}, u32[]{:S(2)}) collective-permute-start(f32[101,512]{1,0:T(8,128)S(1)} %get-tuple-element.25), channel_id=1, source_target_pairs={{0,2},{1,3},{2,4},{3,5},{4,6},{5,7},{6,0},{7,1},{8,10},{9,11},{10,... | collective-permute-start | bytes 620552 | tf_op jit(solution)/shard_map/ppermute | solution.py:95
  112.0 14.1 %collective-permute-start = (f32[101,512]{1,0:T(8,128)S(1)}, f32[101,512]{1,0:T(8,128)S(1)}, u32[]{:S(2)}, u32[]{:S(2)}) collective-permute-start(f32[101,512]{1,0:T(8,128)S(1)} %copy-done.5), channel_id=1, source_target_pairs={{0,1},{1,2},{2,3},{3,4},{4,5},{5,6},{6,7},{7,0},{8,9},{9,10},{10,1... | collective-permute-start | bytes 620552 | tf_op jit(solution)/shard_map/ppermute | solution.py:95
  113.3 12.8 %collective-permute-start.6 = (f32[101,512]{1,0:T(8,128)S(1)}, f32[101,512]{1,0:T(8,128)S(1)}, u32[]{:S(2)}, u32[]{:S(2)}) collective-permute-start(f32[101,512]{1,0:T(8,128)S(1)} %copy-done.4), channel_id=1, source_target_pairs={{0,7},{1,0},{2,1},{3,2},{4,3},{5,4},{6,5},{7,6},{8,15},{9,8},{10,9... | collective-permute-start | bytes 620552 | tf_op jit(solution)/shard_map/ppermute | solution.py:95
  114.1 13.0 %collective-permute-start.5 = (f32[101,512]{1,0:T(8,128)S(1)}, f32[101,512]{1,0:T(8,128)S(1)}, u32[]{:S(2)}, u32[]{:S(2)}) collective-permute-start(f32[101,512]{1,0:T(8,128)S(1)} %copy-done.3), channel_id=1, source_target_pairs={{0,6},{1,7},{2,0},{3,1},{4,2},{5,3},{6,4},{7,5},{8,14},{9,15},{10,... | collective-permute-start | bytes 620552 | tf_op jit(solution)/shard_map/ppermute | solution.py:95
  117.2 14.5 %collective-permute-start.4 = (f32[101,512]{1,0:T(8,128)S(1)}, f32[101,512]{1,0:T(8,128)S(1)}, u32[]{:S(2)}, u32[]{:S(2)}) collective-permute-start(f32[101,512]{1,0:T(8,128)S(1)} %copy-done.2), channel_id=1, source_target_pairs={{0,5},{1,6},{2,7},{3,0},{4,1},{5,2},{6,3},{7,4},{8,13},{9,14},{10,... | collective-permute-start | bytes 620552 | tf_op jit(solution)/shard_map/ppermute | solution.py:95
  126.0 12.6 %collective-permute-start.3 = (f32[101,512]{1,0:T(8,128)S(1)}, f32[101,512]{1,0:T(8,128)S(1)}, u32[]{:S(2)}, u32[]{:S(2)}) collective-permute-start(f32[101,512]{1,0:T(8,128)S(1)} %copy-done.1), channel_id=1, source_target_pairs={{0,4},{1,5},{2,6},{3,7},{4,0},{5,1},{6,2},{7,3},{8,12},{9,13},{10,... | collective-permute-start | bytes 620552 | tf_op jit(solution)/shard_map/ppermute | solution.py:95
  126.1 13.0 %collective-permute-start.2 = (f32[101,512]{1,0:T(8,128)S(1)}, f32[101,512]{1,0:T(8,128)S(1)}, u32[]{:S(2)}, u32[]{:S(2)}) collective-permute-start(f32[101,512]{1,0:T(8,128)S(1)} %copy-done), channel_id=1, source_target_pairs={{0,3},{1,4},{2,5},{3,6},{4,7},{5,0},{6,1},{7,2},{8,11},{9,12},{10,... | collective-permute-start | bytes 620552 | tf_op jit(solution)/shard_map/ppermute | solution.py:95
  126.2 22.8 %collective-permute-start.1 = (f32[101,512]{1,0:T(8,128)S(1)}, f32[101,512]{1,0:T(8,128)S(1)}, u32[]{:S(2)}, u32[]{:S(2)}) collective-permute-start(f32[101,512]{1,0:T(8,128)S(1)} %get-tuple-element.11), channel_id=1, source_target_pairs={{0,2},{1,3},{2,4},{3,5},{4,6},{5,7},{6,0},{7,1},{8,10},{9,11},{10,... | collective-permute-start | bytes 620552 | tf_op jit(solution)/shard_map/ppermute | solution.py:95
  127.1 22.3 %collective-permute-start.7 = (f32[101,512]{1,0:T(8,128)S(1)}, f32[101,512]{1,0:T(8,128)S(1)}, u32[]{:S(2)}, u32[]{:S(2)}) collective-permute-start(f32[101,512]{1,0:T(8,128)S(1)} %get-tuple-element.12), channel_id=1, source_target_pairs={{0,1},{1,2},{2,3},{3,4},{4,5},{5,6},{6,7},{7,0},{8,9},{9,10},{10,1... | collective-permute-start | bytes 620552 | tf_op jit(solution)/shard_map/ppermute | solution.py:95
  131.7 17.7 %collective-permute-start.13 = (f32[101,512]{1,0:T(8,128)S(1)}, f32[101,512]{1,0:T(8,128)S(1)}, u32[]{:S(2)}, u32[]{:S(2)}) collective-permute-start(f32[101,512]{1,0:T(8,128)S(1)} %get-tuple-element.13), channel_id=1, source_target_pairs={{0,7},{1,0},{2,1},{3,2},{4,3},{5,4},{6,5},{7,6},{8,15},{9,8},{10,9... | collective-permute-start | bytes 620552 | tf_op jit(solution)/shard_map/ppermute | solution.py:95
  138.7 12.4 %collective-permute-start.12 = (f32[101,512]{1,0:T(8,128)S(1)}, f32[101,512]{1,0:T(8,128)S(1)}, u32[]{:S(2)}, u32[]{:S(2)}) collective-permute-start(f32[101,512]{1,0:T(8,128)S(1)} %get-tuple-element.14), channel_id=1, source_target_pairs={{0,6},{1,7},{2,0},{3,1},{4,2},{5,3},{6,4},{7,5},{8,14},{9,15},{10,... | collective-permute-start | bytes 620552 | tf_op jit(solution)/shard_map/ppermute | solution.py:95
  139.0 12.1 %collective-permute-start.11 = (f32[101,512]{1,0:T(8,128)S(1)}, f32[101,512]{1,0:T(8,128)S(1)}, u32[]{:S(2)}, u32[]{:S(2)}) collective-permute-start(f32[101,512]{1,0:T(8,128)S(1)} %get-tuple-element.15), channel_id=1, source_target_pairs={{0,5},{1,6},{2,7},{3,0},{4,1},{5,2},{6,3},{7,4},{8,13},{9,14},{10,... | collective-permute-start | bytes 620552 | tf_op jit(solution)/shard_map/ppermute | solution.py:95
  149.0 10.7 %collective-permute-start.10 = (f32[101,512]{1,0:T(8,128)S(1)}, f32[101,512]{1,0:T(8,128)S(1)}, u32[]{:S(2)}, u32[]{:S(2)}) collective-permute-start(f32[101,512]{1,0:T(8,128)S(1)} %get-tuple-element.16), channel_id=1, source_target_pairs={{0,4},{1,5},{2,6},{3,7},{4,0},{5,1},{6,2},{7,3},{8,12},{9,13},{10,... | collective-permute-start | bytes 620552 | tf_op jit(solution)/shard_map/ppermute | solution.py:95
  149.4 10.2 %collective-permute-start.9 = (f32[101,512]{1,0:T(8,128)S(1)}, f32[101,512]{1,0:T(8,128)S(1)}, u32[]{:S(2)}, u32[]{:S(2)}) collective-permute-start(f32[101,512]{1,0:T(8,128)S(1)} %get-tuple-element.17), channel_id=1, source_target_pairs={{0,3},{1,4},{2,5},{3,6},{4,7},{5,0},{6,1},{7,2},{8,11},{9,12},{10,... | collective-permute-start | bytes 620552 | tf_op jit(solution)/shard_map/ppermute | solution.py:95
  149.4 11.7 %collective-permute-start.8 = (f32[101,512]{1,0:T(8,128)S(1)}, f32[101,512]{1,0:T(8,128)S(1)}, u32[]{:S(2)}, u32[]{:S(2)}) collective-permute-start(f32[101,512]{1,0:T(8,128)S(1)} %get-tuple-element.18), channel_id=1, source_target_pairs={{0,2},{1,3},{2,4},{3,5},{4,6},{5,7},{6,0},{7,1},{8,10},{9,11},{10,... | collective-permute-start | bytes 620552 | tf_op jit(solution)/shard_map/ppermute | solution.py:95
  (3 other events, 8.8 us)

commit v7 on v5

--- a/solution.py
+++ b/solution.py
@@ -94,11 +94,10 @@
     first_row = lax.axis_index("rcv") * ch_dev
     norm_scale = 1.0 / math.sqrt(SAMPLES * traces.shape[1] * win_count)
     record = traces[:, 0, :]
-    channel_ids = jnp.arange(ch_dev, dtype=jnp.int32)
-    select = (sources.reshape(-1)[:, None] - first_row == channel_ids[None, :]).astype(
-        traces.dtype
-    )
-    picked = jnp.dot(select, record, preferred_element_type=jnp.float32).astype(jnp.bfloat16)
+    local = sources.reshape(-1) - first_row
+    owned = (local >= 0) & (local < ch_dev)
+    rows = jnp.take(record, jnp.clip(local, 0, ch_dev - 1), axis=0)
+    picked = jnp.where(owned[:, None], rows, jnp.zeros_like(rows))
     source_rows = gather_sources(picked)
     start_at = offsets[0]
     positions = jnp.arange(span, dtype=jnp.int32)
@@ -108,11 +107,14 @@
     per_group = mq.shape[0] // win_count
     by_group = mq.reshape(win_count, per_group, mq.shape[1])
     rt = record.T
+    bounds = [0, 1, 2, per_group] if per_group == 4 else list(range(per_group + 1))
     outs = []
-    for i in range(per_group):
-        part = correlate(by_group[:, i, :], rt, norm_scale)
+    for lo, hi in zip(bounds[:-1], bounds[1:]):
+        chunk = by_group[:, lo:hi, :].reshape(win_count * (hi - lo), mq.shape[1])
+        part = correlate(chunk, rt, norm_scale)
+        part = part.reshape((win_count, hi - lo) + part.shape[1:])
         outs.append(lax.all_to_all(part, "win", 0, 0).sum(axis=0))
-    return jnp.stack(outs, axis=0)
+    return jnp.concatenate(outs, axis=0)
 
 
 def solution(mesh):

time: 159 us -> 168 us (1.057)
  local copies, waits for them, and re-layouts: 17.3 us -> 38.8 us
  waiting for transfers between devices: 45.8 us -> 38.9 us
  other arithmetic: 5.35 us -> 10.9 us
  starting transfers between devices: 25.8 us -> 20.7 us
  matrix products: 3.98 us -> 0 us
  Pallas kernels: 41.7 us -> 38.9 us
    reshape x1 -> x5, local copies, waits for them, and re-layouts: 0.04 us -> 17.7 us  [the longest x3 14.9 us: shards(): part = part.reshape((win_count, hi - lo) + part.shape[1:])]
    all_to_all x4 -> x3, waiting for transfers between devices: 44.5 us -> 37.6 us  [shards(): outs.append(lax.all_to_all(part, 'win', 0, 0).sum(axis=0))]
    all_to_all x4 -> x3, starting transfers between devices: 22.2 us -> 17.2 us  [shards(): outs.append(lax.all_to_all(part, 'win', 0, 0).sum(axis=0))]
    gather x0 -> x1, local copies, waits for them, and re-layouts: none -> 4.75 us  [shards(): rows = jnp.take(record, jnp.clip(local, 0, ch_dev - 1), axis=0)]
    dot_general x1 -> x0, matrix products: 3.98 us -> none  [shards(): jnp.dot(select, record, preferred_element_type=jnp.float32)]
    reduce_sum x4 -> x3, other arithmetic: 4.32 us -> 8.14 us  [shards(): outs.append(lax.all_to_all(part, 'win', 0, 0).sum(axis=0))]
    pallas_call x4 -> x3, Pallas kernels: 41.7 us -> 38.9 us  [correlate(): pl.pallas_call(kernel, grid=(span // width,), in_specs=[pl.BlockSpec(mq.s...]
    unnamed x7 -> x8, local copies, waits for them, and re-layouts: 13.3 us -> 10.9 us
  transfers between devices with their start and end apart: 5 -> 4, of which waited for: 5 -> 3; matrix products, arithmetic and copies ran while one was open for 10% -> 18% of each run, Pallas kernels for 20% -> 17%
where the time goes in v7:
time: 168 us; the launch traced here: 166 us
  waiting for transfers between devices  38.9 us (23%)
  Pallas kernels  38.9 us (23%)
  local copies, waits for them, and re-layouts  38.8 us (23%)
  starting transfers between devices  20.7 us (12%)
  blocking collectives  16.7 us (10%)
  other arithmetic  10.9 us (6%)
    pallas_call x3, Pallas kernels, correlate(): pl.pallas_call(kernel, grid=(span // width,), in_specs=[pl.BlockSpec(mq.s...  38.9 us
    all_to_all x3, waiting for transfers between devices, shards(): outs.append(lax.all_to_all(part, 'win', 0, 0).sum(axis=0))  37.6 us
    all_to_all x3, starting transfers between devices, shards(): outs.append(lax.all_to_all(part, 'win', 0, 0).sum(axis=0))  17.2 us
    all_to_all x1, blocking collectives, gather_sources(): own = lax.all_to_all(pieces, 'rcv', 0, 0).sum(axis=0, dtype=jnp.float32)  16.7 us
    reshape x3, local copies, waits for them, and re-layouts, shards(): part = part.reshape((win_count, hi - lo) + part.shape[1:])  14.9 us
    unnamed x8, local copies, waits for them, and re-layouts  10.9 us
    reduce_sum x3, other arithmetic, shards(): outs.append(lax.all_to_all(part, 'win', 0, 0).sum(axis=0))  8.14 us
    gather x1, local copies, waits for them, and re-layouts, shards(): rows = jnp.take(record, jnp.clip(local, 0, ch_dev - 1), axis=0)  4.75 us
  transfers between devices with their start and end apart: 4, of which 3 were waited for; matrix products, arithmetic and copies ran while one was open for 18% of the time, Pallas kernels for 17%

profile of v7, /device:TPU:8, one launch (start us, length us, event | category | flops | bytes accessed | tf_op | source)
XLA Modules:
  0.0 165.7 jit_solution(4901630529515748194)
XLA Ops:
  0.0 0.7 subtract_clamp_fusion
  0.9 0.7 compare_and_fusion.1
  1.8 4.8 %gather_fusion = bf16[32,6144]{1,0:T(8,128)(2,1)S(1)} fusion(bf16[512,6144]{1,0:T(8,128)(2,1)} %bitcast.32, s32[1024]{0:T(1024)S(1)} %pad_clamp_fusion), kind=kCustom, calls=%fused_computation | custom fusion | bytes 786560 | tf_op jit(solution)/shard_map/jit(_take)/gather | solution.py:99
  6.7 16.7 %all_to_all.25 = bf16[16,32,384]{2,1,0:T(8,128)(2,1)S(1)} all-to-all(bf16[16,32,384]{2,1,0:T(8,128)(2,1)S(1)} %fusion.1), channel_id=1, replica_groups=mesh['rcv'=16,'win'=8] {'rcv'}, dimensions={0} | all-to-all | bytes 786432 | tf_op jit(solution)/shard_map/all_to_all | solution.py:84
  23.4 0.8 broadcast_in_dim.38
  24.2 3.6 %all-to-all-start.1 = ((bf16[16,32,384]{2,1,0:T(8,128)(2,1)}), bf16[16,32,384]{2,1,0:T(8,128)(2,1)S(1)}, u32[]{:S(2)}, u32[]{:S(2)}) async-start(bf16[16,32,384]{2,1,0:T(8,128)(2,1)} %broadcast_in_dim.38), calls=%async_computation.1 | async-start | bytes 786432 | tf_op jit(solution)/shard_map/all_to_all | solution.py:86
  27.8 8.7 %copy.34 = bf16[512,1,6144]{0,2,1:T(8,128)(2,1)} copy(bf16[512,1,6144]{2,0,1:T(8,128)(2,1)} %param.3) | data formatting | bytes 12582912 | tf_op args[0]
  37.1 1.4 all-to-all-done.1
  38.6 0.2 pad_convert_fusion
  38.8 0.2 reshape.112
  39.0 0.3 fusion.4
  39.3 0.8 copy_bitcast_fusion
  40.1 10.4 %shard_map.37 = f32[8,101,512]{2,1,0:T(8,128)} custom-call(f32[8,6272]{1,0:T(8,128)} %get-tuple-element.8.refs_0_, bf16[6144,512]{1,0:T(8,128)(2,1)} %bitcast.29), custom_call_target="tpu_custom_call" | custom-call | tf_op jit(solution)/shard_map/pallas_call | solution.py:63
  50.5 4.4 %copy.40 = f32[8,1,101,512]{3,1,2,0:T(1,128)} copy(f32[8,1,101,512]{3,2,0,1:T(8,128)} %bitcast.34) | data formatting | bytes 3309568 | tf_op jit(solution)/shard_map/reshape | solution.py:115
  55.0 6.8 %all-to-all-start.2 = ((f32[8,1,101,512]{3,1,2,0:T(1,128)}), f32[8,1,101,512]{3,1,2,0:T(1,128)S(1)}, u32[]{:S(2)}, u32[]{:S(2)}) async-start(f32[8,1,101,512]{3,1,2,0:T(1,128)} %copy.40), calls=%async_computation.2 | async-start | bytes 3309568 | tf_op jit(solution)/shard_map/all_to_all | solution.py:116
  61.7 10.4 %shard_map.38 = f32[8,101,512]{2,1,0:T(8,128)} custom-call(f32[8,6272]{1,0:T(8,128)} %get-tuple-element.7.refs_0_, bf16[6144,512]{1,0:T(8,128)(2,1)} %bitcast.30), custom_call_target="tpu_custom_call" | custom-call | tf_op jit(solution)/shard_map/pallas_call | solution.py:63
  72.1 4.3 %copy.42 = f32[8,1,101,512]{3,1,2,0:T(1,128)} copy(f32[8,1,101,512]{3,2,0,1:T(8,128)} %bitcast.35) | data formatting | bytes 3309568 | tf_op jit(solution)/shard_map/reshape | solution.py:115
  76.5 5.9 %all-to-all-done.2 = f32[8,1,101,512]{3,1,2,0:T(1,128)S(1)} async-done(((f32[8,1,101,512]{3,1,2,0:T(1,128)}), f32[8,1,101,512]{3,1,2,0:T(1,128)S(1)}, u32[]{:S(2)}, u32[]{:S(2)}) %all-to-all-start.2) | async-done | bytes 1654816 | tf_op jit(solution)/shard_map/all_to_all | solution.py:116
  82.4 4.7 %all-to-all-start.3 = ((f32[8,1,101,512]{3,1,2,0:T(1,128)}), f32[8,1,101,512]{3,1,2,0:T(1,128)S(1)}, u32[]{:S(2)}, u32[]{:S(2)}) async-start(f32[8,1,101,512]{3,1,2,0:T(1,128)} %copy.42), calls=%async_computation.3 | async-start | bytes 3309568 | tf_op jit(solution)/shard_map/all_to_all | solution.py:116
  87.1 2.1 %slice.16 = f32[8,2,6272]{2,1,0:T(2,128)} slice(f32[8,4,6272]{2,1,0:T(4,128)} %copy-done.2), slice={[0:8], [2:4], [0:6272]} | slice | bytes 802816 | tf_op jit(solution)/shard_map/slice | solution.py:113
  89.2 2.0 %reshape.109.refs_0_ = f32[16,6272]{1,0:T(8,128)} reshape(f32[8,2,6272]{2,1,0:T(2,128)} %slice.16) | data formatting | bytes 802816 | tf_op jit(solution)/shard_map/reshape | solution.py:113
  91.2 18.1 %shard_map.39 = f32[16,101,512]{2,1,0:T(8,128)} custom-call(f32[16,6272]{1,0:T(8,128)} %reshape.109.refs_0_, bf16[6144,512]{1,0:T(8,128)(2,1)} %bitcast.31), custom_call_target="tpu_custom_call" | custom-call | tf_op jit(solution)/shard_map/pallas_call | solution.py:63
  109.3 6.2 %copy.43 = f32[8,2,101,512]{3,1,2,0:T(2,128)} copy(f32[8,2,101,512]{3,2,1,0:T(8,128)} %bitcast.33) | data formatting | bytes 6619136 | tf_op jit(solution)/shard_map/reshape | solution.py:115
  115.5 1.2 copy-done.1
  116.7 5.7 %all-to-all-start.4 = ((f32[8,2,101,512]{3,1,2,0:T(2,128)}), f32[8,2,101,512]{3,1,2,0:T(2,128)S(1)}, u32[]{:S(2)}, u32[]{:S(2)}) async-start(f32[8,2,101,512]{3,1,2,0:T(2,128)} %copy.43), calls=%async_computation.4 | async-start | bytes 6619136 | tf_op jit(solution)/shard_map/all_to_all | solution.py:116
  122.5 2.6 %reduce_sum.44 = f32[101,512]{1,0:T(8,128)S(1)} reduce(f32[8,1,101,512]{3,1,2,0:T(1,128)} %copy-done, f32[]{:T(128)} %constant.40.clone.1), dimensions={0,1}, to_apply=%region_1.2 | reduce | flops 361984 | bytes 1861636 | tf_op jit(solution)/shard_map/reduce_sum | solution.py:116
  125.1 3.3 %reduce_sum.46 = f32[101,512]{1,0:T(8,128)} reduce(f32[8,1,101,512]{3,1,2,0:T(1,128)} %copy-done.1, f32[]{:T(128)} %constant.40.clone.1), dimensions={0,1}, to_apply=%region_2.3 | reduce | flops 361984 | bytes 1861636 | tf_op jit(solution)/shard_map/reduce_sum | solution.py:116
  128.4 31.6 %all-to-all-done.4 = f32[8,2,101,512]{3,1,2,0:T(2,128)S(1)} async-done(((f32[8,2,101,512]{3,1,2,0:T(2,128)}), f32[8,2,101,512]{3,1,2,0:T(2,128)S(1)}, u32[]{:S(2)}, u32[]{:S(2)}) %all-to-all-start.4) | async-done | bytes 3309600 | tf_op jit(solution)/shard_map/all_to_all | solution.py:116
  160.0 2.2 %reduce_sum.48 = f32[2,101,512]{2,0,1:T(2,128)} reduce(f32[8,2,101,512]{3,1,2,0:T(2,128)S(1)} %all-to-all-done.4, f32[]{:T(128)} %constant.40.clone.1), dimensions={0}, to_apply=%region_3.4 | reduce | flops 723968 | bytes 3723268 | tf_op jit(solution)/shard_map/reduce_sum | solution.py:116
  162.2 1.1 copy.47
  163.3 1.0 pad_maximum_fusion
  164.3 1.4 copy.45
  (19 shorter events, 0.8 us)
Async XLA Ops:
  24.2 14.3 %all-to-all-start.1 = ((bf16[16,32,384]{2,1,0:T(8,128)(2,1)}), bf16[16,32,384]{2,1,0:T(8,128)(2,1)S(1)}, u32[]{:S(2)}, u32[]{:S(2)}) async-start(bf16[16,32,384]{2,1,0:T(8,128)(2,1)} %broadcast_in_dim.38), calls=%async_computation.1 | async-start | bytes 786432 | tf_op jit(solution)/shard_map/all_to_all | solution.py:86
  39.0 11.5 %copy-start.2 = (f32[8,4,6272]{2,1,0:T(4,128)}, f32[8,4,6272]{2,1,0:T(4,128)S(1)}, u32[]{:S(2)}) copy-start(f32[8,4,6272]{2,1,0:T(4,128)S(1)} %reshape.112) | copy-start | bytes 2408452
  55.0 27.4 %all-to-all-start.2 = ((f32[8,1,101,512]{3,1,2,0:T(1,128)}), f32[8,1,101,512]{3,1,2,0:T(1,128)S(1)}, u32[]{:S(2)}, u32[]{:S(2)}) async-start(f32[8,1,101,512]{3,1,2,0:T(1,128)} %copy.40), calls=%async_computation.2 | async-start | bytes 3309568 | tf_op jit(solution)/shard_map/all_to_all | solution.py:116
  82.4 27.0 %copy-start = (f32[8,1,101,512]{3,1,2,0:T(1,128)}, f32[8,1,101,512]{3,1,2,0:T(1,128)S(1)}, u32[]{:S(2)}) copy-start(f32[8,1,101,512]{3,1,2,0:T(1,128)S(1)} %all-to-all-done.2) | copy-start | bytes 4964356
  82.4 33.1 %all-to-all-start.3 = ((f32[8,1,101,512]{3,1,2,0:T(1,128)}), f32[8,1,101,512]{3,1,2,0:T(1,128)S(1)}, u32[]{:S(2)}, u32[]{:S(2)}) async-start(f32[8,1,101,512]{3,1,2,0:T(1,128)} %copy.42), calls=%async_computation.3 | async-start | bytes 3309568 | tf_op jit(solution)/shard_map/all_to_all | solution.py:116
  115.5 1.2 copy-start.1
  116.7 43.3 %all-to-all-start.4 = ((f32[8,2,101,512]{3,1,2,0:T(2,128)}), f32[8,2,101,512]{3,1,2,0:T(2,128)S(1)}, u32[]{:S(2)}, u32[]{:S(2)}) async-start(f32[8,2,101,512]{3,1,2,0:T(2,128)} %copy.43), calls=%async_computation.4 | async-start | bytes 6619136 | tf_op jit(solution)/shard_map/all_to_all | solution.py:116

commit v8 on v5

--- a/solution.py
+++ b/solution.py
@@ -14,6 +14,8 @@
 LANE = 128
 FRONT = ROWS - HALF
 CHUNK = 2048
+KEPT = 104
+PARTS = 2
 
 
 def corr_kernel(mq_ref, rt_ref, out_ref, acc_ref, lag_ref, *, scale, pairs, width):
@@ -49,12 +51,14 @@
 
     @pl.when(q == pl.num_programs(0) - 1)
     def _():
+        per = 2 * pairs // out_ref.shape[0]
         for k in range(2 * pairs):
             half = (k % 2) * ROWS
-            out_ref[k] = acc_ref[k // 2, half : half + LAGS, :] * scale
+            at = (k % per) * KEPT
+            out_ref[k // per, at : at + KEPT, :] = acc_ref[k // 2, half : half + KEPT, :] * scale
 
 
-def correlate(mq, rt, scale):
+def correlate(mq, rt, scale, groups):
     n_src = mq.shape[0]
     span, ch = rt.shape
     pairs = n_src // 2
@@ -67,8 +71,8 @@
             pl.BlockSpec(mq.shape, lambda q: (0, 0)),
             pl.BlockSpec((width, ch), lambda q: (q, 0)),
         ],
-        out_specs=pl.BlockSpec((n_src, LAGS, ch), lambda q: (0, 0, 0)),
-        out_shape=jax.ShapeDtypeStruct((n_src, LAGS, ch), jnp.float32),
+        out_specs=pl.BlockSpec((groups, n_src // groups * KEPT, ch), lambda q: (0, 0, 0)),
+        out_shape=jax.ShapeDtypeStruct((groups, n_src // groups * KEPT, ch), jnp.float32),
         scratch_shapes=[
             pltpu.VMEM((pairs, 2 * ROWS, ch), jnp.float32),
             pltpu.VMEM((2, 2 * ROWS, width), jnp.bfloat16),
@@ -108,11 +112,15 @@
     per_group = mq.shape[0] // win_count
     by_group = mq.reshape(win_count, per_group, mq.shape[1])
     rt = record.T
+    parts = PARTS if per_group % PARTS == 0 else per_group
+    per = per_group // parts
     outs = []
-    for i in range(per_group):
-        part = correlate(by_group[:, i, :], rt, norm_scale)
-        outs.append(lax.all_to_all(part, "win", 0, 0).sum(axis=0))
-    return jnp.stack(outs, axis=0)
+    for i in range(parts):
+        chunk = by_group[:, i * per : (i + 1) * per, :].reshape(win_count * per, mq.shape[1])
+        part = correlate(chunk, rt, norm_scale, win_count)
+        summed = lax.all_to_all(part, "win", 0, 0).sum(axis=0)
+        outs.append(summed.reshape(per, KEPT, summed.shape[-1])[:, :LAGS, :])
+    return jnp.concatenate(outs, axis=0)
 
 
 def solution(mesh):

time: 159 us -> 155 us (0.975)
  waiting for transfers between devices: 45.8 us -> 58.1 us
  starting transfers between devices: 25.8 us -> 15.9 us
  Pallas kernels: 41.7 us -> 36.2 us
  local copies, waits for them, and re-layouts: 17.3 us -> 15.5 us
    all_to_all x4 -> x2, waiting for transfers between devices: 44.5 us -> 56.8 us  [shards(): summed = lax.all_to_all(part, 'win', 0, 0).sum(axis=0)]
    all_to_all x4 -> x2, starting transfers between devices: 22.2 us -> 12.3 us  [shards(): summed = lax.all_to_all(part, 'win', 0, 0).sum(axis=0)]
    pallas_call x4 -> x2, Pallas kernels: 41.7 us -> 36.2 us  [correlate(): pl.pallas_call(kernel, grid=(span // width,), in_specs=[pl.BlockSpec(mq.s...]
    unnamed x7 -> x1, local copies, waits for them, and re-layouts: 13.3 us -> 8.69 us
    reshape x0 -> x2, local copies, waits for them, and re-layouts: none -> 3.1 us  [shards(): by_group[:, i * per:(i + 1) * per, :].reshape(win_count * per, mq.shape[1])]
    reduce_sum x4 -> x2, other arithmetic: 4.32 us -> 3.5 us  [shards(): summed = lax.all_to_all(part, 'win', 0, 0).sum(axis=0)]
  transfers between devices with their start and end apart: 5 -> 3, of which waited for: 5 -> 3; matrix products, arithmetic and copies ran while one was open for 10% -> 8% of each run, Pallas kernels for 20% -> 12%
where the time goes in v8:
time: 155 us; the launch traced here: 153 us
  waiting for transfers between devices  58.1 us (37%)
  Pallas kernels  36.2 us (23%)
  blocking collectives  16.7 us (11%)
  starting transfers between devices  15.9 us (10%)
  local copies, waits for them, and re-layouts  15.5 us (10%)
  other arithmetic  5.55 us (4%)
  matrix products  3.98 us (3%)
    all_to_all x2, waiting for transfers between devices, shards(): summed = lax.all_to_all(part, 'win', 0, 0).sum(axis=0)  56.8 us
    pallas_call x2, Pallas kernels, correlate(): pl.pallas_call(kernel, grid=(span // width,), in_specs=[pl.BlockSpec(mq.s...  36.2 us
    all_to_all x1, blocking collectives, gather_sources(): own = lax.all_to_all(pieces, 'rcv', 0, 0).sum(axis=0, dtype=jnp.float32)  16.7 us
    all_to_all x2, starting transfers between devices, shards(): summed = lax.all_to_all(part, 'win', 0, 0).sum(axis=0)  12.3 us
    unnamed x1, local copies, waits for them, and re-layouts  8.69 us
    dot_general x1, matrix products, shards(): jnp.dot(select, record, preferred_element_type=jnp.float32)  3.98 us
    all_to_all x1, starting transfers between devices, gather_sources(): every = lax.all_to_all(spread, 'rcv', 0, 0)  3.55 us
    reduce_sum x2, other arithmetic, shards(): summed = lax.all_to_all(part, 'win', 0, 0).sum(axis=0)  3.5 us
  transfers between devices with their start and end apart: 3, of which 3 were waited for; matrix products, arithmetic and copies ran while one was open for 8% of the time, Pallas kernels for 12%

profile of v8, /device:TPU:8, one launch (start us, length us, event | category | flops | bytes accessed | tf_op | source)
XLA Modules:
  0.0 152.7 jit_solution(3865833060954769742)
XLA Ops:
  0.0 0.7 broadcast_subtract_fusion
  0.7 0.1 copy.13
  0.8 0.1 sub.16
  0.9 4.0 %convolution_convert_fusion = bf16[32,6144]{1,0:T(8,128)(2,1)S(1)} fusion(bf16[512,1,6144]{2,0,1:T(8,128)(2,1)} %param.3, s32[32]{0:T(128)S(1)} %sub.16), kind=kOutput, calls=%fused_computation | convolution fusion | flops 201539584 | bytes 6684800 | tf_op jit(solution)/shard_map/dot_general | solution.py:105
  4.9 16.7 %all_to_all.20 = bf16[16,32,384]{2,1,0:T(8,128)(2,1)S(1)} all-to-all(bf16[16,32,384]{2,1,0:T(8,128)(2,1)S(1)} %bitcast.28), channel_id=1, replica_groups=mesh['rcv'=16,'win'=8] {'rcv'}, dimensions={0} | all-to-all | bytes 786432 | tf_op jit(solution)/shard_map/all_to_all | solution.py:88
  21.5 0.1 reduce_sum.30
  21.6 0.8 broadcast_in_dim.20
  22.4 3.6 %all-to-all-start.1 = ((bf16[16,32,384]{2,1,0:T(8,128)(2,1)}), bf16[16,32,384]{2,1,0:T(8,128)(2,1)S(1)}, u32[]{:S(2)}, u32[]{:S(2)}) async-start(bf16[16,32,384]{2,1,0:T(8,128)(2,1)} %broadcast_in_dim.20), calls=%async_computation.1 | async-start | bytes 786432 | tf_op jit(solution)/shard_map/all_to_all | solution.py:90
  25.9 8.7 %copy.14 = bf16[512,1,6144]{0,2,1:T(8,128)(2,1)} copy(bf16[512,1,6144]{2,0,1:T(8,128)(2,1)} %param.3) | data formatting | bytes 12582912 | tf_op args[0]
  35.3 1.3 all-to-all-done.1
  36.7 0.2 pad_convert_fusion
  36.9 0.2 reshape.54
  37.2 1.1 fusion.3
  38.2 1.0 reshape.49.refs_0_
  39.2 18.1 %shard_map.37 = f32[8,208,512]{2,1,0:T(8,128)} custom-call(f32[16,6272]{1,0:T(8,128)} %reshape.49.refs_0_, bf16[6144,512]{1,0:T(8,128)(2,1)} %bitcast.22), custom_call_target="tpu_custom_call" | custom-call | tf_op jit(solution)/shard_map/pallas_call | solution.py:67
  57.3 6.8 %all-to-all-start.2 = ((f32[8,208,512]{2,1,0:T(8,128)}), f32[8,208,512]{2,1,0:T(8,128)S(1)}, u32[]{:S(2)}, u32[]{:S(2)}) async-start(f32[8,208,512]{2,1,0:T(8,128)} %shard_map.37), calls=%async_computation.2 | async-start | bytes 6815744 | tf_op jit(solution)/shard_map/all_to_all | solution.py:121
  64.1 2.1 %reshape.51.refs_0_ = f32[16,6272]{1,0:T(8,128)} reshape(f32[8,2,6272]{2,1,0:T(2,128)} %get-tuple-element.6) | data formatting | bytes 802816 | tf_op jit(solution)/shard_map/reshape | solution.py:119
  66.2 18.1 %shard_map.38 = f32[8,208,512]{2,1,0:T(8,128)} custom-call(f32[16,6272]{1,0:T(8,128)} %reshape.51.refs_0_, bf16[6144,512]{1,0:T(8,128)(2,1)} %bitcast.23), custom_call_target="tpu_custom_call" | custom-call | tf_op jit(solution)/shard_map/pallas_call | solution.py:67
  84.3 19.3 %all-to-all-done.2 = f32[8,208,512]{2,1,0:T(8,128)S(1)} async-done(((f32[8,208,512]{2,1,0:T(8,128)}), f32[8,208,512]{2,1,0:T(8,128)S(1)}, u32[]{:S(2)}, u32[]{:S(2)}) %all-to-all-start.2) | async-done | bytes 3407904 | tf_op jit(solution)/shard_map/all_to_all | solution.py:121
  103.6 5.6 %all-to-all-start.3 = ((f32[8,208,512]{2,1,0:T(8,128)}), f32[8,208,512]{2,1,0:T(8,128)}, u32[]{:S(2)}, u32[]{:S(2)}) async-start(f32[8,208,512]{2,1,0:T(8,128)} %shard_map.38), calls=%async_computation.3 | async-start | bytes 6815744 | tf_op jit(solution)/shard_map/all_to_all | solution.py:121
  109.1 1.1 reduce_sum.31
  110.3 37.5 %all-to-all-done.3 = f32[8,208,512]{2,1,0:T(8,128)} async-done(((f32[8,208,512]{2,1,0:T(8,128)}), f32[8,208,512]{2,1,0:T(8,128)}, u32[]{:S(2)}, u32[]{:S(2)}) %all-to-all-start.3) | async-done | bytes 3407904 | tf_op jit(solution)/shard_map/all_to_all | solution.py:121
  147.8 2.4 %reduce_sum.32 = f32[208,512]{1,0:T(8,128)S(1)} reduce(f32[8,208,512]{2,1,0:T(8,128)} %all-to-all-done.3, f32[]{:T(128)} %constant.22.clone.1), dimensions={0}, to_apply=%region_2.3 | reduce | flops 745472 | bytes 3833860 | tf_op jit(solution)/shard_map/reduce_sum | solution.py:121
  150.2 1.1 pad_maximum_fusion
  151.2 1.4 copy.17
  (4 shorter events, 0.1 us)
Async XLA Ops:
  22.4 14.3 %all-to-all-start.1 = ((bf16[16,32,384]{2,1,0:T(8,128)(2,1)}), bf16[16,32,384]{2,1,0:T(8,128)(2,1)S(1)}, u32[]{:S(2)}, u32[]{:S(2)}) async-start(bf16[16,32,384]{2,1,0:T(8,128)(2,1)} %broadcast_in_dim.20), calls=%async_computation.1 | async-start | bytes 786432 | tf_op jit(solution)/shard_map/all_to_all | solution.py:90
  57.3 46.2 %all-to-all-start.2 = ((f32[8,208,512]{2,1,0:T(8,128)}), f32[8,208,512]{2,1,0:T(8,128)S(1)}, u32[]{:S(2)}, u32[]{:S(2)}) async-start(f32[8,208,512]{2,1,0:T(8,128)} %shard_map.37), calls=%async_computation.2 | async-start | bytes 6815744 | tf_op jit(solution)/shard_map/all_to_all | solution.py:121
  103.6 44.2 %all-to-all-start.3 = ((f32[8,208,512]{2,1,0:T(8,128)}), f32[8,208,512]{2,1,0:T(8,128)}, u32[]{:S(2)}, u32[]{:S(2)}) async-start(f32[8,208,512]{2,1,0:T(8,128)} %shard_map.38), calls=%async_computation.3 | async-start | bytes 6815744 | tf_op jit(solution)/shard_map/all_to_all | solution.py:121

commit v9 on v8

--- a/solution.py
+++ b/solution.py
@@ -15,7 +15,6 @@
 FRONT = ROWS - HALF
 CHUNK = 2048
 KEPT = 104
-PARTS = 2
 
 
 def corr_kernel(mq_ref, rt_ref, out_ref, acc_ref, lag_ref, *, scale, pairs, width):
@@ -112,11 +111,11 @@
     per_group = mq.shape[0] // win_count
     by_group = mq.reshape(win_count, per_group, mq.shape[1])
     rt = record.T
-    parts = PARTS if per_group % PARTS == 0 else per_group
-    per = per_group // parts
+    bounds = [0, 1, per_group]
     outs = []
-    for i in range(parts):
-        chunk = by_group[:, i * per : (i + 1) * per, :].reshape(win_count * per, mq.shape[1])
+    for lo, hi in zip(bounds[:-1], bounds[1:]):
+        per = hi - lo
+        chunk = by_group[:, lo:hi, :].reshape(win_count * per, mq.shape[1])
         part = correlate(chunk, rt, norm_scale, win_count)
         summed = lax.all_to_all(part, "win", 0, 0).sum(axis=0)
         outs.append(summed.reshape(per, KEPT, summed.shape[-1])[:, :LAGS, :])

time: 155 us -> 151 us (0.974)
  local copies, waits for them, and re-layouts: 15.5 us -> 13.5 us
    reshape x2 -> x1, local copies, waits for them, and re-layouts: 3.1 us -> 1.12 us  [shards(): chunk = by_group[:, lo:hi, :].reshape(win_count * per, mq.shape[1])]
    unnamed x1 -> x2, local copies, waits for them, and re-layouts: 8.69 us -> 9.38 us
  transfers between devices with their start and end apart: 3 -> 3, of which waited for: 3 -> 2; matrix products, arithmetic and copies ran while one was open for 8% -> 7% of each run, Pallas kernels for 12% -> 17%
where the time goes in v9:
time: 151 us; the launch traced here: 150 us
  waiting for transfers between devices  58.5 us (39%)
  Pallas kernels  36.2 us (24%)
  blocking collectives  16.7 us (11%)
  starting transfers between devices  16 us (11%)
  local copies, waits for them, and re-layouts  13.5 us (9%)
  other arithmetic  4.3 us (3%)
  matrix products  3.98 us (3%)
    all_to_all x2, waiting for transfers between devices, shards(): summed = lax.all_to_all(part, 'win', 0, 0).sum(axis=0)  57.1 us
    pallas_call x2, Pallas kernels, correlate(): pl.pallas_call(kernel, grid=(span // width,), in_specs=[pl.BlockSpec(mq.s...  36.2 us
    all_to_all x1, blocking collectives, gather_sources(): own = lax.all_to_all(pieces, 'rcv', 0, 0).sum(axis=0, dtype=jnp.float32)  16.7 us
    all_to_all x2, starting transfers between devices, shards(): summed = lax.all_to_all(part, 'win', 0, 0).sum(axis=0)  12.5 us
    unnamed x2, local copies, waits for them, and re-layouts  9.38 us
    dot_general x1, matrix products, shards(): jnp.dot(select, record, preferred_element_type=jnp.float32)  3.98 us
    all_to_all x1, starting transfers between devices, gather_sources(): every = lax.all_to_all(spread, 'rcv', 0, 0)  3.55 us
    reduce_sum x2, other arithmetic, shards(): summed = lax.all_to_all(part, 'win', 0, 0).sum(axis=0)  3.26 us
  transfers between devices with their start and end apart: 3, of which 2 were waited for; matrix products, arithmetic and copies ran while one was open for 7% of the time, Pallas kernels for 17%

profile of v9, /device:TPU:8, one launch (start us, length us, event | category | flops | bytes accessed | tf_op | source)
XLA Modules:
  0.0 149.9 jit_solution(15905274129846487611)
XLA Ops:
  0.0 0.7 broadcast_subtract_fusion
  0.7 0.1 copy.16
  0.8 0.1 sub.16
  0.9 4.0 %convolution_convert_fusion = bf16[32,6144]{1,0:T(8,128)(2,1)S(1)} fusion(bf16[512,1,6144]{2,0,1:T(8,128)(2,1)} %param.3, s32[32]{0:T(128)S(1)} %sub.16), kind=kOutput, calls=%fused_computation | convolution fusion | flops 201539584 | bytes 6684800 | tf_op jit(solution)/shard_map/dot_general | solution.py:104
  4.9 16.7 %all_to_all.20 = bf16[16,32,384]{2,1,0:T(8,128)(2,1)S(1)} all-to-all(bf16[16,32,384]{2,1,0:T(8,128)(2,1)S(1)} %bitcast.30), channel_id=1, replica_groups=mesh['rcv'=16,'win'=8] {'rcv'}, dimensions={0} | all-to-all | bytes 786432 | tf_op jit(solution)/shard_map/all_to_all | solution.py:87
  21.5 0.1 reduce_sum.30
  21.6 0.8 broadcast_in_dim.20
  22.4 3.6 %all-to-all-start.1 = ((bf16[16,32,384]{2,1,0:T(8,128)(2,1)}), bf16[16,32,384]{2,1,0:T(8,128)(2,1)S(1)}, u32[]{:S(2)}, u32[]{:S(2)}) async-start(bf16[16,32,384]{2,1,0:T(8,128)(2,1)} %broadcast_in_dim.20), calls=%async_computation.1 | async-start | bytes 786432 | tf_op jit(solution)/shard_map/all_to_all | solution.py:89
  25.9 8.7 %copy.17 = bf16[512,1,6144]{0,2,1:T(8,128)(2,1)} copy(bf16[512,1,6144]{2,0,1:T(8,128)(2,1)} %param.3) | data formatting | bytes 12582912 | tf_op args[0]
  35.3 1.3 all-to-all-done.1
  36.7 0.2 pad_convert_fusion
  36.9 0.2 reshape.54
  37.2 0.1 slice.16
  37.3 0.7 copy.28
  38.0 10.5 %shard_map.37 = f32[8,104,512]{2,1,0:T(8,128)} custom-call(f32[8,6272]{1,0:T(8,128)} %bitcast.33, bf16[6144,512]{1,0:T(8,128)(2,1)} %bitcast.25), custom_call_target="tpu_custom_call" | custom-call | tf_op jit(solution)/shard_map/pallas_call | solution.py:66
  48.5 6.8 %all-to-all-start.2 = ((f32[8,104,512]{2,1,0:T(8,128)}), f32[8,104,512]{2,1,0:T(8,128)S(1)}, u32[]{:S(2)}, u32[]{:S(2)}) async-start(f32[8,104,512]{2,1,0:T(8,128)} %shard_map.37), calls=%async_computation.2 | async-start | bytes 3407872 | tf_op jit(solution)/shard_map/all_to_all | solution.py:120
  55.2 0.2 slice.18
  55.4 1.1 reshape.51.refs_0_
  56.5 25.7 %shard_map.38 = f32[8,312,512]{2,1,0:T(8,128)} custom-call(f32[24,6272]{1,0:T(8,128)} %reshape.51.refs_0_, bf16[6144,512]{1,0:T(8,128)(2,1)} %bitcast.26), custom_call_target="tpu_custom_call" | custom-call | tf_op jit(solution)/shard_map/pallas_call | solution.py:66
  82.3 0.0 all-to-all-done.2
  82.3 5.7 %all-to-all-start.3 = ((f32[8,312,512]{2,1,0:T(8,128)}), f32[8,312,512]{2,1,0:T(8,128)}, u32[]{:S(2)}, u32[]{:S(2)}) async-start(f32[8,312,512]{2,1,0:T(8,128)} %shard_map.38), calls=%async_computation.3 | async-start | bytes 10223616 | tf_op jit(solution)/shard_map/all_to_all | solution.py:120
  88.0 0.2 reduce_sum.31
  88.1 57.1 %all-to-all-done.3 = f32[8,312,512]{2,1,0:T(8,128)} async-done(((f32[8,312,512]{2,1,0:T(8,128)}), f32[8,312,512]{2,1,0:T(8,128)}, u32[]{:S(2)}, u32[]{:S(2)}) %all-to-all-start.3) | async-done | bytes 5111840 | tf_op jit(solution)/shard_map/all_to_all | solution.py:120
  145.3 3.1 %reduce_sum.32 = f32[312,512]{1,0:T(8,128)S(1)} reduce(f32[8,312,512]{2,1,0:T(8,128)} %all-to-all-done.3, f32[]{:T(128)} %constant.22.clone.1), dimensions={0}, to_apply=%region_2.3 | reduce | flops 1118208 | bytes 5750788 | tf_op jit(solution)/shard_map/reduce_sum | solution.py:120
  148.4 0.1 pad_maximum_fusion
  148.4 1.4 copy.21
  (4 shorter events, 0.1 us)
Async XLA Ops:
  22.4 14.3 %all-to-all-start.1 = ((bf16[16,32,384]{2,1,0:T(8,128)(2,1)}), bf16[16,32,384]{2,1,0:T(8,128)(2,1)S(1)}, u32[]{:S(2)}, u32[]{:S(2)}) async-start(bf16[16,32,384]{2,1,0:T(8,128)(2,1)} %broadcast_in_dim.20), calls=%async_computation.1 | async-start | bytes 786432 | tf_op jit(solution)/shard_map/all_to_all | solution.py:89
  48.5 33.8 %all-to-all-start.2 = ((f32[8,104,512]{2,1,0:T(8,128)}), f32[8,104,512]{2,1,0:T(8,128)S(1)}, u32[]{:S(2)}, u32[]{:S(2)}) async-start(f32[8,104,512]{2,1,0:T(8,128)} %shard_map.37), calls=%async_computation.2 | async-start | bytes 3407872 | tf_op jit(solution)/shard_map/all_to_all | solution.py:120
  82.3 63.0 %all-to-all-start.3 = ((f32[8,312,512]{2,1,0:T(8,128)}), f32[8,312,512]{2,1,0:T(8,128)}, u32[]{:S(2)}, u32[]{:S(2)}) async-start(f32[8,312,512]{2,1,0:T(8,128)} %shard_map.38), calls=%async_computation.3 | async-start | bytes 10223616 | tf_op jit(solution)/shard_map/all_to_all | solution.py:120

commit v10 on v9

--- a/solution.py
+++ b/solution.py
@@ -14,10 +14,11 @@
 LANE = 128
 FRONT = ROWS - HALF
 CHUNK = 2048
+STACK = 4
 KEPT = 104
 
 
-def corr_kernel(mq_ref, rt_ref, out_ref, acc_ref, lag_ref, *, scale, pairs, width):
+def corr_kernel(mq_ref, rt_ref, out_ref, acc_ref, lag_ref, *, scale, sets, width):
     q = pl.program_id(0)
     u0 = pl.multiple_of(q * width, LANE)
     row = lax.broadcasted_iota(jnp.int32, (ROWS, LANE), 0)
@@ -42,27 +43,27 @@
     def _():
         acc_ref[...] = jnp.zeros_like(acc_ref)
 
-    for p in range(pairs):
+    for p in range(sets):
         slot = p % 2
-        build(2 * p, slot, 0)
-        build(2 * p + 1, slot, 1)
+        for i in range(STACK):
+            build(STACK * p + i, slot, i)
         acc_ref[p] += jnp.dot(lag_ref[slot], rt_ref[...], preferred_element_type=jnp.float32)
 
     @pl.when(q == pl.num_programs(0) - 1)
     def _():
-        per = 2 * pairs // out_ref.shape[0]
-        for k in range(2 * pairs):
-            half = (k % 2) * ROWS
+        per = STACK * sets // out_ref.shape[0]
+        for k in range(STACK * sets):
+            top = (k % STACK) * ROWS
             at = (k % per) * KEPT
-            out_ref[k // per, at : at + KEPT, :] = acc_ref[k // 2, half : half + KEPT, :] * scale
+            out_ref[k // per, at : at + KEPT, :] = acc_ref[k // STACK, top : top + KEPT, :] * scale
 
 
 def correlate(mq, rt, scale, groups):
     n_src = mq.shape[0]
     span, ch = rt.shape
-    pairs = n_src // 2
+    sets = n_src // STACK
     width = CHUNK if span % CHUNK == 0 else span
-    kernel = lambda *refs: corr_kernel(*refs, scale=scale, pairs=pairs, width=width)
+    kernel = lambda *refs: corr_kernel(*refs, scale=scale, sets=sets, width=width)
     return pl.pallas_call(
         kernel,
         grid=(span // width,),
@@ -73,8 +74,8 @@
         out_specs=pl.BlockSpec((groups, n_src // groups * KEPT, ch), lambda q: (0, 0, 0)),
         out_shape=jax.ShapeDtypeStruct((groups, n_src // groups * KEPT, ch), jnp.float32),
         scratch_shapes=[
-            pltpu.VMEM((pairs, 2 * ROWS, ch), jnp.float32),
-            pltpu.VMEM((2, 2 * ROWS, width), jnp.bfloat16),
+            pltpu.VMEM((sets, STACK * ROWS, ch), jnp.float32),
+            pltpu.VMEM((2, STACK * ROWS, width), jnp.bfloat16),
         ],
         compiler_params=pltpu.CompilerParams(dimension_semantics=("arbitrary",)),
     )(mq, rt)

time: 151 us -> 152 us (level)
  no operation moved by 1% of the time
where the time goes in v10:
time: 152 us; the launch traced here: 150 us
  waiting for transfers between devices  58.4 us (38%)
  Pallas kernels  36.3 us (24%)
  blocking collectives  16.7 us (11%)
  starting transfers between devices  16 us (11%)
  local copies, waits for them, and re-layouts  13.5 us (9%)
  other arithmetic  4.3 us (3%)
  matrix products  3.98 us (3%)
    all_to_all x2, waiting for transfers between devices, shards(): summed = lax.all_to_all(part, 'win', 0, 0).sum(axis=0)  57.1 us
    pallas_call x2, Pallas kernels, correlate(): pl.pallas_call(kernel, grid=(span // width,), in_specs=[pl.BlockSpec(mq.s...  36.3 us
    all_to_all x1, blocking collectives, gather_sources(): own = lax.all_to_all(pieces, 'rcv', 0, 0).sum(axis=0, dtype=jnp.float32)  16.7 us
    all_to_all x2, starting transfers between devices, shards(): summed = lax.all_to_all(part, 'win', 0, 0).sum(axis=0)  12.5 us
    unnamed x2, local copies, waits for them, and re-layouts  9.38 us
    dot_general x1, matrix products, shards(): jnp.dot(select, record, preferred_element_type=jnp.float32)  3.98 us
    all_to_all x1, starting transfers between devices, gather_sources(): every = lax.all_to_all(spread, 'rcv', 0, 0)  3.55 us
    reduce_sum x2, other arithmetic, shards(): summed = lax.all_to_all(part, 'win', 0, 0).sum(axis=0)  3.26 us
  transfers between devices with their start and end apart: 3, of which 2 were waited for; matrix products, arithmetic and copies ran while one was open for 7% of the time, Pallas kernels for 17%

profile of v10, /device:TPU:8, one launch (start us, length us, event | category | flops | bytes accessed | tf_op | source)
XLA Modules:
  0.0 150.0 jit_solution(906166126812548744)
XLA Ops:
  0.0 0.7 broadcast_subtract_fusion
  0.7 0.1 copy.16
  0.8 0.1 sub.16
  0.9 4.0 %convolution_convert_fusion = bf16[32,6144]{1,0:T(8,128)(2,1)S(1)} fusion(bf16[512,1,6144]{2,0,1:T(8,128)(2,1)} %param.3, s32[32]{0:T(128)S(1)} %sub.16), kind=kOutput, calls=%fused_computation | convolution fusion | flops 201539584 | bytes 6684800 | tf_op jit(solution)/shard_map/dot_general | solution.py:105
  4.9 16.7 %all_to_all.20 = bf16[16,32,384]{2,1,0:T(8,128)(2,1)S(1)} all-to-all(bf16[16,32,384]{2,1,0:T(8,128)(2,1)S(1)} %bitcast.30), channel_id=1, replica_groups=mesh['rcv'=16,'win'=8] {'rcv'}, dimensions={0} | all-to-all | bytes 786432 | tf_op jit(solution)/shard_map/all_to_all | solution.py:88
  21.5 0.1 reduce_sum.30
  21.6 0.8 broadcast_in_dim.20
  22.4 3.6 %all-to-all-start.1 = ((bf16[16,32,384]{2,1,0:T(8,128)(2,1)}), bf16[16,32,384]{2,1,0:T(8,128)(2,1)S(1)}, u32[]{:S(2)}, u32[]{:S(2)}) async-start(bf16[16,32,384]{2,1,0:T(8,128)(2,1)} %broadcast_in_dim.20), calls=%async_computation.1 | async-start | bytes 786432 | tf_op jit(solution)/shard_map/all_to_all | solution.py:90
  25.9 8.7 %copy.17 = bf16[512,1,6144]{0,2,1:T(8,128)(2,1)} copy(bf16[512,1,6144]{2,0,1:T(8,128)(2,1)} %param.3) | data formatting | bytes 12582912 | tf_op args[0]
  35.3 1.3 all-to-all-done.1
  36.7 0.2 pad_convert_fusion
  36.9 0.2 reshape.54
  37.2 0.1 slice.16
  37.3 0.7 copy.28
  38.0 10.5 %shard_map.37 = f32[8,104,512]{2,1,0:T(8,128)} custom-call(f32[8,6272]{1,0:T(8,128)} %bitcast.33, bf16[6144,512]{1,0:T(8,128)(2,1)} %bitcast.25), custom_call_target="tpu_custom_call" | custom-call | tf_op jit(solution)/shard_map/pallas_call | solution.py:67
  48.5 6.8 %all-to-all-start.2 = ((f32[8,104,512]{2,1,0:T(8,128)}), f32[8,104,512]{2,1,0:T(8,128)S(1)}, u32[]{:S(2)}, u32[]{:S(2)}) async-start(f32[8,104,512]{2,1,0:T(8,128)} %shard_map.37), calls=%async_computation.2 | async-start | bytes 3407872 | tf_op jit(solution)/shard_map/all_to_all | solution.py:121
  55.2 0.2 slice.18
  55.4 1.1 reshape.51.refs_0_
  56.6 25.8 %shard_map.38 = f32[8,312,512]{2,1,0:T(8,128)} custom-call(f32[24,6272]{1,0:T(8,128)} %reshape.51.refs_0_, bf16[6144,512]{1,0:T(8,128)(2,1)} %bitcast.26), custom_call_target="tpu_custom_call" | custom-call | tf_op jit(solution)/shard_map/pallas_call | solution.py:67
  82.4 0.0 all-to-all-done.2
  82.4 5.7 %all-to-all-start.3 = ((f32[8,312,512]{2,1,0:T(8,128)}), f32[8,312,512]{2,1,0:T(8,128)}, u32[]{:S(2)}, u32[]{:S(2)}) async-start(f32[8,312,512]{2,1,0:T(8,128)} %shard_map.38), calls=%async_computation.3 | async-start | bytes 10223616 | tf_op jit(solution)/shard_map/all_to_all | solution.py:121
  88.1 0.2 reduce_sum.31
  88.3 57.1 %all-to-all-done.3 = f32[8,312,512]{2,1,0:T(8,128)} async-done(((f32[8,312,512]{2,1,0:T(8,128)}), f32[8,312,512]{2,1,0:T(8,128)}, u32[]{:S(2)}, u32[]{:S(2)}) %all-to-all-start.3) | async-done | bytes 5111840 | tf_op jit(solution)/shard_map/all_to_all | solution.py:121
  145.4 3.1 %reduce_sum.32 = f32[312,512]{1,0:T(8,128)S(1)} reduce(f32[8,312,512]{2,1,0:T(8,128)} %all-to-all-done.3, f32[]{:T(128)} %constant.22.clone.1), dimensions={0}, to_apply=%region_2.3 | reduce | flops 1118208 | bytes 5750788 | tf_op jit(solution)/shard_map/reduce_sum | solution.py:121
  148.5 0.1 pad_maximum_fusion
  148.6 1.4 copy.21
  (4 shorter events, 0.1 us)
Async XLA Ops:
  22.4 14.3 %all-to-all-start.1 = ((bf16[16,32,384]{2,1,0:T(8,128)(2,1)}), bf16[16,32,384]{2,1,0:T(8,128)(2,1)S(1)}, u32[]{:S(2)}, u32[]{:S(2)}) async-start(bf16[16,32,384]{2,1,0:T(8,128)(2,1)} %broadcast_in_dim.20), calls=%async_computation.1 | async-start | bytes 786432 | tf_op jit(solution)/shard_map/all_to_all | solution.py:90
  48.5 33.9 %all-to-all-start.2 = ((f32[8,104,512]{2,1,0:T(8,128)}), f32[8,104,512]{2,1,0:T(8,128)S(1)}, u32[]{:S(2)}, u32[]{:S(2)}) async-start(f32[8,104,512]{2,1,0:T(8,128)} %shard_map.37), calls=%async_computation.2 | async-start | bytes 3407872 | tf_op jit(solution)/shard_map/all_to_all | solution.py:121
  82.4 63.0 %all-to-all-start.3 = ((f32[8,312,512]{2,1,0:T(8,128)}), f32[8,312,512]{2,1,0:T(8,128)}, u32[]{:S(2)}, u32[]{:S(2)}) async-start(f32[8,312,512]{2,1,0:T(8,128)} %shard_map.38), calls=%async_computation.3 | async-start | bytes 10223616 | tf_op jit(solution)/shard_map/all_to_all | solution.py:121

commit v11 on v9

--- a/solution.py
+++ b/solution.py
@@ -14,10 +14,9 @@
 LANE = 128
 FRONT = ROWS - HALF
 CHUNK = 2048
-KEPT = 104
 
 
-def corr_kernel(mq_ref, rt_ref, out_ref, acc_ref, lag_ref, *, scale, pairs, width):
+def corr_kernel(mq_ref, rt_ref, out_ref, acc_ref, lag_ref, *, scale, pairs, width, base):
     q = pl.program_id(0)
     u0 = pl.multiple_of(q * width, LANE)
     row = lax.broadcasted_iota(jnp.int32, (ROWS, LANE), 0)
@@ -26,7 +25,7 @@
     blocks = width // LANE
 
     def turned(k, b):
-        line = mq_ref[pl.ds(k, 1), pl.ds(u0 + b * LANE, LANE)]
+        line = mq_ref[pl.ds(base + k, 1), pl.ds(u0 + b * LANE, LANE)].astype(jnp.float32)
         return pltpu.roll(jnp.broadcast_to(line, (ROWS, LANE)), 0, 1, stride=1, stride_axis=0)
 
     def build(k, slot, half):
@@ -50,19 +49,18 @@
 
     @pl.when(q == pl.num_programs(0) - 1)
     def _():
-        per = 2 * pairs // out_ref.shape[0]
+        groups = out_ref.shape[0]
         for k in range(2 * pairs):
             half = (k % 2) * ROWS
-            at = (k % per) * KEPT
-            out_ref[k // per, at : at + KEPT, :] = acc_ref[k // 2, half : half + KEPT, :] * scale
+            at = (k // groups) * LAGS
+            out_ref[k % groups, at : at + LAGS, :] = acc_ref[k // 2, half : half + LAGS, :] * scale
 
 
-def correlate(mq, rt, scale, groups):
-    n_src = mq.shape[0]
+def correlate(mq, rt, scale, groups, base, n_src):
     span, ch = rt.shape
     pairs = n_src // 2
     width = CHUNK if span % CHUNK == 0 else span
-    kernel = lambda *refs: corr_kernel(*refs, scale=scale, pairs=pairs, width=width)
+    kernel = lambda *refs: corr_kernel(*refs, scale=scale, pairs=pairs, width=width, base=base)
     return pl.pallas_call(
         kernel,
         grid=(span // width,),
@@ -70,8 +68,8 @@
             pl.BlockSpec(mq.shape, lambda q: (0, 0)),
             pl.BlockSpec((width, ch), lambda q: (q, 0)),
         ],
-        out_specs=pl.BlockSpec((groups, n_src // groups * KEPT, ch), lambda q: (0, 0, 0)),
-        out_shape=jax.ShapeDtypeStruct((groups, n_src // groups * KEPT, ch), jnp.float32),
+        out_specs=pl.BlockSpec((groups, n_src // groups * LAGS, ch), lambda q: (0, 0, 0)),
+        out_shape=jax.ShapeDtypeStruct((groups, n_src // groups * LAGS, ch), jnp.float32),
         scratch_shapes=[
             pltpu.VMEM((pairs, 2 * ROWS, ch), jnp.float32),
             pltpu.VMEM((2, 2 * ROWS, width), jnp.bfloat16),
@@ -98,27 +96,23 @@
     norm_scale = 1.0 / math.sqrt(SAMPLES * traces.shape[1] * win_count)
     record = traces[:, 0, :]
     channel_ids = jnp.arange(ch_dev, dtype=jnp.int32)
-    select = (sources.reshape(-1)[:, None] - first_row == channel_ids[None, :]).astype(
-        traces.dtype
-    )
+    wanted = sources.T.reshape(-1)
+    select = (wanted[:, None] - first_row == channel_ids[None, :]).astype(traces.dtype)
     picked = jnp.dot(select, record, preferred_element_type=jnp.float32).astype(jnp.bfloat16)
-    source_rows = gather_sources(picked)
     start_at = offsets[0]
     positions = jnp.arange(span, dtype=jnp.int32)
     inside = (positions >= start_at + HALF) & (positions < start_at + HALF + SAMPLES)
-    masked = jnp.where(inside[None, :], source_rows, jnp.zeros_like(source_rows))
-    mq = jnp.pad(masked.astype(jnp.float32), ((0, 0), (FRONT, LANE - FRONT)))
+    masked = jnp.where(inside[None, :], picked, jnp.zeros_like(picked))
+    mq = gather_sources(jnp.pad(masked, ((0, 0), (FRONT, LANE - FRONT))))
     per_group = mq.shape[0] // win_count
-    by_group = mq.reshape(win_count, per_group, mq.shape[1])
     rt = record.T
     bounds = [0, 1, per_group]
     outs = []
     for lo, hi in zip(bounds[:-1], bounds[1:]):
         per = hi - lo
-        chunk = by_group[:, lo:hi, :].reshape(win_count * per, mq.shape[1])
-        part = correlate(chunk, rt, norm_scale, win_count)
+        part = correlate(mq, rt, norm_scale, win_count, lo * win_count, per * win_count)
         summed = lax.all_to_all(part, "win", 0, 0).sum(axis=0)
-        outs.append(summed.reshape(per, KEPT, summed.shape[-1])[:, :LAGS, :])
+        outs.append(summed.reshape(per, LAGS, summed.shape[-1]))
     return jnp.concatenate(outs, axis=0)
 
 

time: 151 us -> 155 us (1.026)
  blocking collectives: 16.7 us -> 18.3 us
    all_to_all x1, waiting for transfers between devices: 1.33 us -> 3.64 us  [gather_sources(): every = lax.all_to_all(spread, 'rcv', 0, 0)]
    all_to_all x1, blocking collectives: 16.7 us -> 18.3 us  [gather_sources(): own = lax.all_to_all(pieces, 'rcv', 0, 0).sum(axis=0, dtype=jnp.float32)]
    unnamed x2 -> x1, local copies, waits for them, and re-layouts: 9.38 us -> 8.69 us
  transfers between devices with their start and end apart: 3 -> 3, of which waited for: 2 -> 2; matrix products, arithmetic and copies ran while one was open for 7% -> 6% of each run, Pallas kernels for 17% -> 17%
where the time goes in v11:
time: 155 us; the launch traced here: 153 us
  waiting for transfers between devices  59.3 us (38%)
  Pallas kernels  36.2 us (23%)
  blocking collectives  18.3 us (12%)
  starting transfers between devices  16 us (10%)
  local copies, waits for them, and re-layouts  14.4 us (9%)
  other arithmetic  4.08 us (3%)
  matrix products  3.98 us (3%)
    all_to_all x2, waiting for transfers between devices, shards(): summed = lax.all_to_all(part, 'win', 0, 0).sum(axis=0)  55.7 us
    pallas_call x2, Pallas kernels, correlate(): pl.pallas_call(kernel, grid=(span // width,), in_specs=[pl.BlockSpec(mq.s...  36.2 us
    all_to_all x1, blocking collectives, gather_sources(): own = lax.all_to_all(pieces, 'rcv', 0, 0).sum(axis=0, dtype=jnp.float32)  18.3 us
    all_to_all x2, starting transfers between devices, shards(): summed = lax.all_to_all(part, 'win', 0, 0).sum(axis=0)  12.5 us
    unnamed x1, local copies, waits for them, and re-layouts  8.69 us
    dot_general x1, matrix products, shards(): jnp.dot(select, record, preferred_element_type=jnp.float32)  3.98 us
    all_to_all x1, waiting for transfers between devices, gather_sources(): every = lax.all_to_all(spread, 'rcv', 0, 0)  3.64 us
    all_to_all x1, starting transfers between devices, gather_sources(): every = lax.all_to_all(spread, 'rcv', 0, 0)  3.57 us
  transfers between devices with their start and end apart: 3, of which 2 were waited for; matrix products, arithmetic and copies ran while one was open for 6% of the time, Pallas kernels for 17%

profile of v11, /device:TPU:8, one launch (start us, length us, event | category | flops | bytes accessed | tf_op | source)
XLA Modules:
  0.0 153.1 jit_solution(841153243912635734)
XLA Ops:
  0.7 0.7 subtract_bitcast_fusion
  1.3 0.1 sub.20
  1.4 4.0 %fusion = bf16[32,6144]{1,0:T(8,128)(2,1)S(1)} fusion(bf16[512,1,6144]{2,0,1:T(8,128)(2,1)} %param.3, pred[6144]{0:T(1024)(128)(4,1)S(1)} %fusion.3, s32[32]{0:T(128)S(1)} %sub.20), kind=kOutput, calls=%fused_computation.1 | convolution fusion | flops 201736192 | bytes 6690944 | tf_op jit(solution)/shard_map/dot_general | solution.py:101
  5.4 0.2 pad.4
  5.6 1.2 reshape.33
  6.8 0.3 copy.12
  7.1 18.3 %all_to_all.20 = bf16[16,32,392]{2,1,0:T(8,128)(2,1)S(1)} all-to-all(bf16[16,32,392]{2,1,0:T(8,128)(2,1)S(1)} %bitcast.18), channel_id=1, replica_groups=mesh['rcv'=16,'win'=8] {'rcv'}, dimensions={0} | all-to-all | bytes 802816 | tf_op jit(solution)/shard_map/all_to_all | solution.py:85
  25.4 0.1 reduce_sum.30
  25.5 0.8 broadcast_in_dim.21
  26.4 3.6 %all-to-all-start.1 = ((bf16[16,32,392]{2,1,0:T(8,128)(2,1)}), bf16[16,32,392]{2,1,0:T(8,128)(2,1)S(1)}, u32[]{:S(2)}, u32[]{:S(2)}) async-start(bf16[16,32,392]{2,1,0:T(8,128)(2,1)} %broadcast_in_dim.21), calls=%async_computation.1 | async-start | bytes 1048576 | tf_op jit(solution)/shard_map/all_to_all | solution.py:87
  29.9 8.7 %copy.7 = bf16[512,1,6144]{0,2,1:T(8,128)(2,1)} copy(bf16[512,1,6144]{2,0,1:T(8,128)(2,1)} %param.3) | data formatting | bytes 12582912 | tf_op args[0]
  38.6 3.6 %all-to-all-done.1 = bf16[16,32,392]{2,1,0:T(8,128)(2,1)S(1)} async-done(((bf16[16,32,392]{2,1,0:T(8,128)(2,1)}), bf16[16,32,392]{2,1,0:T(8,128)(2,1)S(1)}, u32[]{:S(2)}, u32[]{:S(2)}) %all-to-all-start.1) | async-done | bytes 401440 | tf_op jit(solution)/shard_map/all_to_all | solution.py:87
  42.3 0.3 copy.9
  42.6 1.3 reshape.34.refs_0_
  43.9 10.5 %shard_map.37 = f32[8,101,512]{2,1,0:T(8,128)} custom-call(bf16[32,6272]{1,0:T(8,128)(2,1)} %reshape.34.refs_0_, bf16[6144,512]{1,0:T(8,128)(2,1)} %bitcast.15), custom_call_target="tpu_custom_call" | custom-call | tf_op jit(solution)/shard_map/pallas_call | solution.py:64
  54.4 6.8 %all-to-all-start.2 = ((f32[8,101,512]{2,1,0:T(8,128)}), f32[8,101,512]{2,1,0:T(8,128)S(1)}, u32[]{:S(2)}, u32[]{:S(2)}) async-start(f32[8,101,512]{2,1,0:T(8,128)} %shard_map.37), calls=%async_computation.2 | async-start | bytes 3407872 | tf_op jit(solution)/shard_map/all_to_all | solution.py:114
  61.2 25.7 %shard_map.38 = f32[8,303,512]{2,1,0:T(8,128)} custom-call(bf16[32,6272]{1,0:T(8,128)(2,1)} %reshape.34.refs_0_, bf16[6144,512]{1,0:T(8,128)(2,1)} %bitcast.16), custom_call_target="tpu_custom_call" | custom-call | tf_op jit(solution)/shard_map/pallas_call | solution.py:64
  86.9 0.0 all-to-all-done.2
  86.9 5.7 %all-to-all-start.3 = ((f32[8,303,512]{2,1,0:T(8,128)}), f32[8,303,512]{2,1,0:T(8,128)}, u32[]{:S(2)}, u32[]{:S(2)}) async-start(f32[8,303,512]{2,1,0:T(8,128)} %shard_map.38), calls=%async_computation.3 | async-start | bytes 9961472 | tf_op jit(solution)/shard_map/all_to_all | solution.py:114
  92.6 0.2 reduce_sum.31
  92.8 55.7 %all-to-all-done.3 = f32[8,303,512]{2,1,0:T(8,128)} async-done(((f32[8,303,512]{2,1,0:T(8,128)}), f32[8,303,512]{2,1,0:T(8,128)}, u32[]{:S(2)}, u32[]{:S(2)}) %all-to-all-start.3) | async-done | bytes 4964384 | tf_op jit(solution)/shard_map/all_to_all | solution.py:114
  148.4 3.1 %reduce_sum.32 = f32[303,512]{1,0:T(8,128)S(1)} reduce(f32[8,303,512]{2,1,0:T(8,128)} %all-to-all-done.3, f32[]{:T(128)} %constant.21.clone.1), dimensions={0}, to_apply=%region_2.3 | reduce | flops 1085952 | bytes 5584900 | tf_op jit(solution)/shard_map/reduce_sum | solution.py:114
  151.5 0.1 reshape.36
  151.6 0.1 pad_maximum_fusion
  151.6 1.4 copy.10
  (1 shorter events, 0.0 us)
Async XLA Ops:
  26.4 15.9 %all-to-all-start.1 = ((bf16[16,32,392]{2,1,0:T(8,128)(2,1)}), bf16[16,32,392]{2,1,0:T(8,128)(2,1)S(1)}, u32[]{:S(2)}, u32[]{:S(2)}) async-start(bf16[16,32,392]{2,1,0:T(8,128)(2,1)} %broadcast_in_dim.21), calls=%async_computation.1 | async-start | bytes 1048576 | tf_op jit(solution)/shard_map/all_to_all | solution.py:87
  54.4 32.5 %all-to-all-start.2 = ((f32[8,101,512]{2,1,0:T(8,128)}), f32[8,101,512]{2,1,0:T(8,128)S(1)}, u32[]{:S(2)}, u32[]{:S(2)}) async-start(f32[8,101,512]{2,1,0:T(8,128)} %shard_map.37), calls=%async_computation.2 | async-start | bytes 3407872 | tf_op jit(solution)/shard_map/all_to_all | solution.py:114
  86.9 61.5 %all-to-all-start.3 = ((f32[8,303,512]{2,1,0:T(8,128)}), f32[8,303,512]{2,1,0:T(8,128)}, u32[]{:S(2)}, u32[]{:S(2)}) async-start(f32[8,303,512]{2,1,0:T(8,128)} %shard_map.38), calls=%async_computation.3 | async-start | bytes 9961472 | tf_op jit(solution)/shard_map/all_to_all | solution.py:114

commit v12 on v11

--- a/solution.py
+++ b/solution.py
@@ -102,8 +102,9 @@
     start_at = offsets[0]
     positions = jnp.arange(span, dtype=jnp.int32)
     inside = (positions >= start_at + HALF) & (positions < start_at + HALF + SAMPLES)
-    masked = jnp.where(inside[None, :], picked, jnp.zeros_like(picked))
-    mq = gather_sources(jnp.pad(masked, ((0, 0), (FRONT, LANE - FRONT))))
+    source_rows = gather_sources(picked)
+    masked = jnp.where(inside[None, :], source_rows, jnp.zeros_like(source_rows))
+    mq = jnp.pad(masked, ((0, 0), (FRONT, LANE - FRONT)))
     per_group = mq.shape[0] // win_count
     rt = record.T
     bounds = [0, 1, per_group]

time: 155 us -> 148 us (0.955)
  local copies, waits for them, and re-layouts: 14.4 us -> 12.1 us
  waiting for transfers between devices: 59.3 us -> 57 us
  blocking collectives: 18.3 us -> 16.7 us
    all_to_all x1, waiting for transfers between devices: 3.64 us -> 1.33 us  [gather_sources(): every = lax.all_to_all(spread, 'rcv', 0, 0)]
    all_to_all x1, blocking collectives: 18.3 us -> 16.7 us  [gather_sources(): own = lax.all_to_all(pieces, 'rcv', 0, 0).sum(axis=0, dtype=jnp.float32)]
  transfers between devices with their start and end apart: 3 -> 3, of which waited for: 2 -> 2; matrix products, arithmetic and copies ran while one was open for 6% -> 6% of each run, Pallas kernels for 17% -> 18%
where the time goes in v12:
time: 148 us; the launch traced here: 147 us
  waiting for transfers between devices  57 us (39%)
  Pallas kernels  36.2 us (24%)
  blocking collectives  16.7 us (11%)
  starting transfers between devices  16 us (11%)
  local copies, waits for them, and re-layouts  12.1 us (8%)
  other arithmetic  4.09 us (3%)
  matrix products  3.97 us (3%)
    all_to_all x2, waiting for transfers between devices, shards(): summed = lax.all_to_all(part, 'win', 0, 0).sum(axis=0)  55.7 us
    pallas_call x2, Pallas kernels, correlate(): pl.pallas_call(kernel, grid=(span // width,), in_specs=[pl.BlockSpec(mq.s...  36.2 us
    all_to_all x1, blocking collectives, gather_sources(): own = lax.all_to_all(pieces, 'rcv', 0, 0).sum(axis=0, dtype=jnp.float32)  16.7 us
    all_to_all x2, starting transfers between devices, shards(): summed = lax.all_to_all(part, 'win', 0, 0).sum(axis=0)  12.5 us
    unnamed x1, local copies, waits for them, and re-layouts  8.69 us
    dot_general x1, matrix products, shards(): jnp.dot(select, record, preferred_element_type=jnp.float32)  3.97 us
    all_to_all x1, starting transfers between devices, gather_sources(): every = lax.all_to_all(spread, 'rcv', 0, 0)  3.55 us
    reduce_sum x2, other arithmetic, shards(): summed = lax.all_to_all(part, 'win', 0, 0).sum(axis=0)  3.22 us
  transfers between devices with their start and end apart: 3, of which 2 were waited for; matrix products, arithmetic and copies ran while one was open for 6% of the time, Pallas kernels for 18%

profile of v12, /device:TPU:8, one launch (start us, length us, event | category | flops | bytes accessed | tf_op | source)
XLA Modules:
  0.0 146.8 jit_solution(14239773661024026159)
XLA Ops:
  0.0 0.7 subtract_bitcast_fusion
  0.7 0.1 sub.20
  0.8 4.0 %convolution_convert_fusion = bf16[32,6144]{1,0:T(8,128)(2,1)S(1)} fusion(bf16[512,1,6144]{2,0,1:T(8,128)(2,1)} %param.3, s32[32]{0:T(128)S(1)} %sub.20), kind=kOutput, calls=%fused_computation | convolution fusion | flops 201539584 | bytes 6684800 | tf_op jit(solution)/shard_map/dot_general | solution.py:101
  4.8 16.7 %all_to_all.20 = bf16[16,32,384]{2,1,0:T(8,128)(2,1)S(1)} all-to-all(bf16[16,32,384]{2,1,0:T(8,128)(2,1)S(1)} %bitcast.25), channel_id=1, replica_groups=mesh['rcv'=16,'win'=8] {'rcv'}, dimensions={0} | all-to-all | bytes 786432 | tf_op jit(solution)/shard_map/all_to_all | solution.py:85
  21.5 0.1 reduce_sum.30
  21.5 0.8 broadcast_in_dim.20
  22.3 3.6 %all-to-all-start.1 = ((bf16[16,32,384]{2,1,0:T(8,128)(2,1)}), bf16[16,32,384]{2,1,0:T(8,128)(2,1)S(1)}, u32[]{:S(2)}, u32[]{:S(2)}) async-start(bf16[16,32,384]{2,1,0:T(8,128)(2,1)} %broadcast_in_dim.20), calls=%async_computation.1 | async-start | bytes 786432 | tf_op jit(solution)/shard_map/all_to_all | solution.py:87
  25.9 8.7 %copy.7 = bf16[512,1,6144]{0,2,1:T(8,128)(2,1)} copy(bf16[512,1,6144]{2,0,1:T(8,128)(2,1)} %param.3) | data formatting | bytes 12582912 | tf_op args[0]
  35.2 1.3 all-to-all-done.1
  36.7 0.9 pad.4.refs_0_
  37.6 10.5 %shard_map.37 = f32[8,101,512]{2,1,0:T(8,128)} custom-call(bf16[32,6272]{1,0:T(8,128)(2,1)} %pad.4.refs_0_, bf16[6144,512]{1,0:T(8,128)(2,1)} %bitcast.21), custom_call_target="tpu_custom_call" | custom-call | tf_op jit(solution)/shard_map/pallas_call | solution.py:64
  48.1 6.8 %all-to-all-start.2 = ((f32[8,101,512]{2,1,0:T(8,128)}), f32[8,101,512]{2,1,0:T(8,128)S(1)}, u32[]{:S(2)}, u32[]{:S(2)}) async-start(f32[8,101,512]{2,1,0:T(8,128)} %shard_map.37), calls=%async_computation.2 | async-start | bytes 3407872 | tf_op jit(solution)/shard_map/all_to_all | solution.py:115
  54.8 25.7 %shard_map.38 = f32[8,303,512]{2,1,0:T(8,128)} custom-call(bf16[32,6272]{1,0:T(8,128)(2,1)} %pad.4.refs_0_, bf16[6144,512]{1,0:T(8,128)(2,1)} %bitcast.22), custom_call_target="tpu_custom_call" | custom-call | tf_op jit(solution)/shard_map/pallas_call | solution.py:64
  80.5 0.0 all-to-all-done.2
  80.5 5.7 %all-to-all-start.3 = ((f32[8,303,512]{2,1,0:T(8,128)}), f32[8,303,512]{2,1,0:T(8,128)}, u32[]{:S(2)}, u32[]{:S(2)}) async-start(f32[8,303,512]{2,1,0:T(8,128)} %shard_map.38), calls=%async_computation.3 | async-start | bytes 9961472 | tf_op jit(solution)/shard_map/all_to_all | solution.py:115
  86.3 0.2 reduce_sum.31
  86.4 55.7 %all-to-all-done.3 = f32[8,303,512]{2,1,0:T(8,128)} async-done(((f32[8,303,512]{2,1,0:T(8,128)}), f32[8,303,512]{2,1,0:T(8,128)}, u32[]{:S(2)}, u32[]{:S(2)}) %all-to-all-start.3) | async-done | bytes 4964384 | tf_op jit(solution)/shard_map/all_to_all | solution.py:115
  142.1 3.1 %reduce_sum.32 = f32[303,512]{1,0:T(8,128)S(1)} reduce(f32[8,303,512]{2,1,0:T(8,128)} %all-to-all-done.3, f32[]{:T(128)} %constant.21.clone.1), dimensions={0}, to_apply=%region_2.3 | reduce | flops 1085952 | bytes 5584900 | tf_op jit(solution)/shard_map/reduce_sum | solution.py:115
  145.2 0.1 reshape.36
  145.2 0.1 pad_maximum_fusion
  145.3 1.4 copy.10
  (4 shorter events, 0.1 us)
Async XLA Ops:
  22.3 14.3 %all-to-all-start.1 = ((bf16[16,32,384]{2,1,0:T(8,128)(2,1)}), bf16[16,32,384]{2,1,0:T(8,128)(2,1)S(1)}, u32[]{:S(2)}, u32[]{:S(2)}) async-start(bf16[16,32,384]{2,1,0:T(8,128)(2,1)} %broadcast_in_dim.20), calls=%async_computation.1 | async-start | bytes 786432 | tf_op jit(solution)/shard_map/all_to_all | solution.py:87
  48.1 32.5 %all-to-all-start.2 = ((f32[8,101,512]{2,1,0:T(8,128)}), f32[8,101,512]{2,1,0:T(8,128)S(1)}, u32[]{:S(2)}, u32[]{:S(2)}) async-start(f32[8,101,512]{2,1,0:T(8,128)} %shard_map.37), calls=%async_computation.2 | async-start | bytes 3407872 | tf_op jit(solution)/shard_map/all_to_all | solution.py:115
  80.5 61.6 %all-to-all-start.3 = ((f32[8,303,512]{2,1,0:T(8,128)}), f32[8,303,512]{2,1,0:T(8,128)}, u32[]{:S(2)}, u32[]{:S(2)}) async-start(f32[8,303,512]{2,1,0:T(8,128)} %shard_map.38), calls=%async_computation.3 | async-start | bytes 9961472 | tf_op jit(solution)/shard_map/all_to_all | solution.py:115

commit v13 on v12

--- a/solution.py
+++ b/solution.py
@@ -13,7 +13,7 @@
 ROWS = 128
 LANE = 128
 FRONT = ROWS - HALF
-CHUNK = 2048
+CHUNK = 3072
 
 
 def corr_kernel(mq_ref, rt_ref, out_ref, acc_ref, lag_ref, *, scale, pairs, width, base):

time: 148 us -> 148 us (level)
  transfers between devices with their start and end apart: 3 -> 3, of which waited for: 2 -> 2; matrix products, arithmetic and copies ran while one was open for 6% -> 6% of each run, Pallas kernels for 18% -> 17%
where the time goes in v13:
time: 148 us; the launch traced here: 147 us
  waiting for transfers between devices  57 us (39%)
  Pallas kernels  36.1 us (24%)
  blocking collectives  16.7 us (11%)
  starting transfers between devices  16 us (11%)
  local copies, waits for them, and re-layouts  12.1 us (8%)
  other arithmetic  4.09 us (3%)
  matrix products  3.97 us (3%)
    all_to_all x2, waiting for transfers between devices, shards(): summed = lax.all_to_all(part, 'win', 0, 0).sum(axis=0)  55.7 us
    pallas_call x2, Pallas kernels, correlate(): pl.pallas_call(kernel, grid=(span // width,), in_specs=[pl.BlockSpec(mq.s...  36.1 us
    all_to_all x1, blocking collectives, gather_sources(): own = lax.all_to_all(pieces, 'rcv', 0, 0).sum(axis=0, dtype=jnp.float32)  16.7 us
    all_to_all x2, starting transfers between devices, shards(): summed = lax.all_to_all(part, 'win', 0, 0).sum(axis=0)  12.5 us
    unnamed x1, local copies, waits for them, and re-layouts  8.69 us
    dot_general x1, matrix products, shards(): jnp.dot(select, record, preferred_element_type=jnp.float32)  3.97 us
    all_to_all x1, starting transfers between devices, gather_sources(): every = lax.all_to_all(spread, 'rcv', 0, 0)  3.55 us
    reduce_sum x2, other arithmetic, shards(): summed = lax.all_to_all(part, 'win', 0, 0).sum(axis=0)  3.22 us
  transfers between devices with their start and end apart: 3, of which 2 were waited for; matrix products, arithmetic and copies ran while one was open for 6% of the time, Pallas kernels for 17%

profile of v13, /device:TPU:8, one launch (start us, length us, event | category | flops | bytes accessed | tf_op | source)
XLA Modules:
  0.0 146.6 jit_solution(9849694094074735123)
XLA Ops:
  0.0 0.7 subtract_bitcast_fusion
  0.7 0.1 sub.20
  0.8 4.0 %convolution_convert_fusion = bf16[32,6144]{1,0:T(8,128)(2,1)S(1)} fusion(bf16[512,1,6144]{2,0,1:T(8,128)(2,1)} %param.3, s32[32]{0:T(128)S(1)} %sub.20), kind=kOutput, calls=%fused_computation | convolution fusion | flops 201539584 | bytes 6684800 | tf_op jit(solution)/shard_map/dot_general | solution.py:101
  4.8 16.7 %all_to_all.20 = bf16[16,32,384]{2,1,0:T(8,128)(2,1)S(1)} all-to-all(bf16[16,32,384]{2,1,0:T(8,128)(2,1)S(1)} %bitcast.25), channel_id=1, replica_groups=mesh['rcv'=16,'win'=8] {'rcv'}, dimensions={0} | all-to-all | bytes 786432 | tf_op jit(solution)/shard_map/all_to_all | solution.py:85
  21.5 0.1 reduce_sum.30
  21.5 0.8 broadcast_in_dim.20
  22.3 3.6 %all-to-all-start.1 = ((bf16[16,32,384]{2,1,0:T(8,128)(2,1)}), bf16[16,32,384]{2,1,0:T(8,128)(2,1)S(1)}, u32[]{:S(2)}, u32[]{:S(2)}) async-start(bf16[16,32,384]{2,1,0:T(8,128)(2,1)} %broadcast_in_dim.20), calls=%async_computation.1 | async-start | bytes 786432 | tf_op jit(solution)/shard_map/all_to_all | solution.py:87
  25.9 8.7 %copy.7 = bf16[512,1,6144]{0,2,1:T(8,128)(2,1)} copy(bf16[512,1,6144]{2,0,1:T(8,128)(2,1)} %param.3) | data formatting | bytes 12582912 | tf_op args[0]
  35.2 1.3 all-to-all-done.1
  36.7 0.9 pad.4.refs_0_
  37.6 10.5 %shard_map.37 = f32[8,101,512]{2,1,0:T(8,128)} custom-call(bf16[32,6272]{1,0:T(8,128)(2,1)} %pad.4.refs_0_, bf16[6144,512]{1,0:T(8,128)(2,1)} %bitcast.21), custom_call_target="tpu_custom_call" | custom-call | tf_op jit(solution)/shard_map/pallas_call | solution.py:64
  48.1 6.8 %all-to-all-start.2 = ((f32[8,101,512]{2,1,0:T(8,128)}), f32[8,101,512]{2,1,0:T(8,128)S(1)}, u32[]{:S(2)}, u32[]{:S(2)}) async-start(f32[8,101,512]{2,1,0:T(8,128)} %shard_map.37), calls=%async_computation.2 | async-start | bytes 3407872 | tf_op jit(solution)/shard_map/all_to_all | solution.py:115
  54.8 25.6 %shard_map.38 = f32[8,303,512]{2,1,0:T(8,128)} custom-call(bf16[32,6272]{1,0:T(8,128)(2,1)} %pad.4.refs_0_, bf16[6144,512]{1,0:T(8,128)(2,1)} %bitcast.22), custom_call_target="tpu_custom_call" | custom-call | tf_op jit(solution)/shard_map/pallas_call | solution.py:64
  80.4 0.0 all-to-all-done.2
  80.4 5.7 %all-to-all-start.3 = ((f32[8,303,512]{2,1,0:T(8,128)}), f32[8,303,512]{2,1,0:T(8,128)}, u32[]{:S(2)}, u32[]{:S(2)}) async-start(f32[8,303,512]{2,1,0:T(8,128)} %shard_map.38), calls=%async_computation.3 | async-start | bytes 9961472 | tf_op jit(solution)/shard_map/all_to_all | solution.py:115
  86.1 0.2 reduce_sum.31
  86.3 55.7 %all-to-all-done.3 = f32[8,303,512]{2,1,0:T(8,128)} async-done(((f32[8,303,512]{2,1,0:T(8,128)}), f32[8,303,512]{2,1,0:T(8,128)}, u32[]{:S(2)}, u32[]{:S(2)}) %all-to-all-start.3) | async-done | bytes 4964384 | tf_op jit(solution)/shard_map/all_to_all | solution.py:115
  142.0 3.1 %reduce_sum.32 = f32[303,512]{1,0:T(8,128)S(1)} reduce(f32[8,303,512]{2,1,0:T(8,128)} %all-to-all-done.3, f32[]{:T(128)} %constant.21.clone.1), dimensions={0}, to_apply=%region_2.3 | reduce | flops 1085952 | bytes 5584900 | tf_op jit(solution)/shard_map/reduce_sum | solution.py:115
  145.1 0.1 reshape.36
  145.1 0.1 pad_maximum_fusion
  145.2 1.4 copy.10
  (4 shorter events, 0.1 us)
Async XLA Ops:
  22.3 14.3 %all-to-all-start.1 = ((bf16[16,32,384]{2,1,0:T(8,128)(2,1)}), bf16[16,32,384]{2,1,0:T(8,128)(2,1)S(1)}, u32[]{:S(2)}, u32[]{:S(2)}) async-start(bf16[16,32,384]{2,1,0:T(8,128)(2,1)} %broadcast_in_dim.20), calls=%async_computation.1 | async-start | bytes 786432 | tf_op jit(solution)/shard_map/all_to_all | solution.py:87
  48.1 32.4 %all-to-all-start.2 = ((f32[8,101,512]{2,1,0:T(8,128)}), f32[8,101,512]{2,1,0:T(8,128)S(1)}, u32[]{:S(2)}, u32[]{:S(2)}) async-start(f32[8,101,512]{2,1,0:T(8,128)} %shard_map.37), calls=%async_computation.2 | async-start | bytes 3407872 | tf_op jit(solution)/shard_map/all_to_all | solution.py:115
  80.4 61.6 %all-to-all-start.3 = ((f32[8,303,512]{2,1,0:T(8,128)}), f32[8,303,512]{2,1,0:T(8,128)}, u32[]{:S(2)}, u32[]{:S(2)}) async-start(f32[8,303,512]{2,1,0:T(8,128)} %shard_map.38), calls=%async_computation.3 | async-start | bytes 9961472 | tf_op jit(solution)/shard_map/all_to_all | solution.py:115

commit v14 on v12

--- a/solution.py
+++ b/solution.py
@@ -10,9 +10,9 @@
 SAMPLES = 6000
 HALF = 50
 LAGS = 101
-ROWS = 128
+ROWS = 112
 LANE = 128
-FRONT = ROWS - HALF
+FRONT = LANE - HALF
 CHUNK = 2048
 
 

time: 148 us -> 145 us (0.980)
  Pallas kernels: 36.2 us -> 32.7 us
    pallas_call x2, Pallas kernels: 36.2 us -> 32.7 us  [correlate(): pl.pallas_call(kernel, grid=(span // width,), in_specs=[pl.BlockSpec(mq.s...]
  transfers between devices with their start and end apart: 3 -> 3, of which waited for: 2 -> 2; matrix products, arithmetic and copies ran while one was open for 6% -> 6% of each run, Pallas kernels for 18% -> 16%
where the time goes in v14:
time: 145 us; the launch traced here: 143 us
  waiting for transfers between devices  57 us (39%)
  Pallas kernels  32.7 us (23%)
  blocking collectives  16.7 us (12%)
  starting transfers between devices  16 us (11%)
  local copies, waits for them, and re-layouts  12.1 us (8%)
  other arithmetic  4.09 us (3%)
  matrix products  3.97 us (3%)
    all_to_all x2, waiting for transfers between devices, shards(): summed = lax.all_to_all(part, 'win', 0, 0).sum(axis=0)  55.7 us
    pallas_call x2, Pallas kernels, correlate(): pl.pallas_call(kernel, grid=(span // width,), in_specs=[pl.BlockSpec(mq.s...  32.7 us
    all_to_all x1, blocking collectives, gather_sources(): own = lax.all_to_all(pieces, 'rcv', 0, 0).sum(axis=0, dtype=jnp.float32)  16.7 us
    all_to_all x2, starting transfers between devices, shards(): summed = lax.all_to_all(part, 'win', 0, 0).sum(axis=0)  12.5 us
    unnamed x1, local copies, waits for them, and re-layouts  8.69 us
    dot_general x1, matrix products, shards(): jnp.dot(select, record, preferred_element_type=jnp.float32)  3.97 us
    all_to_all x1, starting transfers between devices, gather_sources(): every = lax.all_to_all(spread, 'rcv', 0, 0)  3.55 us
    reduce_sum x2, other arithmetic, shards(): summed = lax.all_to_all(part, 'win', 0, 0).sum(axis=0)  3.22 us
  transfers between devices with their start and end apart: 3, of which 2 were waited for; matrix products, arithmetic and copies ran while one was open for 6% of the time, Pallas kernels for 16%

profile of v14, /device:TPU:8, one launch (start us, length us, event | category | flops | bytes accessed | tf_op | source)
XLA Modules:
  0.0 143.2 jit_solution(14423922455411874566)
XLA Ops:
  0.0 0.7 subtract_bitcast_fusion
  0.7 0.1 sub.20
  0.8 4.0 %convolution_convert_fusion = bf16[32,6144]{1,0:T(8,128)(2,1)S(1)} fusion(bf16[512,1,6144]{2,0,1:T(8,128)(2,1)} %param.3, s32[32]{0:T(128)S(1)} %sub.20), kind=kOutput, calls=%fused_computation | convolution fusion | flops 201539584 | bytes 6684800 | tf_op jit(solution)/shard_map/dot_general | solution.py:101
  4.8 16.7 %all_to_all.20 = bf16[16,32,384]{2,1,0:T(8,128)(2,1)S(1)} all-to-all(bf16[16,32,384]{2,1,0:T(8,128)(2,1)S(1)} %bitcast.25), channel_id=1, replica_groups=mesh['rcv'=16,'win'=8] {'rcv'}, dimensions={0} | all-to-all | bytes 786432 | tf_op jit(solution)/shard_map/all_to_all | solution.py:85
  21.5 0.1 reduce_sum.30
  21.5 0.8 broadcast_in_dim.20
  22.3 3.6 %all-to-all-start.1 = ((bf16[16,32,384]{2,1,0:T(8,128)(2,1)}), bf16[16,32,384]{2,1,0:T(8,128)(2,1)S(1)}, u32[]{:S(2)}, u32[]{:S(2)}) async-start(bf16[16,32,384]{2,1,0:T(8,128)(2,1)} %broadcast_in_dim.20), calls=%async_computation.1 | async-start | bytes 786432 | tf_op jit(solution)/shard_map/all_to_all | solution.py:87
  25.9 8.7 %copy.7 = bf16[512,1,6144]{0,2,1:T(8,128)(2,1)} copy(bf16[512,1,6144]{2,0,1:T(8,128)(2,1)} %param.3) | data formatting | bytes 12582912 | tf_op args[0]
  35.2 1.3 all-to-all-done.1
  36.6 0.9 pad.4.refs_0_
  37.6 9.6 %shard_map.37 = f32[8,101,512]{2,1,0:T(8,128)} custom-call(bf16[32,6272]{1,0:T(8,128)(2,1)} %pad.4.refs_0_, bf16[6144,512]{1,0:T(8,128)(2,1)} %bitcast.21), custom_call_target="tpu_custom_call" | custom-call | tf_op jit(solution)/shard_map/pallas_call | solution.py:64
  47.2 6.8 %all-to-all-start.2 = ((f32[8,101,512]{2,1,0:T(8,128)}), f32[8,101,512]{2,1,0:T(8,128)S(1)}, u32[]{:S(2)}, u32[]{:S(2)}) async-start(f32[8,101,512]{2,1,0:T(8,128)} %shard_map.37), calls=%async_computation.2 | async-start | bytes 3407872 | tf_op jit(solution)/shard_map/all_to_all | solution.py:115
  53.9 23.1 %shard_map.38 = f32[8,303,512]{2,1,0:T(8,128)} custom-call(bf16[32,6272]{1,0:T(8,128)(2,1)} %pad.4.refs_0_, bf16[6144,512]{1,0:T(8,128)(2,1)} %bitcast.22), custom_call_target="tpu_custom_call" | custom-call | tf_op jit(solution)/shard_map/pallas_call | solution.py:64
  77.0 0.0 all-to-all-done.2
  77.0 5.7 %all-to-all-start.3 = ((f32[8,303,512]{2,1,0:T(8,128)}), f32[8,303,512]{2,1,0:T(8,128)}, u32[]{:S(2)}, u32[]{:S(2)}) async-start(f32[8,303,512]{2,1,0:T(8,128)} %shard_map.38), calls=%async_computation.3 | async-start | bytes 9961472 | tf_op jit(solution)/shard_map/all_to_all | solution.py:115
  82.7 0.2 reduce_sum.31
  82.9 55.7 %all-to-all-done.3 = f32[8,303,512]{2,1,0:T(8,128)} async-done(((f32[8,303,512]{2,1,0:T(8,128)}), f32[8,303,512]{2,1,0:T(8,128)}, u32[]{:S(2)}, u32[]{:S(2)}) %all-to-all-start.3) | async-done | bytes 4964384 | tf_op jit(solution)/shard_map/all_to_all | solution.py:115
  138.6 3.1 %reduce_sum.32 = f32[303,512]{1,0:T(8,128)S(1)} reduce(f32[8,303,512]{2,1,0:T(8,128)} %all-to-all-done.3, f32[]{:T(128)} %constant.21.clone.1), dimensions={0}, to_apply=%region_2.3 | reduce | flops 1085952 | bytes 5584900 | tf_op jit(solution)/shard_map/reduce_sum | solution.py:115
  141.7 0.1 reshape.36
  141.7 0.1 pad_maximum_fusion
  141.8 1.4 copy.10
  (4 shorter events, 0.1 us)
Async XLA Ops:
  22.3 14.3 %all-to-all-start.1 = ((bf16[16,32,384]{2,1,0:T(8,128)(2,1)}), bf16[16,32,384]{2,1,0:T(8,128)(2,1)S(1)}, u32[]{:S(2)}, u32[]{:S(2)}) async-start(bf16[16,32,384]{2,1,0:T(8,128)(2,1)} %broadcast_in_dim.20), calls=%async_computation.1 | async-start | bytes 786432 | tf_op jit(solution)/shard_map/all_to_all | solution.py:87
  47.2 29.9 %all-to-all-start.2 = ((f32[8,101,512]{2,1,0:T(8,128)}), f32[8,101,512]{2,1,0:T(8,128)S(1)}, u32[]{:S(2)}, u32[]{:S(2)}) async-start(f32[8,101,512]{2,1,0:T(8,128)} %shard_map.37), calls=%async_computation.2 | async-start | bytes 3407872 | tf_op jit(solution)/shard_map/all_to_all | solution.py:115
  77.0 61.6 %all-to-all-start.3 = ((f32[8,303,512]{2,1,0:T(8,128)}), f32[8,303,512]{2,1,0:T(8,128)}, u32[]{:S(2)}, u32[]{:S(2)}) async-start(f32[8,303,512]{2,1,0:T(8,128)} %shard_map.38), calls=%async_computation.3 | async-start | bytes 9961472 | tf_op jit(solution)/shard_map/all_to_all | solution.py:115

commit v15 on v14

--- a/solution.py
+++ b/solution.py
@@ -10,7 +10,7 @@
 SAMPLES = 6000
 HALF = 50
 LAGS = 101
-ROWS = 112
+ROWS = 104
 LANE = 128
 FRONT = LANE - HALF
 CHUNK = 2048

time: 145 us -> 143 us (0.986)
  Pallas kernels: 32.7 us -> 31 us
    pallas_call x2, Pallas kernels: 32.7 us -> 31 us  [correlate(): pl.pallas_call(kernel, grid=(span // width,), in_specs=[pl.BlockSpec(mq.s...]
  transfers between devices with their start and end apart: 3 -> 3, of which waited for: 2 -> 2; matrix products, arithmetic and copies ran while one was open for 6% -> 6% of each run, Pallas kernels for 16% -> 15%
where the time goes in v15:
time: 143 us; the launch traced here: 142 us
  waiting for transfers between devices  57 us (40%)
  Pallas kernels  31 us (22%)
  blocking collectives  16.7 us (12%)
  starting transfers between devices  16 us (11%)
  local copies, waits for them, and re-layouts  12.1 us (8%)
  other arithmetic  4.09 us (3%)
  matrix products  3.97 us (3%)
    all_to_all x2, waiting for transfers between devices, shards(): summed = lax.all_to_all(part, 'win', 0, 0).sum(axis=0)  55.7 us
    pallas_call x2, Pallas kernels, correlate(): pl.pallas_call(kernel, grid=(span // width,), in_specs=[pl.BlockSpec(mq.s...  31 us
    all_to_all x1, blocking collectives, gather_sources(): own = lax.all_to_all(pieces, 'rcv', 0, 0).sum(axis=0, dtype=jnp.float32)  16.7 us
    all_to_all x2, starting transfers between devices, shards(): summed = lax.all_to_all(part, 'win', 0, 0).sum(axis=0)  12.5 us
    unnamed x1, local copies, waits for them, and re-layouts  8.69 us
    dot_general x1, matrix products, shards(): jnp.dot(select, record, preferred_element_type=jnp.float32)  3.97 us
    all_to_all x1, starting transfers between devices, gather_sources(): every = lax.all_to_all(spread, 'rcv', 0, 0)  3.55 us
    reduce_sum x2, other arithmetic, shards(): summed = lax.all_to_all(part, 'win', 0, 0).sum(axis=0)  3.22 us
  transfers between devices with their start and end apart: 3, of which 2 were waited for; matrix products, arithmetic and copies ran while one was open for 6% of the time, Pallas kernels for 15%

profile of v15, /device:TPU:8, one launch (start us, length us, event | category | flops | bytes accessed | tf_op | source)
XLA Modules:
  0.0 141.5 jit_solution(179305914351049730)
XLA Ops:
  0.0 0.7 subtract_bitcast_fusion
  0.7 0.1 sub.20
  0.8 4.0 %convolution_convert_fusion = bf16[32,6144]{1,0:T(8,128)(2,1)S(1)} fusion(bf16[512,1,6144]{2,0,1:T(8,128)(2,1)} %param.3, s32[32]{0:T(128)S(1)} %sub.20), kind=kOutput, calls=%fused_computation | convolution fusion | flops 201539584 | bytes 6684800 | tf_op jit(solution)/shard_map/dot_general | solution.py:101
  4.8 16.7 %all_to_all.20 = bf16[16,32,384]{2,1,0:T(8,128)(2,1)S(1)} all-to-all(bf16[16,32,384]{2,1,0:T(8,128)(2,1)S(1)} %bitcast.25), channel_id=1, replica_groups=mesh['rcv'=16,'win'=8] {'rcv'}, dimensions={0} | all-to-all | bytes 786432 | tf_op jit(solution)/shard_map/all_to_all | solution.py:85
  21.5 0.1 reduce_sum.30
  21.5 0.8 broadcast_in_dim.20
  22.3 3.6 %all-to-all-start.1 = ((bf16[16,32,384]{2,1,0:T(8,128)(2,1)}), bf16[16,32,384]{2,1,0:T(8,128)(2,1)S(1)}, u32[]{:S(2)}, u32[]{:S(2)}) async-start(bf16[16,32,384]{2,1,0:T(8,128)(2,1)} %broadcast_in_dim.20), calls=%async_computation.1 | async-start | bytes 786432 | tf_op jit(solution)/shard_map/all_to_all | solution.py:87
  25.9 8.7 %copy.7 = bf16[512,1,6144]{0,2,1:T(8,128)(2,1)} copy(bf16[512,1,6144]{2,0,1:T(8,128)(2,1)} %param.3) | data formatting | bytes 12582912 | tf_op args[0]
  35.2 1.3 all-to-all-done.1
  36.6 0.9 pad.4.refs_0_
  37.6 9.2 %shard_map.37 = f32[8,101,512]{2,1,0:T(8,128)} custom-call(bf16[32,6272]{1,0:T(8,128)(2,1)} %pad.4.refs_0_, bf16[6144,512]{1,0:T(8,128)(2,1)} %bitcast.21), custom_call_target="tpu_custom_call" | custom-call | tf_op jit(solution)/shard_map/pallas_call | solution.py:64
  46.8 6.8 %all-to-all-start.2 = ((f32[8,101,512]{2,1,0:T(8,128)}), f32[8,101,512]{2,1,0:T(8,128)S(1)}, u32[]{:S(2)}, u32[]{:S(2)}) async-start(f32[8,101,512]{2,1,0:T(8,128)} %shard_map.37), calls=%async_computation.2 | async-start | bytes 3407872 | tf_op jit(solution)/shard_map/all_to_all | solution.py:115
  53.5 21.8 %shard_map.38 = f32[8,303,512]{2,1,0:T(8,128)} custom-call(bf16[32,6272]{1,0:T(8,128)(2,1)} %pad.4.refs_0_, bf16[6144,512]{1,0:T(8,128)(2,1)} %bitcast.22), custom_call_target="tpu_custom_call" | custom-call | tf_op jit(solution)/shard_map/pallas_call | solution.py:64
  75.3 0.0 all-to-all-done.2
  75.3 5.7 %all-to-all-start.3 = ((f32[8,303,512]{2,1,0:T(8,128)}), f32[8,303,512]{2,1,0:T(8,128)}, u32[]{:S(2)}, u32[]{:S(2)}) async-start(f32[8,303,512]{2,1,0:T(8,128)} %shard_map.38), calls=%async_computation.3 | async-start | bytes 9961472 | tf_op jit(solution)/shard_map/all_to_all | solution.py:115
  81.0 0.2 reduce_sum.31
  81.2 55.7 %all-to-all-done.3 = f32[8,303,512]{2,1,0:T(8,128)} async-done(((f32[8,303,512]{2,1,0:T(8,128)}), f32[8,303,512]{2,1,0:T(8,128)}, u32[]{:S(2)}, u32[]{:S(2)}) %all-to-all-start.3) | async-done | bytes 4964384 | tf_op jit(solution)/shard_map/all_to_all | solution.py:115
  136.9 3.1 %reduce_sum.32 = f32[303,512]{1,0:T(8,128)S(1)} reduce(f32[8,303,512]{2,1,0:T(8,128)} %all-to-all-done.3, f32[]{:T(128)} %constant.21.clone.1), dimensions={0}, to_apply=%region_2.3 | reduce | flops 1085952 | bytes 5584900 | tf_op jit(solution)/shard_map/reduce_sum | solution.py:115
  140.0 0.1 reshape.36
  140.0 0.1 pad_maximum_fusion
  140.1 1.4 %copy.10 = f32[4,101,512]{2,0,1:T(4,128)} copy(f32[4,101,512]{2,1,0:T(8,128)S(1)} %pad_maximum_fusion) | data formatting | bytes 1654784 | tf_op jit(solution)/shard_map/concatenate | solution.py:117
  (4 shorter events, 0.1 us)
Async XLA Ops:
  22.3 14.3 %all-to-all-start.1 = ((bf16[16,32,384]{2,1,0:T(8,128)(2,1)}), bf16[16,32,384]{2,1,0:T(8,128)(2,1)S(1)}, u32[]{:S(2)}, u32[]{:S(2)}) async-start(bf16[16,32,384]{2,1,0:T(8,128)(2,1)} %broadcast_in_dim.20), calls=%async_computation.1 | async-start | bytes 786432 | tf_op jit(solution)/shard_map/all_to_all | solution.py:87
  46.8 28.6 %all-to-all-start.2 = ((f32[8,101,512]{2,1,0:T(8,128)}), f32[8,101,512]{2,1,0:T(8,128)S(1)}, u32[]{:S(2)}, u32[]{:S(2)}) async-start(f32[8,101,512]{2,1,0:T(8,128)} %shard_map.37), calls=%async_computation.2 | async-start | bytes 3407872 | tf_op jit(solution)/shard_map/all_to_all | solution.py:115
  75.3 61.6 %all-to-all-start.3 = ((f32[8,303,512]{2,1,0:T(8,128)}), f32[8,303,512]{2,1,0:T(8,128)}, u32[]{:S(2)}, u32[]{:S(2)}) async-start(f32[8,303,512]{2,1,0:T(8,128)} %shard_map.38), calls=%async_computation.3 | async-start | bytes 9961472 | tf_op jit(solution)/shard_map/all_to_all | solution.py:115
